TPU v7x, 32 devices: a whole 2x2x4 slice. The times are simulated.
32 devices in a mesh: vx: 2 (over x), vy: 4 (over z), col: 4 (over y, core).
Axes of the slice: x: 2, y: 2, z: 4, core: 2. Of those that a mesh axis runs over, the one named last changes fastest.
Arguments:
- right_side: float32 [128, 8192], P('col', ('vx', 'vy')), may hold values from -40 to 40
- shift: float32 [8192], P(('vx', 'vy')), may hold values from 0.5 to 5
- edge_ends: int32 [2, 131072], P(None, ('vx', 'vy')), may hold values from 0 to 1535, as said below
- weights: float32 [131072], P(('vx', 'vy')), may hold values from 0.2 to 2
- halo_rows: int32 [64, 64], P(('vx', 'vy')), may hold values from 0 to 1023, as said below
Outputs:
- solution: float32 [128, 8192], P('col', ('vx', 'vy'))
- resistance: float32 [131072], P(('vx', 'vy'))
Inputs may be any that keep to these rules, and one draw needn't show every extreme that they name: edge_ends[0] holds local rows below 1024; edge_ends[1] holds a local row below 1024 or 1024 plus a mirror slot; every one of a partition's 8 * 64 mirror slots is named by some edge of it. `halo_rows`: each row lists 64 distinct local rows.
All inputs are finite; a program needn't handle non-finite values.
Results may differ from a plain program's by a relative error of at most 0.0001.
Values sent between devices are 32-bit elements; how exact they have to be, the bound alone decides.
No kernel may reach another device: no remote copies, remote signals or barrier semaphores. Data moves between devices by JAX's collectives and lax.ppermute only.
A program may use at most 64 MiB of HBM per device.

v0:
```python
import jax
import jax.numpy as jnp
from jax import lax
from jax.sharding import PartitionSpec as P

ITERS = 2


def trade(blocks, back):
    if back:
        return lax.all_to_all(blocks, ("vx", "vy"), split_axis=1, concat_axis=1, tiled=True)
    return lax.all_to_all(blocks, ("vx", "vy"), split_axis=1, concat_axis=1, tiled=True)


def extend(field, halo_rows):
    mirrored = trade(field[:, halo_rows], False)
    return jnp.concatenate([field, mirrored.reshape(field.shape[0], -1)], axis=1)


def operate(field, shift, head_rows, tail_slots, weights, halo_rows):
    count = field.shape[1]
    width = field.shape[0]
    extended = extend(field, halo_rows)
    flow = (field[:, head_rows] - extended[:, tail_slots]) * weights
    summed = (
        jnp.zeros(extended.shape, jnp.float32)
        .at[:, head_rows]
        .add(flow)
        .at[:, tail_slots]
        .add(-flow)
    )
    returned = trade(summed[:, count:].reshape(width, halo_rows.shape[0], halo_rows.shape[1]), True)
    local = summed[:, :count].at[:, halo_rows.reshape(-1)].add(returned.reshape(width, -1))
    return shift * field + local


def two_products(residual, image):
    return lax.psum(
        (jnp.sum(residual * residual, axis=1), jnp.sum(residual * image, axis=1)), ("vx", "vy")
    )


def body(right_side, shift, edge_ends, weights, halo_rows):
    head_rows = edge_ends[0]
    tail_slots = edge_ends[1]
    solution = jnp.zeros_like(right_side)
    residual = right_side
    image = operate(residual, shift, head_rows, tail_slots, weights, halo_rows)
    norm_now, product = two_products(residual, image)
    alpha = norm_now / product
    direction = residual
    along = image
    for step in range(ITERS):
        solution = solution + alpha[:, None] * direction
        residual = residual - alpha[:, None] * along
        if step + 1 < ITERS:
            image = operate(residual, shift, head_rows, tail_slots, weights, halo_rows)
            norm_next, product = two_products(residual, image)
            ratio = norm_next / norm_now
            alpha = norm_next / (product - ratio * norm_next / alpha)
            direction = residual + ratio[:, None] * direction
            along = image + ratio[:, None] * along
            norm_now = norm_next
    extended = extend(solution, halo_rows)
    gap = solution[:, head_rows] - extended[:, tail_slots]
    partial_total = jnp.sum(gap * gap, axis=0)
    resistance = lax.psum(partial_total, "col")
    return (solution, resistance)


def solution(mesh):
    placed = (
        P("col", ("vx", "vy")),
        P(("vx", "vy")),
        P(None, ("vx", "vy")),
        P(("vx", "vy")),
        P(("vx", "vy"), None),
    )
    return jax.shard_map(
        body,
        mesh=mesh,
        in_specs=placed,
        out_specs=(P("col", ("vx", "vy")), P(("vx", "vy"))),
        check_vma=False,
    )
```

profile of v0, /device:TPU:0, one launch (start us, length us, event | category | flops | bytes accessed | tf_op | source)
XLA Modules:
  0.0 851.7 jit_solution(14894153450890281217)
XLA Ops:
  7.2 0.7 compare_select_fusion.4
  7.9 1.1 copy.77
  9.0 1.0 gather_fusion.1
  10.1 0.1 copy.71
  10.2 0.8 reshape.282
  11.0 7.3 all-to-all-start
  18.2 0.8 reshape.141
  19.0 1.2 compare_select_fusion.2
  20.2 54.4 %gather_fusion = f32[16384,32]{1,0:T(8,128)} fusion(f32[32,1024]{0,1:T(8,128)S(1)} %copy.77, s32[16384]{0:T(1024)S(1)} %broadcast_clamp_fusion.1), kind=kCustom, calls=%fused_computation | custom fusion | bytes 4259840 | tf_op jit(solution)/shard_map/gather | solution.py:24
  74.7 0.1 multiply_reduce_fusion.4
  74.8 0.5 broadcast.140
  75.3 0.8 reduce.1
  76.3 0.1 reshape.140
  76.4 0.3 copy.73
  76.7 54.4 %gather_fusion.2 = f32[16384,32]{1,0:T(8,128)} fusion(f32[32,1536]{0,1:T(8,128)S(1)} %copy.73, s32[16384]{0:T(1024)S(1)} %broadcast_clamp_fusion), kind=kCustom, calls=%fused_computation.2 | custom fusion | bytes 4259840 | tf_op jit(solution)/shard_map/gather | solution.py:24
  131.1 96.4 %scatter_custom_fusion = f32[32,1536]{0,1:T(8,128)S(1)} fusion(s32[16384]{0:T(1024)S(1)} %bitcast.57, f32[16384,32]{1,0:T(8,128)} %gather_fusion, f32[16384,32]{1,0:T(8,128)} %gather_fusion.2, f32[16384]{0:T(1024)S(1)} %copy-done.1, f32[]{:T(128)} %constant.4.clone.1), kind=kCustom, calls=%fused_computation.22 | custom fusion | flops 1572864 | bytes 4456452 | tf_op jit(solution)/shard_map/scatter-add | solution.py:28
  227.5 87.8 %scatter_custom_fusion.1 = f32[32,1536]{0,1:T(8,128)S(1)} fusion(f32[32,1536]{0,1:T(8,128)S(1)} %scatter_custom_fusion, s32[16384]{0:T(1024)S(1)} %bitcast.54, f32[16384,32]{1,0:T(8,128)} %gather_fusion, f32[16384,32]{1,0:T(8,128)} %gather_fusion.2, f32[16384]{0:T(1024)S(1)} %copy-done.1), kind=kCustom, calls=%fused_computation.17 | custom fusion | flops 2097152 | bytes 4456448 | tf_op jit(solution)/shard_map/scatter-add | solution.py:30
  315.3 0.1 copy.74
  315.4 0.8 reshape.284
  316.1 6.0 all-to-all-start.1
  322.1 0.2 slice_add_fusion.1
  322.4 6.8 all-to-all-done.1
  329.1 0.8 reduce.2
  330.1 0.1 reshape.237
  330.2 0.1 copy.76
  330.3 3.5 scatter_fusion
  333.8 0.2 multiply_reduce_fusion.3
  334.0 17.8 %all-reduce.1 = (f32[32]{0:T(128)S(1)}, f32[32]{0:T(128)S(1)}) all-reduce(f32[32]{0:T(128)S(1)} %multiply_reduce_fusion.4, f32[32]{0:T(128)S(1)} %multiply_reduce_fusion.3), channel_id=1, replica_groups=mesh['vx'=2,'vy'=4,'col'=4] {'vx','vy'}, use_global_device_ids=true, to_apply=%region_1.0 | all-reduce | flops 64 | bytes 512 | tf_op jit(solution)/shard_map/psum | solution.py:38
  351.9 1.0 gather_fusion.4
  352.9 0.1 copy.80
  353.1 0.8 reshape.286
  353.8 3.5 all-to-all-start.2
  357.4 54.4 %gather_fusion.3 = f32[16384,32]{1,0:T(8,128)} fusion(f32[32,1024]{0,1:T(8,128)S(1)} %multiply_subtract_fusion, s32[16384]{0:T(1024)S(1)} %broadcast_clamp_fusion.1), kind=kCustom, calls=%fused_computation.3 | custom fusion | bytes 4259840 | tf_op jit(solution)/shard_map/gather | solution.py:24
  411.8 0.8 reduce.3
  412.6 0.1 reshape.287
  412.7 0.1 copy.91
  412.9 54.4 %gather_fusion.5 = f32[16384,32]{1,0:T(8,128)} fusion(f32[32,1536]{0,1:T(8,128)S(1)} %pad_maximum_fusion, s32[16384]{0:T(1024)S(1)} %broadcast_clamp_fusion), kind=kCustom, calls=%fused_computation.5 | custom fusion | bytes 4259840 | tf_op jit(solution)/shard_map/gather | solution.py:24
  467.3 96.4 %scatter_custom_fusion.3 = f32[32,1536]{0,1:T(8,128)S(1)} fusion(s32[16384]{0:T(1024)S(1)} %bitcast.58, f32[16384,32]{1,0:T(8,128)} %gather_fusion.3, f32[16384,32]{1,0:T(8,128)} %gather_fusion.5, f32[16384]{0:T(1024)S(1)} %copy-done.1, f32[]{:T(128)} %constant.4.clone.1), kind=kCustom, calls=%fused_computation.23 | custom fusion | flops 1572864 | bytes 4456452 | tf_op jit(solution)/shard_map/scatter-add | solution.py:28
  563.7 87.8 %scatter_custom_fusion.4 = f32[32,1536]{0,1:T(8,128)S(1)} fusion(f32[32,1536]{0,1:T(8,128)S(1)} %scatter_custom_fusion.3, s32[16384]{0:T(1024)S(1)} %bitcast.55, f32[16384,32]{1,0:T(8,128)} %gather_fusion.3, f32[16384,32]{1,0:T(8,128)} %gather_fusion.5, f32[16384]{0:T(1024)S(1)} %copy-done.1), kind=kCustom, calls=%fused_computation.15 | custom fusion | flops 2097152 | bytes 4456448 | tf_op jit(solution)/shard_map/scatter-add | solution.py:30
  651.4 0.1 copy.83
  651.6 0.8 reshape.288
  652.3 5.7 all-to-all-start.3
  658.1 0.2 slice_add_fusion
  658.3 6.8 all-to-all-done.3
  665.1 0.8 reduce.4
  665.9 0.1 reshape.289
  666.0 0.1 reshape.261
  666.1 0.1 copy.85
  666.3 3.5 scatter_fusion.1
  669.8 0.2 multiply_reduce_fusion.1
  669.9 17.9 %all-reduce = (f32[32]{0:T(128)S(1)}, f32[32]{0:T(128)S(1)}) all-reduce(f32[32]{0:T(128)S(1)} %get-tuple-element.13, f32[32]{0:T(128)S(1)} %get-tuple-element.12), channel_id=1, replica_groups=mesh['vx'=2,'vy'=4,'col'=4] {'vx','vy'}, use_global_device_ids=true, to_apply=%region_8.0 | all-reduce | flops 64 | bytes 512 | tf_op jit(solution)/shard_map/psum | solution.py:38
  687.8 0.1 multiply_add_fusion
  687.9 1.0 gather_fusion.7
  689.0 0.1 copy.87
  689.1 0.8 reshape.290
  689.9 3.4 all-to-all-start.4
  693.3 54.4 %gather_fusion.6 = f32[16384,32]{1,0:T(8,128)} fusion(f32[32,1024]{0,1:T(8,128)S(1)} %multiply_add_fusion, s32[16384]{0:T(1024)S(1)} %broadcast_clamp_fusion.1), kind=kCustom, calls=%fused_computation.6 | custom fusion | bytes 4259840 | tf_op jit(solution)/shard_map/gather | solution.py:65
  747.7 0.8 reduce.5
  748.6 0.1 copy.92
  748.8 54.4 %gather_fusion.8 = f32[16384,32]{1,0:T(8,128)} fusion(f32[32,1536]{0,1:T(8,128)S(1)} %pad_maximum_fusion.1, s32[16384]{0:T(1024)S(1)} %broadcast_clamp_fusion), kind=kCustom, calls=%fused_computation.8 | custom fusion | bytes 4259840 | tf_op jit(solution)/shard_map/gather | solution.py:65
  803.2 7.6 multiply_reduce_fusion
  810.8 0.8 copy.90
  811.7 31.7 %all-reduce.4.cloned.1.call-done = f32[16384]{0:T(1024)} async-done(((f32[16384]{0:T(1024)}), f32[16384]{0:T(1024)}) %all-reduce.4.cloned.1.call-update) | async-done | bytes 65552 | tf_op jit(solution)/shard_map/psum | solution.py:67
  843.4 1.5 copy.100
  (33 shorter events, 1.0 us)
Async XLA Ops:
  11.0 63.8 %all-to-all-start = ((f32[8,1,2048]{2,1,0:T(1,128)}), f32[8,1,2048]{2,1,0:T(1,128)S(1)}, u32[]{:S(2)}, u32[]{:S(2)}) async-start(f32[8,1,2048]{2,1,0:T(1,128)} %reshape.282), calls=%async_computation | async-start | bytes 131072 | tf_op jit(solution)/shard_map/all_to_all | solution.py:12
  20.2 54.4 %copy-start = (f32[32,1024]{1,0:T(8,128)S(1)}, f32[32,1024]{1,0:T(8,128)}, u32[]{:S(2)}) copy-start(f32[32,1024]{1,0:T(8,128)} %param.5) | copy-start | bytes 393220
  76.7 54.4 %copy-start.1 = (f32[16384]{0:T(1024)S(1)}, f32[16384]{0:T(1024)}, u32[]{:S(2)}) copy-start(f32[16384]{0:T(1024)} %param.8) | copy-start | bytes 196612
  227.4 94.7 %copy-start.2 = (f32[1024]{0:T(1024)S(1)}, f32[1024]{0:T(1024)}, u32[]{:S(2)}) copy-start(f32[1024]{0:T(1024)} %param.6) | copy-start | bytes 12292
  316.1 13.0 %all-to-all-start.1 = ((f32[8,1,2048]{2,1,0:T(1,128)}), f32[8,1,2048]{2,1,0:T(1,128)S(1)}, u32[]{:S(2)}, u32[]{:S(2)}) async-start(f32[8,1,2048]{2,1,0:T(1,128)} %reshape.284), calls=%async_computation.1 | async-start | bytes 131072 | tf_op jit(solution)/shard_map/all_to_all | solution.py:11
  353.8 58.0 %all-to-all-start.2 = ((f32[8,1,2048]{2,1,0:T(1,128)}), f32[8,1,2048]{2,1,0:T(1,128)S(1)}, u32[]{:S(2)}, u32[]{:S(2)}) async-start(f32[8,1,2048]{2,1,0:T(1,128)} %reshape.286), calls=%async_computation.2 | async-start | bytes 131072 | tf_op jit(solution)/shard_map/all_to_all | solution.py:12
  652.3 12.7 %all-to-all-start.3 = ((f32[8,1,2048]{2,1,0:T(1,128)}), f32[8,1,2048]{2,1,0:T(1,128)S(1)}, u32[]{:S(2)}, u32[]{:S(2)}) async-start(f32[8,1,2048]{2,1,0:T(1,128)} %reshape.288), calls=%async_computation.3 | async-start | bytes 131072 | tf_op jit(solution)/shard_map/all_to_all | solution.py:11
  689.9 57.8 %all-to-all-start.4 = ((f32[8,1,2048]{2,1,0:T(1,128)}), f32[8,1,2048]{2,1,0:T(1,128)S(1)}, u32[]{:S(2)}, u32[]{:S(2)}) async-start(f32[8,1,2048]{2,1,0:T(1,128)} %reshape.290), calls=%async_computation.4 | async-start | bytes 131072 | tf_op jit(solution)/shard_map/all_to_all | solution.py:12
  693.2 150.2 %all-reduce.4.cloned.1.call-start = ((), (), s32[]{:S(2)}) async-start(), calls=%async_computation.5 | async-start | bytes 131072 | tf_op jit(solution)/shard_map/psum | solution.py:67
Sparse Core Ops, SparseCore 0:
  811.0 32.3 all-reduce.3
where the time goes:
time: 853 us; the launch traced here: 852 us
  other arithmetic  390 us (46%)
  local copies, waits for them, and re-layouts  340 us (40%)
  waiting for transfers between devices  45.3 us (5%)
  blocking collectives  35.7 us (4%)
  starting transfers between devices  25.9 us (3%)
  between operations  14.4 us (2%)
    scatter-add x4, other arithmetic, operate(): summed = jnp.zeros(extended.shape, jnp.float32).at[:, head_rows].add(flow...  368 us
    gather x4, local copies, waits for them, and re-layouts, operate(): flow = (field[:, head_rows] - extended[:, tail_slots]) * weights  218 us
    gather x2, local copies, waits for them, and re-layouts, body(): gap = solution[:, head_rows] - extended[:, tail_slots]  109 us
    psum x2, blocking collectives, two_products(): lax.psum((jnp.sum(residual * residual, axis=1), jnp.sum(residual * image,...  35.7 us
    psum x1, waiting for transfers between devices, body(): resistance = lax.psum(partial_total, 'col')  31.7 us
    all_to_all x5, starting transfers between devices, trade(): lax.all_to_all(blocks, ('vx', 'vy'), split_axis=1, concat_axis=1, tiled=T...  25.9 us
  transfers between devices with their start and end apart: 6, of which 3 were waited for; matrix products, arithmetic and copies ran while one was open for 20% of the time, Pallas kernels for 0%

commit v1 on v0

--- a/solution.py
+++ b/solution.py
@@ -1,19 +1,99 @@
 import jax
 import jax.numpy as jnp
 from jax import lax
+from jax.experimental import pallas as pl
+from jax.experimental.pallas import tpu as pltpu
 from jax.sharding import PartitionSpec as P
 
 ITERS = 2
 
 
-def trade(blocks, back):
-    if back:
-        return lax.all_to_all(blocks, ("vx", "vy"), split_axis=1, concat_axis=1, tiled=True)
+def trade(blocks):
     return lax.all_to_all(blocks, ("vx", "vy"), split_axis=1, concat_axis=1, tiled=True)
 
 
+def split3(values):
+    first = values.astype(jnp.bfloat16)
+    rest = values - first.astype(jnp.float32)
+    second = rest.astype(jnp.bfloat16)
+    third = (rest - second.astype(jnp.float32)).astype(jnp.bfloat16)
+    return jnp.concatenate([first, second, third], axis=0)
+
+
+def edge_tile(rows):
+    return 1024 if rows <= 2048 else 256
+
+
+def flow_kernel(local, scatter):
+    def kernel(xs_ref, head_ref, tail_ref, w_ref, out_ref, *acc):
+        step = pl.program_id(0)
+        width, rows = xs_ref.shape
+        tile = head_ref.shape[1]
+        head = head_ref[...]
+        tail = tail_ref[...]
+        g_head = (lax.broadcasted_iota(jnp.int32, (local, tile), 0) == head).astype(jnp.bfloat16)
+        g_tail = (lax.broadcasted_iota(jnp.int32, (rows, tile), 0) == tail).astype(jnp.bfloat16)
+        xs = split3(xs_ref[...])
+        near = jnp.dot(xs[:, :local], g_head, preferred_element_type=jnp.float32)
+        far = jnp.dot(xs, g_tail, preferred_element_type=jnp.float32)
+        gap = near - far
+        gap = gap[:width] + gap[width:2 * width] + gap[2 * width:]
+        if not scatter:
+            out_ref[...] = jnp.sum(gap * gap, axis=0, keepdims=True)
+            return
+        acc_head, acc_tail = acc
+
+        flow = split3(gap * w_ref[...])
+        dims = (((1,), (1,)), ((), ()))
+        first = step == 0
+        acc_head[...] = jnp.where(first, 0.0, acc_head[...]) + lax.dot_general(
+            flow, g_head, dims, preferred_element_type=jnp.float32
+        )
+        acc_tail[...] = jnp.where(first, 0.0, acc_tail[...]) + lax.dot_general(
+            flow, g_tail, dims, preferred_element_type=jnp.float32
+        )
+
+        @pl.when(step == pl.num_programs(0) - 1)
+        def _():
+            th = acc_head[...]
+            tt = acc_tail[...]
+            th = th[:width] + th[width:2 * width] + th[2 * width:]
+            tt = tt[:width] + tt[width:2 * width] + tt[2 * width:]
+            out_ref[:, :local] = th - tt[:, :local]
+            out_ref[:, local:] = -tt[:, local:]
+
+    return kernel
+
+
+def edge_pass(extended, head_rows, tail_slots, weights, local, scatter):
+    width, rows = extended.shape
+    edges = head_rows.shape[1]
+    tile = edge_tile(rows)
+    edge_spec = pl.BlockSpec((1, tile), lambda i: (0, i))
+    full = pl.BlockSpec((width, rows), lambda i: (0, 0))
+    if scatter:
+        out_shape = jax.ShapeDtypeStruct((width, rows), jnp.float32)
+        out_spec = pl.BlockSpec((width, rows), lambda i: (0, 0))
+        scratch = [pltpu.VMEM((3 * width, local), jnp.float32), pltpu.VMEM((3 * width, rows), jnp.float32)]
+    else:
+        out_shape = jax.ShapeDtypeStruct((1, edges), jnp.float32)
+        out_spec = edge_spec
+        scratch = []
+    return pl.pallas_call(
+        flow_kernel(local, scatter),
+        grid=(edges // tile,),
+        in_specs=[full, edge_spec, edge_spec, edge_spec],
+        out_specs=out_spec,
+        out_shape=out_shape,
+        scratch_shapes=scratch,
+        compiler_params=pltpu.CompilerParams(
+            dimension_semantics=("arbitrary",), vmem_limit_bytes=48 * 1024 * 1024
+        ),
+    )(extended, head_rows, tail_slots, weights)
+
+
 def extend(field, halo_rows):
-    mirrored = trade(field[:, halo_rows], False)
+    mirrored = trade(field[:, halo_rows])
     return jnp.concatenate([field, mirrored.reshape(field.shape[0], -1)], axis=1)
 
 
@@ -21,15 +101,8 @@
     count = field.shape[1]
     width = field.shape[0]
     extended = extend(field, halo_rows)
-    flow = (field[:, head_rows] - extended[:, tail_slots]) * weights
-    summed = (
-        jnp.zeros(extended.shape, jnp.float32)
-        .at[:, head_rows]
-        .add(flow)
-        .at[:, tail_slots]
-        .add(-flow)
-    )
-    returned = trade(summed[:, count:].reshape(width, halo_rows.shape[0], halo_rows.shape[1]), True)
+    summed = edge_pass(extended, head_rows, tail_slots, weights, count, True)
+    returned = trade(summed[:, count:].reshape(width, halo_rows.shape[0], halo_rows.shape[1]))
     local = summed[:, :count].at[:, halo_rows.reshape(-1)].add(returned.reshape(width, -1))
     return shift * field + local
 
@@ -41,8 +114,9 @@
 
 
 def body(right_side, shift, edge_ends, weights, halo_rows):
-    head_rows = edge_ends[0]
-    tail_slots = edge_ends[1]
+    head_rows = edge_ends[0:1]
+    tail_slots = edge_ends[1:2]
+    weights = weights[None, :]
     solution = jnp.zeros_like(right_side)
     residual = right_side
     image = operate(residual, shift, head_rows, tail_slots, weights, halo_rows)
@@ -62,8 +136,7 @@
             along = image + ratio[:, None] * along
             norm_now = norm_next
     extended = extend(solution, halo_rows)
-    gap = solution[:, head_rows] - extended[:, tail_slots]
-    partial_total = jnp.sum(gap * gap, axis=0)
+    partial_total = edge_pass(extended, head_rows, tail_slots, weights, solution.shape[1], False)[0]
     resistance = lax.psum(partial_total, "col")
     return (solution, resistance)
 

time: 853 us -> 282 us (0.33)
  other arithmetic: 390 us -> 12.6 us
  local copies, waits for them, and re-layouts: 340 us -> 14 us
  Pallas kernels: 0 us -> 123 us
  blocking collectives: 35.7 us -> 54.6 us
  starting transfers between devices: 25.9 us -> 14.4 us
    scatter-add x4 -> x0, other arithmetic: 368 us -> none  [operate(): summed = jnp.zeros(extended.shape, jnp.float32).at[:, head_rows].add(flow...]
    gather x12 -> x6, local copies, waits for them, and re-layouts: 330 us -> 3.46 us  [extend(): mirrored = trade(field[:, halo_rows])]
    pallas_call x0 -> x3, Pallas kernels: none -> 123 us  [edge_pass(): pl.pallas_call(flow_kernel(local, scatter), grid=(edges // tile,), in_spe...]
    all_to_all x0 -> x2, blocking collectives: none -> 19.1 us  [trade(): lax.all_to_all(blocks, ('vx', 'vy'), split_axis=1, concat_axis=1, tiled=T...]
    all_to_all x5 -> x3, starting transfers between devices: 25.9 us -> 14.2 us  [trade(): lax.all_to_all(blocks, ('vx', 'vy'), split_axis=1, concat_axis=1, tiled=T...]
    all_to_all x5 -> x3, waiting for transfers between devices: 13.6 us -> 19.8 us  [trade(): lax.all_to_all(blocks, ('vx', 'vy'), split_axis=1, concat_axis=1, tiled=T...]
  transfers between devices with their start and end apart: 6 -> 4, of which waited for: 3 -> 4; matrix products, arithmetic and copies ran while one was open for 20% -> 0% of each run, Pallas kernels for 0% -> 0%
where the time goes in v1:
time: 282 us; the launch traced here: 281 us
  Pallas kernels  123 us (44%)
  blocking collectives  54.6 us (19%)
  waiting for transfers between devices  48.3 us (17%)
  starting transfers between devices  14.4 us (5%)
  between operations  14.4 us (5%)
  local copies, waits for them, and re-layouts  14 us (5%)
  other arithmetic  12.6 us (4%)
    pallas_call x3, Pallas kernels, edge_pass(): pl.pallas_call(flow_kernel(local, scatter), grid=(edges // tile,), in_spe...  123 us
    psum x2, blocking collectives, two_products(): lax.psum((jnp.sum(residual * residual, axis=1), jnp.sum(residual * image,...  35.5 us
    psum x1, waiting for transfers between devices, body(): resistance = lax.psum(partial_total, 'col')  28.5 us
    all_to_all x3, waiting for transfers between devices, trade(): lax.all_to_all(blocks, ('vx', 'vy'), split_axis=1, concat_axis=1, tiled=T...  19.8 us
    all_to_all x2, blocking collectives, trade(): lax.all_to_all(blocks, ('vx', 'vy'), split_axis=1, concat_axis=1, tiled=T...  19.1 us
    all_to_all x3, starting transfers between devices, trade(): lax.all_to_all(blocks, ('vx', 'vy'), split_axis=1, concat_axis=1, tiled=T...  14.2 us
    unnamed x27, local copies, waits for them, and re-layouts  7.21 us
    scatter-add x2, other arithmetic, operate(): summed[:, :count].at[:, halo_rows.reshape(-1)]  7.01 us
  transfers between devices with their start and end apart: 4, of which 4 were waited for; matrix products, arithmetic and copies ran while one was open for 0% of the time, Pallas kernels for 0%

profile of v1, /device:TPU:0, one launch (start us, length us, event | category | flops | bytes accessed | tf_op | source)
XLA Modules:
  0.0 281.0 jit_solution(15006386364913710772)
XLA Ops:
  7.2 0.7 compare_select_fusion.1
  7.9 1.1 copy.43
  9.0 1.0 gather_fusion
  10.1 0.1 copy.37
  10.2 0.8 reshape.115
  11.0 7.4 %all-to-all-start = ((f32[8,1,2048]{2,1,0:T(1,128)}), f32[8,1,2048]{2,1,0:T(1,128)S(1)}, u32[]{:S(2)}, u32[]{:S(2)}) async-start(f32[8,1,2048]{2,1,0:T(1,128)} %reshape.115), calls=%async_computation | async-start | bytes 131072 | tf_op jit(solution)/shard_map/all_to_all | solution.py:12
  18.5 0.1 fusion
  18.6 6.8 %all-to-all-done = f32[8,1,2048]{2,1,0:T(1,128)S(1)} async-done(((f32[8,1,2048]{2,1,0:T(1,128)}), f32[8,1,2048]{2,1,0:T(1,128)S(1)}, u32[]{:S(2)}, u32[]{:S(2)}) %all-to-all-start) | async-done | bytes 65568 | tf_op jit(solution)/shard_map/all_to_all | solution.py:12
  25.4 0.6 broadcast.46
  26.0 0.8 reduce
  26.8 0.1 reshape.116
  27.0 0.1 reshape.61
  27.1 0.8 copy-done.1
  27.9 0.8 copy-done
  28.7 52.5 %shard_map.68 = f32[32,1536]{1,0:T(8,128)S(1)} custom-call(f32[32,1536]{1,0:T(8,128)S(1)} %pad_maximum_fusion.xs_ref, s32[1,16384]{1,0:T(1,128)S(1)} %get-tuple-element.13.head_ref, s32[1,16384]{1,0:T(1,128)S(1)} %get-tuple-element.12.tail_ref, f32[1,16384]{1,0:T(1,128)S(1)} %bitcast.31), custom_call_target="tpu_custom_call" | custom-call | tf_op jit(solution)/shard_map/pallas_call | solution.py:82
  81.2 0.1 reshape.63
  81.3 0.8 reshape.117
  82.1 3.5 %all-to-all-start.1 = ((f32[8,1,2048]{2,1,0:T(1,128)}), f32[8,1,2048]{2,1,0:T(1,128)S(1)}, u32[]{:S(2)}, u32[]{:S(2)}) async-start(f32[8,1,2048]{2,1,0:T(1,128)} %reshape.117), calls=%async_computation.1 | async-start | bytes 131072 | tf_op jit(solution)/shard_map/all_to_all | solution.py:12
  85.6 0.1 multiply_reduce_fusion.3
  85.7 0.2 copy.41
  85.9 6.6 %all-to-all-done.1 = f32[8,1,2048]{2,1,0:T(1,128)S(1)} async-done(((f32[8,1,2048]{2,1,0:T(1,128)}), f32[8,1,2048]{2,1,0:T(1,128)S(1)}, u32[]{:S(2)}, u32[]{:S(2)}) %all-to-all-start.1) | async-done | bytes 65568 | tf_op jit(solution)/shard_map/all_to_all | solution.py:12
  92.5 0.8 reduce.1
  93.4 0.1 reshape.118
  93.5 0.1 reshape.94
  93.6 0.1 copy.42
  93.8 3.5 %scatter_fusion = f32[32,1024]{0,1:T(8,128)S(1)} fusion(f32[32,1024]{0,1:T(8,128)S(1)} %copy.41, s32[512]{0:T(512)S(1)} %bitcast.46, f32[512,32]{1,0:T(8,128)S(1)} %copy.42), kind=kCustom, calls=%fused_computation.3 | custom fusion | flops 16384 | bytes 198656 | tf_op jit(solution)/shard_map/scatter-add | solution.py:106
  97.3 0.2 multiply_reduce_fusion
  97.4 0.2 copy.44
  97.6 17.8 %all-reduce.1 = (f32[32]{0:T(128)S(1)}, f32[32]{0:T(128)S(1)}) all-reduce(f32[32]{0:T(128)S(1)} %get-tuple-element.10, f32[32]{0:T(128)S(1)} %multiply_reduce_fusion), channel_id=1, replica_groups=mesh['vx'=2,'vy'=4,'col'=4] {'vx','vy'}, use_global_device_ids=true, to_apply=%region_1.0 | all-reduce | flops 64 | bytes 512 | tf_op jit(solution)/shard_map/psum | solution.py:111
  115.4 0.2 copy.45
  115.6 1.0 gather_fusion.1
  116.7 0.1 copy.46
  116.8 0.1 reshape.119
  117.0 9.5 %all_to_all.25 = f32[8,1,2048]{2,1,0:T(1,128)S(1)} all-to-all(f32[8,1,2048]{2,1,0:T(1,128)S(1)} %reshape.119), channel_id=1, replica_groups=mesh['vx'=2,'vy'=4,'col'=4] {'vx','vy'}, dimensions={0} | all-to-all | bytes 131072 | tf_op jit(solution)/shard_map/all_to_all | solution.py:12
  126.5 0.8 reduce.2
  127.3 0.1 reshape.120
  127.5 0.1 reshape.65
  127.6 52.5 %shard_map.69 = f32[32,1536]{1,0:T(8,128)S(1)} custom-call(f32[32,1536]{1,0:T(8,128)S(1)} %pad_maximum_fusion.1.xs_ref, s32[1,16384]{1,0:T(1,128)S(1)} %get-tuple-element.13.head_ref, s32[1,16384]{1,0:T(1,128)S(1)} %get-tuple-element.12.tail_ref, f32[1,16384]{1,0:T(1,128)S(1)} %bitcast.32), custom_call_target="tpu_custom_call" | custom-call | tf_op jit(solution)/shard_map/pallas_call | solution.py:82
  180.1 0.1 reshape.66
  180.2 0.8 reshape.121
  181.0 3.4 %all-to-all-start.3 = ((f32[8,1,2048]{2,1,0:T(1,128)}), f32[8,1,2048]{2,1,0:T(1,128)S(1)}, u32[]{:S(2)}, u32[]{:S(2)}) async-start(f32[8,1,2048]{2,1,0:T(1,128)} %reshape.121), calls=%async_computation.3 | async-start | bytes 131072 | tf_op jit(solution)/shard_map/all_to_all | solution.py:12
  184.4 0.2 all-reduce.4.cloned.1.call-start
  184.6 0.2 copy.50
  184.8 6.5 %all-to-all-done.3 = f32[8,1,2048]{2,1,0:T(1,128)S(1)} async-done(((f32[8,1,2048]{2,1,0:T(1,128)}), f32[8,1,2048]{2,1,0:T(1,128)S(1)}, u32[]{:S(2)}, u32[]{:S(2)}) %all-to-all-start.3) | async-done | bytes 65568 | tf_op jit(solution)/shard_map/all_to_all | solution.py:12
  191.3 0.8 reduce.3
  192.1 0.1 reshape.122
  192.3 0.1 reshape.102
  192.4 0.1 copy.51
  192.5 3.5 %scatter_fusion.1 = f32[32,1024]{0,1:T(8,128)S(1)} fusion(f32[32,1024]{0,1:T(8,128)S(1)} %copy.50, s32[512]{0:T(512)S(1)} %bitcast.47, f32[512,32]{1,0:T(8,128)S(1)} %copy.51), kind=kCustom, calls=%fused_computation.4 | custom fusion | flops 16384 | bytes 198656 | tf_op jit(solution)/shard_map/scatter-add | solution.py:106
  196.1 0.2 copy.52
  196.2 0.1 multiply_reduce_fusion.1
  196.4 17.8 %all-reduce = (f32[32]{0:T(128)S(1)}, f32[32]{0:T(128)S(1)}) all-reduce(f32[32]{0:T(128)S(1)} %get-tuple-element.3, f32[32]{0:T(128)S(1)} %get-tuple-element.2), channel_id=1, replica_groups=mesh['vx'=2,'vy'=4,'col'=4] {'vx','vy'}, use_global_device_ids=true, to_apply=%region_6.0 | all-reduce | flops 64 | bytes 512 | tf_op jit(solution)/shard_map/psum | solution.py:111
  214.1 0.1 multiply_add_fusion
  214.3 0.2 copy.53
  214.5 1.0 gather_fusion.2
  215.5 0.1 copy.54
  215.6 0.1 reshape.123
  215.8 9.5 %all_to_all.26 = f32[8,1,2048]{2,1,0:T(1,128)S(1)} all-to-all(f32[8,1,2048]{2,1,0:T(1,128)S(1)} %reshape.123), channel_id=1, replica_groups=mesh['vx'=2,'vy'=4,'col'=4] {'vx','vy'}, dimensions={0} | all-to-all | bytes 131072 | tf_op jit(solution)/shard_map/all_to_all | solution.py:12
  225.3 0.8 reduce.4
  226.2 0.1 reshape.124
  226.3 0.1 reshape.68
  226.4 17.8 %shard_map.70 = f32[1,16384]{1,0:T(1,128)} custom-call(f32[32,1536]{1,0:T(8,128)S(1)} %pad_maximum_fusion.2.xs_ref, s32[1,16384]{1,0:T(1,128)S(1)} %get-tuple-element.13.head_ref, s32[1,16384]{1,0:T(1,128)S(1)} %get-tuple-element.12.tail_ref, f32[1,16384]{1,0:T(1,128)S(1)} %bitcast.33), custom_call_target="tpu_custom_call" | custom-call | tf_op jit(solution)/shard_map/pallas_call | solution.py:82
  244.2 28.5 %all-reduce.4.cloned.1.call-done = f32[16384]{0:T(1024)} async-done(((f32[16384]{0:T(1024)}), f32[16384]{0:T(1024)}) %all-reduce.4.cloned.1.call-update) | async-done | bytes 65552 | tf_op jit(solution)/shard_map/psum | solution.py:140
  272.7 1.5 copy.63
  (34 shorter events, 0.9 us)
Async XLA Ops:
  10.2 8.2 %copy-start.3 = (s32[2,16384]{1,0:T(2,128)S(1)}, s32[2,16384]{1,0:T(2,128)}, u32[]{:S(2)}) copy-start(s32[2,16384]{1,0:T(2,128)} %param.7) | copy-start | bytes 393220
  11.0 7.4 %copy-start.5 = (s32[8,64]{1,0:T(8,128)S(1)}, s32[8,64]{1,0:T(8,128)}, u32[]{:S(2)}) copy-start(s32[8,64]{1,0:T(8,128)} %param.9) | copy-start | bytes 6148
  11.0 14.4 %all-to-all-start = ((f32[8,1,2048]{2,1,0:T(1,128)}), f32[8,1,2048]{2,1,0:T(1,128)S(1)}, u32[]{:S(2)}, u32[]{:S(2)}) async-start(f32[8,1,2048]{2,1,0:T(1,128)} %reshape.115), calls=%async_computation | async-start | bytes 131072 | tf_op jit(solution)/shard_map/all_to_all | solution.py:12
  27.0 0.9 copy-start.1
  27.9 0.8 copy-start
  82.1 3.5 %copy-start.4 = (f32[1024]{0:T(1024)S(1)}, f32[1024]{0:T(1024)}, u32[]{:S(2)}) copy-start(f32[1024]{0:T(1024)} %param.6) | copy-start | bytes 12292
  82.1 10.4 %all-to-all-start.1 = ((f32[8,1,2048]{2,1,0:T(1,128)}), f32[8,1,2048]{2,1,0:T(1,128)S(1)}, u32[]{:S(2)}, u32[]{:S(2)}) async-start(f32[8,1,2048]{2,1,0:T(1,128)} %reshape.117), calls=%async_computation.1 | async-start | bytes 131072 | tf_op jit(solution)/shard_map/all_to_all | solution.py:12
  181.0 10.3 %all-to-all-start.3 = ((f32[8,1,2048]{2,1,0:T(1,128)}), f32[8,1,2048]{2,1,0:T(1,128)S(1)}, u32[]{:S(2)}, u32[]{:S(2)}) async-start(f32[8,1,2048]{2,1,0:T(1,128)} %reshape.121), calls=%async_computation.3 | async-start | bytes 131072 | tf_op jit(solution)/shard_map/all_to_all | solution.py:12
  184.4 88.3 %all-reduce.4.cloned.1.call-start = ((), (), s32[]{:S(2)}) async-start(), calls=%async_computation.5 | async-start | bytes 131072 | tf_op jit(solution)/shard_map/psum | solution.py:140
  214.2 12.2 %copy-start.2 = (f32[32,1024]{1,0:T(8,128)}, f32[32,1024]{1,0:T(8,128)S(1)}, u32[]{:S(2)}) copy-start(f32[32,1024]{1,0:T(8,128)S(1)} %multiply_add_fusion) | copy-start | bytes 393220
Sparse Core Ops, SparseCore 0:
  244.3 28.3 all-reduce.3

commit v2 on v1

--- a/solution.py
+++ b/solution.py
@@ -97,11 +97,15 @@
     return jnp.concatenate([field, mirrored.reshape(field.shape[0], -1)], axis=1)
 
 
+def gathered(field, halo_rows):
+    return lax.all_gather(extend(field, halo_rows), "col", axis=0, tiled=True)
+
+
 def operate(field, shift, head_rows, tail_slots, weights, halo_rows):
     count = field.shape[1]
     width = field.shape[0]
-    extended = extend(field, halo_rows)
-    summed = edge_pass(extended, head_rows, tail_slots, weights, count, True)
+    partial = edge_pass(gathered(field, halo_rows), head_rows, tail_slots, weights, count, True)
+    summed = lax.psum_scatter(partial, "col", scatter_dimension=0, tiled=True)
     returned = trade(summed[:, count:].reshape(width, halo_rows.shape[0], halo_rows.shape[1]))
     local = summed[:, :count].at[:, halo_rows.reshape(-1)].add(returned.reshape(width, -1))
     return shift * field + local
@@ -114,9 +118,12 @@
 
 
 def body(right_side, shift, edge_ends, weights, halo_rows):
-    head_rows = edge_ends[0:1]
-    tail_slots = edge_ends[1:2]
-    weights = weights[None, :]
+    groups = lax.axis_size("col")
+    share = edge_ends.shape[1] // groups
+    start = lax.axis_index("col") * share
+    head_rows = lax.dynamic_slice_in_dim(edge_ends[0:1], start, share, axis=1)
+    tail_slots = lax.dynamic_slice_in_dim(edge_ends[1:2], start, share, axis=1)
+    weights = lax.dynamic_slice_in_dim(weights[None, :], start, share, axis=1)
     solution = jnp.zeros_like(right_side)
     residual = right_side
     image = operate(residual, shift, head_rows, tail_slots, weights, halo_rows)
@@ -135,9 +142,8 @@
             direction = residual + ratio[:, None] * direction
             along = image + ratio[:, None] * along
             norm_now = norm_next
-    extended = extend(solution, halo_rows)
-    partial_total = edge_pass(extended, head_rows, tail_slots, weights, solution.shape[1], False)[0]
-    resistance = lax.psum(partial_total, "col")
+    total = edge_pass(gathered(solution, halo_rows), head_rows, tail_slots, weights, solution.shape[1], False)[0]
+    resistance = lax.all_gather(total, "col", axis=0, tiled=True)
     return (solution, resistance)
 
 

time: 282 us -> 255 us (0.904)
  Pallas kernels: 123 us -> 50.5 us
  blocking collectives: 54.6 us -> 84 us
  waiting for transfers between devices: 48.3 us -> 59.2 us
  starting transfers between devices: 14.4 us -> 18.5 us
    pallas_call x3, Pallas kernels: 123 us -> 50.5 us  [edge_pass(): pl.pallas_call(flow_kernel(local, scatter), grid=(edges // tile,), in_spe...]
    reduce_scatter x0 -> x2, waiting for transfers between devices: none -> 39.7 us  [operate(): summed = lax.psum_scatter(partial, 'col', scatter_dimension=0, tiled=True)]
    all_gather x0 -> x4, blocking collectives: none -> 29.4 us  [the longest x3 24.1 us: gathered(): return lax.all_gather(extend(field, halo_rows), 'col', axis=0, tiled=True)]
    psum x1 -> x0, waiting for transfers between devices: 28.5 us -> none  [body(): resistance = lax.psum(partial_total, 'col')]
    all_to_all x3, starting transfers between devices: 14.2 us -> 18.4 us  [trade(): lax.all_to_all(blocks, ('vx', 'vy'), split_axis=1, concat_axis=1, tiled=T...]
    unnamed x27 -> x29, local copies, waits for them, and re-layouts: 7.21 us -> 6.21 us
  transfers between devices with their start and end apart: 4 -> 5, of which waited for: 4 -> 5; matrix products, arithmetic and copies ran while one was open for 0% -> 1% of each run, Pallas kernels for 0% -> 0%
where the time goes in v2:
time: 255 us; the launch traced here: 254 us
  blocking collectives  84 us (33%)
  waiting for transfers between devices  59.2 us (23%)
  Pallas kernels  50.5 us (20%)
  starting transfers between devices  18.5 us (7%)
  local copies, waits for them, and re-layouts  15.4 us (6%)
  between operations  14.4 us (6%)
  other arithmetic  12.5 us (5%)
    pallas_call x3, Pallas kernels, edge_pass(): pl.pallas_call(flow_kernel(local, scatter), grid=(edges // tile,), in_spe...  50.5 us
    reduce_scatter x2, waiting for transfers between devices, operate(): summed = lax.psum_scatter(partial, 'col', scatter_dimension=0, tiled=True)  39.7 us
    psum x2, blocking collectives, two_products(): lax.psum((jnp.sum(residual * residual, axis=1), jnp.sum(residual * image,...  35.6 us
    all_gather x3, blocking collectives, gathered(): return lax.all_gather(extend(field, halo_rows), 'col', axis=0, tiled=True)  24.1 us
    all_to_all x3, waiting for transfers between devices, trade(): lax.all_to_all(blocks, ('vx', 'vy'), split_axis=1, concat_axis=1, tiled=T...  19.4 us
    all_to_all x2, blocking collectives, trade(): lax.all_to_all(blocks, ('vx', 'vy'), split_axis=1, concat_axis=1, tiled=T...  19 us
    all_to_all x3, starting transfers between devices, trade(): lax.all_to_all(blocks, ('vx', 'vy'), split_axis=1, concat_axis=1, tiled=T...  18.4 us
    scatter-add x2, other arithmetic, operate(): summed[:, :count].at[:, halo_rows.reshape(-1)]  7.01 us
  transfers between devices with their start and end apart: 5, of which 5 were waited for; matrix products, arithmetic and copies ran while one was open for 1% of the time, Pallas kernels for 0%

profile of v2, /device:TPU:0, one launch (start us, length us, event | category | flops | bytes accessed | tf_op | source)
XLA Modules:
  0.0 254.4 jit_solution(17520349731995574714)
XLA Ops:
  7.2 0.7 compare_select_fusion.1
  7.9 1.1 copy.43
  9.0 1.0 gather_fusion
  10.1 0.1 copy.37
  10.2 0.8 reshape.117
  11.0 7.3 %all-to-all-start = ((f32[8,1,2048]{2,1,0:T(1,128)}), f32[8,1,2048]{2,1,0:T(1,128)S(1)}, u32[]{:S(2)}, u32[]{:S(2)}) async-start(f32[8,1,2048]{2,1,0:T(1,128)} %reshape.117), calls=%async_computation | async-start | bytes 131072 | tf_op jit(solution)/shard_map/all_to_all | solution.py:12
  18.3 0.1 fusion
  18.4 0.7 dynamic-slice.3
  19.2 6.1 %all-to-all-done = f32[8,1,2048]{2,1,0:T(1,128)S(1)} async-done(((f32[8,1,2048]{2,1,0:T(1,128)}), f32[8,1,2048]{2,1,0:T(1,128)S(1)}, u32[]{:S(2)}, u32[]{:S(2)}) %all-to-all-start) | async-done | bytes 65568 | tf_op jit(solution)/shard_map/all_to_all | solution.py:12
  25.2 0.6 broadcast.46
  25.8 0.8 reduce
  26.8 0.1 reshape.62
  26.9 0.8 copy-done
  27.8 8.6 %all_gather.12.xs_ref = f32[128,1536]{1,0:T(8,128)S(1)} all-gather(f32[32,1536]{1,0:T(8,128)S(1)} %pad_maximum_fusion), channel_id=1, replica_groups=mesh['vx'=2,'vy'=4,'col'=4] {'col'}, dimensions={0}, use_global_device_ids=true | all-gather | bytes 983040 | tf_op jit(solution)/shard_map/all_gather | solution.py:101
  36.4 20.7 %shard_map.68 = f32[128,1536]{1,0:T(8,128)} custom-call(f32[128,1536]{1,0:T(8,128)S(1)} %all_gather.12.xs_ref, s32[1,4096]{1,0:T(1,128)S(1)} %get-tuple-element.15.head_ref, s32[1,4096]{1,0:T(1,128)S(1)} %get-tuple-element.14.tail_ref, f32[1,4096]{1,0:T(1,128)S(1)} %bitcast.31), custom_call_target="tpu_custom_call" | custom-call | tf_op jit(solution)/shard_map/pallas_call | solution.py:82
  57.1 0.7 copy-done.6
  57.8 19.0 %reduce-scatter.3.cloned.1.call-done = f32[32,1536]{1,0:T(8,128)} async-done(((f32[128,1536]{1,0:T(8,128)}), f32[32,1536]{1,0:T(8,128)}) %reduce-scatter.3.cloned.1.call-update) | async-done | bytes 196624 | tf_op jit(solution)/shard_map/reduce_scatter | solution.py:108
  76.9 0.8 slice-done
  77.8 0.8 reshape.119
  78.6 5.6 %all-to-all-start.1 = ((f32[8,1,2048]{2,1,0:T(1,128)}), f32[8,1,2048]{2,1,0:T(1,128)S(1)}, u32[]{:S(2)}, u32[]{:S(2)}) async-start(f32[8,1,2048]{2,1,0:T(1,128)} %reshape.119), calls=%async_computation.2 | async-start | bytes 131072 | tf_op jit(solution)/shard_map/all_to_all | solution.py:12
  84.3 0.1 multiply_reduce_fusion.3
  84.4 0.2 copy.41
  84.6 6.6 %all-to-all-done.1 = f32[8,1,2048]{2,1,0:T(1,128)S(1)} async-done(((f32[8,1,2048]{2,1,0:T(1,128)}), f32[8,1,2048]{2,1,0:T(1,128)S(1)}, u32[]{:S(2)}, u32[]{:S(2)}) %all-to-all-start.1) | async-done | bytes 65568 | tf_op jit(solution)/shard_map/all_to_all | solution.py:12
  91.2 0.8 reduce.1
  92.2 0.1 reshape.95
  92.3 0.1 copy.42
  92.4 3.5 %scatter_fusion = f32[32,1024]{0,1:T(8,128)S(1)} fusion(f32[32,1024]{0,1:T(8,128)S(1)} %copy.41, s32[512]{0:T(512)S(1)} %bitcast.47, f32[512,32]{1,0:T(8,128)S(1)} %copy.42), kind=kCustom, calls=%fused_computation.3 | custom fusion | flops 16384 | bytes 198656 | tf_op jit(solution)/shard_map/scatter-add | solution.py:110
  96.0 0.2 multiply_reduce_fusion
  96.1 0.2 copy.44
  96.3 17.8 %all-reduce.1 = (f32[32]{0:T(128)S(1)}, f32[32]{0:T(128)S(1)}) all-reduce(f32[32]{0:T(128)S(1)} %get-tuple-element.10, f32[32]{0:T(128)S(1)} %multiply_reduce_fusion), channel_id=1, replica_groups=mesh['vx'=2,'vy'=4,'col'=4] {'vx','vy'}, use_global_device_ids=true, to_apply=%region_1.0 | all-reduce | flops 64 | bytes 512 | tf_op jit(solution)/shard_map/psum | solution.py:115
  114.2 0.2 copy.45
  114.4 1.0 gather_fusion.1
  115.4 0.1 copy.46
  115.6 0.1 reshape.121
  115.7 9.5 %all_to_all.25 = f32[8,1,2048]{2,1,0:T(1,128)S(1)} all-to-all(f32[8,1,2048]{2,1,0:T(1,128)S(1)} %reshape.121), channel_id=1, replica_groups=mesh['vx'=2,'vy'=4,'col'=4] {'vx','vy'}, dimensions={0} | all-to-all | bytes 131072 | tf_op jit(solution)/shard_map/all_to_all | solution.py:12
  125.2 0.8 reduce.2
  126.2 0.1 reshape.66
  126.3 7.8 %all_gather.13.xs_ref = f32[128,1536]{1,0:T(8,128)S(1)} all-gather(f32[32,1536]{1,0:T(8,128)S(1)} %pad_maximum_fusion.1), channel_id=1, replica_groups=mesh['vx'=2,'vy'=4,'col'=4] {'col'}, dimensions={0}, use_global_device_ids=true | all-gather | bytes 983040 | tf_op jit(solution)/shard_map/all_gather | solution.py:101
  134.1 20.7 %shard_map.69 = f32[128,1536]{1,0:T(8,128)} custom-call(f32[128,1536]{1,0:T(8,128)S(1)} %all_gather.13.xs_ref, s32[1,4096]{1,0:T(1,128)S(1)} %get-tuple-element.15.head_ref, s32[1,4096]{1,0:T(1,128)S(1)} %get-tuple-element.14.tail_ref, f32[1,4096]{1,0:T(1,128)S(1)} %bitcast.32), custom_call_target="tpu_custom_call" | custom-call | tf_op jit(solution)/shard_map/pallas_call | solution.py:82
  154.9 20.7 %reduce-scatter.5.cloned.1.call-done = f32[32,1536]{1,0:T(8,128)} async-done(((f32[128,1536]{1,0:T(8,128)}), f32[32,1536]{1,0:T(8,128)}) %reduce-scatter.5.cloned.1.call-update) | async-done | bytes 196624 | tf_op jit(solution)/shard_map/reduce_scatter | solution.py:108
  175.5 0.8 slice-done.1
  176.5 0.8 reshape.123
  177.3 5.5 %all-to-all-start.3 = ((f32[8,1,2048]{2,1,0:T(1,128)}), f32[8,1,2048]{2,1,0:T(1,128)S(1)}, u32[]{:S(2)}, u32[]{:S(2)}) async-start(f32[8,1,2048]{2,1,0:T(1,128)} %reshape.123), calls=%async_computation.5 | async-start | bytes 131072 | tf_op jit(solution)/shard_map/all_to_all | solution.py:12
  182.8 0.2 copy.50
  183.0 6.8 %all-to-all-done.3 = f32[8,1,2048]{2,1,0:T(1,128)S(1)} async-done(((f32[8,1,2048]{2,1,0:T(1,128)}), f32[8,1,2048]{2,1,0:T(1,128)S(1)}, u32[]{:S(2)}, u32[]{:S(2)}) %all-to-all-start.3) | async-done | bytes 65568 | tf_op jit(solution)/shard_map/all_to_all | solution.py:12
  189.8 0.8 reduce.3
  190.8 0.1 reshape.103
  190.9 0.1 copy.51
  191.0 3.5 %scatter_fusion.1 = f32[32,1024]{0,1:T(8,128)S(1)} fusion(f32[32,1024]{0,1:T(8,128)S(1)} %copy.50, s32[512]{0:T(512)S(1)} %bitcast.48, f32[512,32]{1,0:T(8,128)S(1)} %copy.51), kind=kCustom, calls=%fused_computation.4 | custom fusion | flops 16384 | bytes 198656 | tf_op jit(solution)/shard_map/scatter-add | solution.py:110
  194.5 0.2 copy.52
  194.7 0.1 multiply_reduce_fusion.1
  194.8 17.8 %all-reduce = (f32[32]{0:T(128)S(1)}, f32[32]{0:T(128)S(1)}) all-reduce(f32[32]{0:T(128)S(1)} %get-tuple-element.3, f32[32]{0:T(128)S(1)} %get-tuple-element.2), channel_id=1, replica_groups=mesh['vx'=2,'vy'=4,'col'=4] {'vx','vy'}, use_global_device_ids=true, to_apply=%region_7.0 | all-reduce | flops 64 | bytes 512 | tf_op jit(solution)/shard_map/psum | solution.py:115
  212.6 0.1 multiply_add_fusion
  212.8 0.2 copy.53
  213.0 1.0 gather_fusion.2
  214.0 0.1 copy.54
  214.1 0.1 reshape.125
  214.3 9.5 %all_to_all.26 = f32[8,1,2048]{2,1,0:T(1,128)S(1)} all-to-all(f32[8,1,2048]{2,1,0:T(1,128)S(1)} %reshape.125), channel_id=1, replica_groups=mesh['vx'=2,'vy'=4,'col'=4] {'vx','vy'}, dimensions={0} | all-to-all | bytes 131072 | tf_op jit(solution)/shard_map/all_to_all | solution.py:12
  223.8 0.8 reduce.4
  224.8 0.1 reshape.69
  224.9 7.7 %all_gather.14.xs_ref = f32[128,1536]{1,0:T(8,128)S(1)} all-gather(f32[32,1536]{1,0:T(8,128)S(1)} %pad_maximum_fusion.2), channel_id=1, replica_groups=mesh['vx'=2,'vy'=4,'col'=4] {'col'}, dimensions={0}, use_global_device_ids=true | all-gather | bytes 983040 | tf_op jit(solution)/shard_map/all_gather | solution.py:101
  232.6 9.1 %shard_map.70 = f32[1,4096]{1,0:T(1,128)S(1)} custom-call(f32[128,1536]{1,0:T(8,128)S(1)} %all_gather.14.xs_ref, s32[1,4096]{1,0:T(1,128)S(1)} %get-tuple-element.15.head_ref, s32[1,4096]{1,0:T(1,128)S(1)} %get-tuple-element.14.tail_ref, f32[1,4096]{1,0:T(1,128)S(1)} %bitcast.33), custom_call_target="tpu_custom_call" | custom-call | tf_op jit(solution)/shard_map/pallas_call | solution.py:82
  241.7 5.2 %all-gather = f32[1,16384]{1,0:T(1,128)S(1)} all-gather(f32[1,4096]{1,0:T(1,128)S(1)} %shard_map.70), channel_id=2, replica_groups=mesh['vx'=2,'vy'=4,'col'=4] {'col'}, dimensions={1}, use_global_device_ids=true | all-gather | bytes 81920 | tf_op jit(solution)/shard_map/all_gather | solution.py:146
  246.9 0.6 copy.63
  (47 shorter events, 1.6 us)
Async XLA Ops:
  10.2 8.1 %copy-start.4 = (s32[2,16384]{1,0:T(2,128)S(1)}, s32[2,16384]{1,0:T(2,128)}, u32[]{:S(2)}) copy-start(s32[2,16384]{1,0:T(2,128)} %param.7) | copy-start | bytes 393220
  11.0 14.2 %all-to-all-start = ((f32[8,1,2048]{2,1,0:T(1,128)}), f32[8,1,2048]{2,1,0:T(1,128)S(1)}, u32[]{:S(2)}, u32[]{:S(2)}) async-start(f32[8,1,2048]{2,1,0:T(1,128)} %reshape.117), calls=%async_computation | async-start | bytes 131072 | tf_op jit(solution)/shard_map/all_to_all | solution.py:12
  18.3 58.6 %reduce-scatter.3.cloned.1.call-start = ((), (), s32[]{:S(2)}) async-start(), calls=%async_computation.7 | async-start | bytes 983040 | tf_op jit(solution)/shard_map/reduce_scatter | solution.py:108
  26.8 0.9 copy-start
  57.1 0.7 copy-start.6
  76.9 0.8 slice-start
  77.8 6.5 %copy-start.2 = (f32[32,1536]{1,0:T(8,128)S(1)}, f32[32,1536]{1,0:T(8,128)}, u32[]{:S(2)}) copy-start(f32[32,1536]{1,0:T(8,128)} %reduce-scatter.3.cloned.1.call-done) | copy-start | bytes 589828
  78.6 5.7 %copy-start.5 = (f32[1024]{0:T(1024)S(1)}, f32[1024]{0:T(1024)}, u32[]{:S(2)}) copy-start(f32[1024]{0:T(1024)} %param.6) | copy-start | bytes 12292
  78.6 12.6 %all-to-all-start.1 = ((f32[8,1,2048]{2,1,0:T(1,128)}), f32[8,1,2048]{2,1,0:T(1,128)S(1)}, u32[]{:S(2)}, u32[]{:S(2)}) async-start(f32[8,1,2048]{2,1,0:T(1,128)} %reshape.119), calls=%async_computation.2 | async-start | bytes 131072 | tf_op jit(solution)/shard_map/all_to_all | solution.py:12
  84.2 91.3 %reduce-scatter.5.cloned.1.call-start = ((), (), s32[]{:S(2)}) async-start(), calls=%async_computation.8 | async-start | bytes 983040 | tf_op jit(solution)/shard_map/reduce_scatter | solution.py:108
  175.5 0.8 slice-start.1
  176.5 6.3 %copy-start.3 = (f32[32,1536]{1,0:T(8,128)S(1)}, f32[32,1536]{1,0:T(8,128)}, u32[]{:S(2)}) copy-start(f32[32,1536]{1,0:T(8,128)} %reduce-scatter.5.cloned.1.call-done) | copy-start | bytes 589828
  177.3 12.5 %all-to-all-start.3 = ((f32[8,1,2048]{2,1,0:T(1,128)}), f32[8,1,2048]{2,1,0:T(1,128)S(1)}, u32[]{:S(2)}, u32[]{:S(2)}) async-start(f32[8,1,2048]{2,1,0:T(1,128)} %reshape.123), calls=%async_computation.5 | async-start | bytes 131072 | tf_op jit(solution)/shard_map/all_to_all | solution.py:12
  212.7 12.1 %copy-start.1 = (f32[32,1024]{1,0:T(8,128)}, f32[32,1024]{1,0:T(8,128)S(1)}, u32[]{:S(2)}) copy-start(f32[32,1024]{1,0:T(8,128)S(1)} %multiply_add_fusion) | copy-start | bytes 393220
Sparse Core Ops, SparseCore 0:
  57.2 19.5 reduce-scatter.2
  155.0 20.5 reduce-scatter.4

commit v3 on v1

--- a/solution.py
+++ b/solution.py
@@ -24,48 +24,35 @@
     return 1024 if rows <= 2048 else 256
 
 
-def flow_kernel(local, scatter):
+def flow_kernel(scatter):
     def kernel(xs_ref, head_ref, tail_ref, w_ref, out_ref, *acc):
         step = pl.program_id(0)
         width, rows = xs_ref.shape
         tile = head_ref.shape[1]
-        head = head_ref[...]
-        tail = tail_ref[...]
-        g_head = (lax.broadcasted_iota(jnp.int32, (local, tile), 0) == head).astype(jnp.bfloat16)
-        g_tail = (lax.broadcasted_iota(jnp.int32, (rows, tile), 0) == tail).astype(jnp.bfloat16)
-        xs = split3(xs_ref[...])
-        near = jnp.dot(xs[:, :local], g_head, preferred_element_type=jnp.float32)
-        far = jnp.dot(xs, g_tail, preferred_element_type=jnp.float32)
-        gap = near - far
+        index = lax.broadcasted_iota(jnp.int32, (rows, tile), 0)
+        ends = (index == head_ref[...]).astype(jnp.float32) - (index == tail_ref[...]).astype(jnp.float32)
+        ends = ends.astype(jnp.bfloat16)
+        gap = jnp.dot(split3(xs_ref[...]), ends, preferred_element_type=jnp.float32)
         gap = gap[:width] + gap[width:2 * width] + gap[2 * width:]
         if not scatter:
             out_ref[...] = jnp.sum(gap * gap, axis=0, keepdims=True)
             return
-        acc_head, acc_tail = acc
-
+        (total,) = acc
         flow = split3(gap * w_ref[...])
         dims = (((1,), (1,)), ((), ()))
-        first = step == 0
-        acc_head[...] = jnp.where(first, 0.0, acc_head[...]) + lax.dot_general(
-            flow, g_head, dims, preferred_element_type=jnp.float32
-        )
-        acc_tail[...] = jnp.where(first, 0.0, acc_tail[...]) + lax.dot_general(
-            flow, g_tail, dims, preferred_element_type=jnp.float32
+        total[...] = jnp.where(step == 0, 0.0, total[...]) + lax.dot_general(
+            flow, ends, dims, preferred_element_type=jnp.float32
         )
 
         @pl.when(step == pl.num_programs(0) - 1)
         def _():
-            th = acc_head[...]
-            tt = acc_tail[...]
-            th = th[:width] + th[width:2 * width] + th[2 * width:]
-            tt = tt[:width] + tt[width:2 * width] + tt[2 * width:]
-            out_ref[:, :local] = th - tt[:, :local]
-            out_ref[:, local:] = -tt[:, local:]
+            sums = total[...]
+            out_ref[...] = sums[:width] + sums[width:2 * width] + sums[2 * width:]
 
     return kernel
 
 
-def edge_pass(extended, head_rows, tail_slots, weights, local, scatter):
+def edge_pass(extended, head_rows, tail_slots, weights, scatter):
     width, rows = extended.shape
     edges = head_rows.shape[1]
     tile = edge_tile(rows)
@@ -74,13 +61,13 @@
     if scatter:
         out_shape = jax.ShapeDtypeStruct((width, rows), jnp.float32)
         out_spec = pl.BlockSpec((width, rows), lambda i: (0, 0))
-        scratch = [pltpu.VMEM((3 * width, local), jnp.float32), pltpu.VMEM((3 * width, rows), jnp.float32)]
+        scratch = [pltpu.VMEM((3 * width, rows), jnp.float32)]
     else:
         out_shape = jax.ShapeDtypeStruct((1, edges), jnp.float32)
         out_spec = edge_spec
         scratch = []
     return pl.pallas_call(
-        flow_kernel(local, scatter),
+        flow_kernel(scatter),
         grid=(edges // tile,),
         in_specs=[full, edge_spec, edge_spec, edge_spec],
         out_specs=out_spec,
@@ -97,11 +84,14 @@
     return jnp.concatenate([field, mirrored.reshape(field.shape[0], -1)], axis=1)
 
 
+def gathered(field, halo_rows):
+    return lax.all_gather(extend(field, halo_rows), "col", axis=0, tiled=True)
+
+
 def operate(field, shift, head_rows, tail_slots, weights, halo_rows):
     count = field.shape[1]
     width = field.shape[0]
-    extended = extend(field, halo_rows)
-    summed = edge_pass(extended, head_rows, tail_slots, weights, count, True)
+    summed = edge_pass(extend(field, halo_rows), head_rows, tail_slots, weights, True)
     returned = trade(summed[:, count:].reshape(width, halo_rows.shape[0], halo_rows.shape[1]))
     local = summed[:, :count].at[:, halo_rows.reshape(-1)].add(returned.reshape(width, -1))
     return shift * field + local
@@ -117,6 +107,9 @@
     head_rows = edge_ends[0:1]
     tail_slots = edge_ends[1:2]
     weights = weights[None, :]
+    share = edge_ends.shape[1] // lax.axis_size("col")
+    start = lax.axis_index("col") * share
+    quarter = [lax.dynamic_slice_in_dim(item, start, share, axis=1) for item in (head_rows, tail_slots, weights)]
     solution = jnp.zeros_like(right_side)
     residual = right_side
     image = operate(residual, shift, head_rows, tail_slots, weights, halo_rows)
@@ -135,9 +128,8 @@
             direction = residual + ratio[:, None] * direction
             along = image + ratio[:, None] * along
             norm_now = norm_next
-    extended = extend(solution, halo_rows)
-    partial_total = edge_pass(extended, head_rows, tail_slots, weights, solution.shape[1], False)[0]
-    resistance = lax.psum(partial_total, "col")
+    total = edge_pass(gathered(solution, halo_rows), *quarter, False)[0]
+    resistance = lax.all_gather(total, "col", axis=0, tiled=True)
     return (solution, resistance)
 
 

time: 282 us -> 224 us (0.79)
  Pallas kernels: 123 us -> 91 us
  waiting for transfers between devices: 48.3 us -> 33.9 us
  between operations: 14.4 us -> 1.02 us
  starting transfers between devices: 14.4 us -> 20.9 us
  blocking collectives: 54.6 us -> 49.4 us
    pallas_call x3, Pallas kernels: 123 us -> 91 us  [edge_pass(): pl.pallas_call(flow_kernel(scatter), grid=(edges // tile,), in_specs=[ful...]
    psum x1 -> x0, waiting for transfers between devices: 28.5 us -> none  [body(): resistance = lax.psum(partial_total, 'col')]
    all_to_all x2 -> x0, blocking collectives: 19.1 us -> none  [trade(): lax.all_to_all(blocks, ('vx', 'vy'), split_axis=1, concat_axis=1, tiled=T...]
    all_to_all x3 -> x5, waiting for transfers between devices: 19.8 us -> 33.9 us  [trade(): lax.all_to_all(blocks, ('vx', 'vy'), split_axis=1, concat_axis=1, tiled=T...]
    all_gather x0 -> x2, blocking collectives: none -> 13.9 us  [the longest x1 8.63 us: gathered(): return lax.all_gather(extend(field, halo_rows), 'col', axis=0, tiled=True)]
    all_to_all x3 -> x5, starting transfers between devices: 14.2 us -> 20.9 us  [trade(): lax.all_to_all(blocks, ('vx', 'vy'), split_axis=1, concat_axis=1, tiled=T...]
  transfers between devices with their start and end apart: 4 -> 5, of which waited for: 4 -> 5; matrix products, arithmetic and copies ran while one was open for 0% -> 0% of each run, Pallas kernels for 0% -> 0%
where the time goes in v3:
time: 224 us; the launch traced here: 223 us
  Pallas kernels  91 us (41%)
  blocking collectives  49.4 us (22%)
  waiting for transfers between devices  33.9 us (15%)
  starting transfers between devices  20.9 us (9%)
  local copies, waits for them, and re-layouts  14.4 us (6%)
  other arithmetic  12.8 us (6%)
    pallas_call x3, Pallas kernels, edge_pass(): pl.pallas_call(flow_kernel(scatter), grid=(edges // tile,), in_specs=[ful...  91 us
    psum x2, blocking collectives, two_products(): lax.psum((jnp.sum(residual * residual, axis=1), jnp.sum(residual * image,...  35.5 us
    all_to_all x5, waiting for transfers between devices, trade(): lax.all_to_all(blocks, ('vx', 'vy'), split_axis=1, concat_axis=1, tiled=T...  33.9 us
    all_to_all x5, starting transfers between devices, trade(): lax.all_to_all(blocks, ('vx', 'vy'), split_axis=1, concat_axis=1, tiled=T...  20.9 us
    all_gather x1, blocking collectives, gathered(): return lax.all_gather(extend(field, halo_rows), 'col', axis=0, tiled=True)  8.63 us
    unnamed x27, local copies, waits for them, and re-layouts  7.64 us
    scatter-add x2, other arithmetic, operate(): summed[:, :count].at[:, halo_rows.reshape(-1)]  7.19 us
    all_gather x1, blocking collectives, body(): resistance = lax.all_gather(total, 'col', axis=0, tiled=True)  5.25 us
  transfers between devices with their start and end apart: 5, of which 5 were waited for; matrix products, arithmetic and copies ran while one was open for 0% of the time, Pallas kernels for 0%

profile of v3, /device:TPU:0, one launch (start us, length us, event | category | flops | bytes accessed | tf_op | source)
XLA Modules:
  0.0 223.5 jit_solution(912595727207635167)
XLA Ops:
  0.6 0.7 compare_select_fusion.1
  1.4 1.1 copy.43
  2.5 1.0 gather_fusion
  3.6 0.1 copy.37
  3.7 0.8 reshape.117
  4.5 7.4 %all-to-all-start = ((f32[8,1,2048]{2,1,0:T(1,128)}), f32[8,1,2048]{2,1,0:T(1,128)S(1)}, u32[]{:S(2)}, u32[]{:S(2)}) async-start(f32[8,1,2048]{2,1,0:T(1,128)} %reshape.117), calls=%async_computation | async-start | bytes 131072 | tf_op jit(solution)/shard_map/all_to_all | solution.py:12
  11.9 0.1 fusion
  12.1 6.8 %all-to-all-done = f32[8,1,2048]{2,1,0:T(1,128)S(1)} async-done(((f32[8,1,2048]{2,1,0:T(1,128)}), f32[8,1,2048]{2,1,0:T(1,128)S(1)}, u32[]{:S(2)}, u32[]{:S(2)}) %all-to-all-start) | async-done | bytes 65568 | tf_op jit(solution)/shard_map/all_to_all | solution.py:12
  18.8 0.6 broadcast.46
  19.4 0.8 reduce
  20.3 0.1 reshape.118
  20.5 0.1 reshape.62
  20.6 0.8 copy-done.1
  21.4 0.8 copy-done
  22.2 41.8 %shard_map.68 = f32[32,1536]{1,0:T(8,128)S(1)} custom-call(f32[32,1536]{1,0:T(8,128)S(1)} %pad_maximum_fusion.xs_ref, s32[1,16384]{1,0:T(1,128)S(1)} %get-tuple-element.13.head_ref, s32[1,16384]{1,0:T(1,128)S(1)} %get-tuple-element.12.tail_ref, f32[1,16384]{1,0:T(1,128)S(1)} %bitcast.32), custom_call_target="tpu_custom_call" | custom-call | tf_op jit(solution)/shard_map/pallas_call | solution.py:69
  64.0 0.1 reshape.64
  64.1 0.8 reshape.119
  64.9 3.5 %all-to-all-start.1 = ((f32[8,1,2048]{2,1,0:T(1,128)}), f32[8,1,2048]{2,1,0:T(1,128)S(1)}, u32[]{:S(2)}, u32[]{:S(2)}) async-start(f32[8,1,2048]{2,1,0:T(1,128)} %reshape.119), calls=%async_computation.1 | async-start | bytes 131072 | tf_op jit(solution)/shard_map/all_to_all | solution.py:12
  68.4 0.1 multiply_reduce_fusion.3
  68.5 0.2 copy.41
  68.7 6.6 %all-to-all-done.1 = f32[8,1,2048]{2,1,0:T(1,128)S(1)} async-done(((f32[8,1,2048]{2,1,0:T(1,128)}), f32[8,1,2048]{2,1,0:T(1,128)S(1)}, u32[]{:S(2)}, u32[]{:S(2)}) %all-to-all-start.1) | async-done | bytes 65568 | tf_op jit(solution)/shard_map/all_to_all | solution.py:12
  75.3 0.8 reduce.1
  76.2 0.1 reshape.120
  76.3 0.1 reshape.95
  76.4 0.1 copy.42
  76.6 3.5 %scatter_fusion = f32[32,1024]{0,1:T(8,128)S(1)} fusion(f32[32,1024]{0,1:T(8,128)S(1)} %copy.41, s32[512]{0:T(512)S(1)} %bitcast.48, f32[512,32]{1,0:T(8,128)S(1)} %copy.42), kind=kCustom, calls=%fused_computation.3 | custom fusion | flops 16384 | bytes 198656 | tf_op jit(solution)/shard_map/scatter-add | solution.py:96
  80.1 0.2 multiply_reduce_fusion
  80.2 0.2 copy.44
  80.4 17.8 %all-reduce.1 = (f32[32]{0:T(128)S(1)}, f32[32]{0:T(128)S(1)}) all-reduce(f32[32]{0:T(128)S(1)} %get-tuple-element.10, f32[32]{0:T(128)S(1)} %multiply_reduce_fusion), channel_id=1, replica_groups=mesh['vx'=2,'vy'=4,'col'=4] {'vx','vy'}, use_global_device_ids=true, to_apply=%region_1.0 | all-reduce | flops 64 | bytes 512 | tf_op jit(solution)/shard_map/psum | solution.py:101
  98.3 0.2 copy.45
  98.5 1.0 gather_fusion.1
  99.5 0.1 copy.46
  99.6 0.8 reshape.121
  100.4 3.4 %all-to-all-start.2 = ((f32[8,1,2048]{2,1,0:T(1,128)}), f32[8,1,2048]{2,1,0:T(1,128)S(1)}, u32[]{:S(2)}, u32[]{:S(2)}) async-start(f32[8,1,2048]{2,1,0:T(1,128)} %reshape.121), calls=%async_computation.2 | async-start | bytes 131072 | tf_op jit(solution)/shard_map/all_to_all | solution.py:12
  103.8 6.9 %all-to-all-done.2 = f32[8,1,2048]{2,1,0:T(1,128)S(1)} async-done(((f32[8,1,2048]{2,1,0:T(1,128)}), f32[8,1,2048]{2,1,0:T(1,128)S(1)}, u32[]{:S(2)}, u32[]{:S(2)}) %all-to-all-start.2) | async-done | bytes 65568 | tf_op jit(solution)/shard_map/all_to_all | solution.py:12
  110.7 0.8 reduce.2
  111.7 0.1 reshape.66
  111.8 41.8 %shard_map.69 = f32[32,1536]{1,0:T(8,128)S(1)} custom-call(f32[32,1536]{1,0:T(8,128)S(1)} %pad_maximum_fusion.1.xs_ref, s32[1,16384]{1,0:T(1,128)S(1)} %get-tuple-element.13.head_ref, s32[1,16384]{1,0:T(1,128)S(1)} %get-tuple-element.12.tail_ref, f32[1,16384]{1,0:T(1,128)S(1)} %bitcast.33), custom_call_target="tpu_custom_call" | custom-call | tf_op jit(solution)/shard_map/pallas_call | solution.py:69
  153.8 0.8 reshape.123
  154.5 3.4 %all-to-all-start.3 = ((f32[8,1,2048]{2,1,0:T(1,128)}), f32[8,1,2048]{2,1,0:T(1,128)S(1)}, u32[]{:S(2)}, u32[]{:S(2)}) async-start(f32[8,1,2048]{2,1,0:T(1,128)} %reshape.123), calls=%async_computation.3 | async-start | bytes 131072 | tf_op jit(solution)/shard_map/all_to_all | solution.py:12
  157.9 0.2 copy.50
  158.1 6.7 %all-to-all-done.3 = f32[8,1,2048]{2,1,0:T(1,128)S(1)} async-done(((f32[8,1,2048]{2,1,0:T(1,128)}), f32[8,1,2048]{2,1,0:T(1,128)S(1)}, u32[]{:S(2)}, u32[]{:S(2)}) %all-to-all-start.3) | async-done | bytes 65568 | tf_op jit(solution)/shard_map/all_to_all | solution.py:12
  164.8 0.8 reduce.3
  165.7 0.1 reshape.124
  165.9 0.1 reshape.103
  165.9 0.1 copy.51
  166.1 3.7 %scatter_fusion.1 = f32[32,1024]{0,1:T(8,128)S(1)} fusion(f32[32,1024]{0,1:T(8,128)S(1)} %copy.50, s32[512]{0:T(512)S(1)} %bitcast.49, f32[512,32]{1,0:T(8,128)S(1)} %copy.51), kind=kCustom, calls=%fused_computation.4 | custom fusion | flops 16384 | bytes 198656 | tf_op jit(solution)/shard_map/scatter-add | solution.py:96
  169.8 0.2 copy.52
  169.9 0.1 multiply_reduce_fusion.1
  170.1 17.8 %all-reduce = (f32[32]{0:T(128)S(1)}, f32[32]{0:T(128)S(1)}) all-reduce(f32[32]{0:T(128)S(1)} %get-tuple-element.3, f32[32]{0:T(128)S(1)} %get-tuple-element.2), channel_id=1, replica_groups=mesh['vx'=2,'vy'=4,'col'=4] {'vx','vy'}, use_global_device_ids=true, to_apply=%region_6.0 | all-reduce | flops 64 | bytes 512 | tf_op jit(solution)/shard_map/psum | solution.py:101
  187.9 0.1 multiply_add_fusion
  188.0 0.2 copy.53
  188.2 1.0 gather_fusion.2
  189.2 0.1 copy.54
  189.4 0.8 reshape.125
  190.1 3.4 %all-to-all-start.4 = ((f32[8,1,2048]{2,1,0:T(1,128)}), f32[8,1,2048]{2,1,0:T(1,128)S(1)}, u32[]{:S(2)}, u32[]{:S(2)}) async-start(f32[8,1,2048]{2,1,0:T(1,128)} %reshape.125), calls=%async_computation.4 | async-start | bytes 131072 | tf_op jit(solution)/shard_map/all_to_all | solution.py:12
  193.5 6.9 %all-to-all-done.4 = f32[8,1,2048]{2,1,0:T(1,128)S(1)} async-done(((f32[8,1,2048]{2,1,0:T(1,128)}), f32[8,1,2048]{2,1,0:T(1,128)S(1)}, u32[]{:S(2)}, u32[]{:S(2)}) %all-to-all-start.4) | async-done | bytes 65568 | tf_op jit(solution)/shard_map/all_to_all | solution.py:12
  200.4 0.8 reduce.4
  201.3 0.1 reshape.126
  201.4 0.1 reshape.69
  201.6 8.6 %all_gather.6.xs_ref = f32[128,1536]{1,0:T(8,128)S(1)} all-gather(f32[32,1536]{1,0:T(8,128)S(1)} %pad_maximum_fusion.2), channel_id=1, replica_groups=mesh['vx'=2,'vy'=4,'col'=4] {'col'}, dimensions={0}, use_global_device_ids=true | all-gather | bytes 983040 | tf_op jit(solution)/shard_map/all_gather | solution.py:88
  210.2 7.4 %shard_map.70 = f32[1,4096]{1,0:T(1,128)S(1)} custom-call(f32[128,1536]{1,0:T(8,128)S(1)} %all_gather.6.xs_ref, s32[1,4096]{1,0:T(1,128)S(1)} %get-tuple-element.15.head_ref, s32[1,4096]{1,0:T(1,128)S(1)} %get-tuple-element.14.tail_ref, f32[1,4096]{1,0:T(1,128)S(1)} %bitcast.34), custom_call_target="tpu_custom_call" | custom-call | tf_op jit(solution)/shard_map/pallas_call | solution.py:69
  217.6 5.2 %all-gather = f32[1,16384]{1,0:T(1,128)S(1)} all-gather(f32[1,4096]{1,0:T(1,128)S(1)} %shard_map.70), channel_id=2, replica_groups=mesh['vx'=2,'vy'=4,'col'=4] {'col'}, dimensions={1}, use_global_device_ids=true | all-gather | bytes 81920 | tf_op jit(solution)/shard_map/all_gather | solution.py:132
  222.8 0.6 copy.63
  (37 shorter events, 1.1 us)
Async XLA Ops:
  3.7 8.2 %copy-start.3 = (s32[2,16384]{1,0:T(2,128)S(1)}, s32[2,16384]{1,0:T(2,128)}, u32[]{:S(2)}) copy-start(s32[2,16384]{1,0:T(2,128)} %param.7) | copy-start | bytes 393220
  4.5 7.4 %copy-start.5 = (s32[8,64]{1,0:T(8,128)S(1)}, s32[8,64]{1,0:T(8,128)}, u32[]{:S(2)}) copy-start(s32[8,64]{1,0:T(8,128)} %param.9) | copy-start | bytes 6148
  4.5 14.4 %all-to-all-start = ((f32[8,1,2048]{2,1,0:T(1,128)}), f32[8,1,2048]{2,1,0:T(1,128)S(1)}, u32[]{:S(2)}, u32[]{:S(2)}) async-start(f32[8,1,2048]{2,1,0:T(1,128)} %reshape.117), calls=%async_computation | async-start | bytes 131072 | tf_op jit(solution)/shard_map/all_to_all | solution.py:12
  20.5 0.9 copy-start.1
  21.4 0.8 copy-start
  64.9 3.5 %copy-start.4 = (f32[1024]{0:T(1024)S(1)}, f32[1024]{0:T(1024)}, u32[]{:S(2)}) copy-start(f32[1024]{0:T(1024)} %param.6) | copy-start | bytes 12292
  64.9 10.4 %all-to-all-start.1 = ((f32[8,1,2048]{2,1,0:T(1,128)}), f32[8,1,2048]{2,1,0:T(1,128)S(1)}, u32[]{:S(2)}, u32[]{:S(2)}) async-start(f32[8,1,2048]{2,1,0:T(1,128)} %reshape.119), calls=%async_computation.1 | async-start | bytes 131072 | tf_op jit(solution)/shard_map/all_to_all | solution.py:12
  100.4 10.3 %all-to-all-start.2 = ((f32[8,1,2048]{2,1,0:T(1,128)}), f32[8,1,2048]{2,1,0:T(1,128)S(1)}, u32[]{:S(2)}, u32[]{:S(2)}) async-start(f32[8,1,2048]{2,1,0:T(1,128)} %reshape.121), calls=%async_computation.2 | async-start | bytes 131072 | tf_op jit(solution)/shard_map/all_to_all | solution.py:12
  154.5 10.3 %all-to-all-start.3 = ((f32[8,1,2048]{2,1,0:T(1,128)}), f32[8,1,2048]{2,1,0:T(1,128)S(1)}, u32[]{:S(2)}, u32[]{:S(2)}) async-start(f32[8,1,2048]{2,1,0:T(1,128)} %reshape.123), calls=%async_computation.3 | async-start | bytes 131072 | tf_op jit(solution)/shard_map/all_to_all | solution.py:12
  188.0 13.6 %copy-start.2 = (f32[32,1024]{1,0:T(8,128)}, f32[32,1024]{1,0:T(8,128)S(1)}, u32[]{:S(2)}) copy-start(f32[32,1024]{1,0:T(8,128)S(1)} %multiply_add_fusion) | copy-start | bytes 393220
  190.1 10.3 %all-to-all-start.4 = ((f32[8,1,2048]{2,1,0:T(1,128)}), f32[8,1,2048]{2,1,0:T(1,128)S(1)}, u32[]{:S(2)}, u32[]{:S(2)}) async-start(f32[8,1,2048]{2,1,0:T(1,128)} %reshape.125), calls=%async_computation.4 | async-start | bytes 131072 | tf_op jit(solution)/shard_map/all_to_all | solution.py:12

commit v4 on v3

--- a/solution.py
+++ b/solution.py
@@ -25,7 +25,8 @@
 
 
 def flow_kernel(scatter):
-    def kernel(xs_ref, head_ref, tail_ref, w_ref, out_ref, *acc):
+    def kernel(xs_ref, head_ref, tail_ref, w_ref, *out_ref):
+        out_ref, acc = (out_ref[:2], out_ref[2:]) if scatter else (out_ref[0], ())
         step = pl.program_id(0)
         width, rows = xs_ref.shape
         tile = head_ref.shape[1]
@@ -38,7 +39,12 @@
             out_ref[...] = jnp.sum(gap * gap, axis=0, keepdims=True)
             return
         (total,) = acc
-        flow = split3(gap * w_ref[...])
+        energy_ref = out_ref[1]
+        out_ref = out_ref[0]
+        weighted = gap * w_ref[...]
+        energy = jnp.sum(gap * weighted, axis=1, keepdims=True)
+        energy_ref[...] = jnp.where(step == 0, 0.0, energy_ref[...]) + energy
+        flow = split3(weighted)
         dims = (((1,), (1,)), ((), ()))
         total[...] = jnp.where(step == 0, 0.0, total[...]) + lax.dot_general(
             flow, ends, dims, preferred_element_type=jnp.float32
@@ -59,8 +65,8 @@
     edge_spec = pl.BlockSpec((1, tile), lambda i: (0, i))
     full = pl.BlockSpec((width, rows), lambda i: (0, 0))
     if scatter:
-        out_shape = jax.ShapeDtypeStruct((width, rows), jnp.float32)
-        out_spec = pl.BlockSpec((width, rows), lambda i: (0, 0))
+        out_shape = (jax.ShapeDtypeStruct((width, rows), jnp.float32), jax.ShapeDtypeStruct((width, 1), jnp.float32))
+        out_spec = (pl.BlockSpec((width, rows), lambda i: (0, 0)), pl.BlockSpec((width, 1), lambda i: (0, 0)))
         scratch = [pltpu.VMEM((3 * width, rows), jnp.float32)]
     else:
         out_shape = jax.ShapeDtypeStruct((1, edges), jnp.float32)
@@ -91,16 +97,18 @@
 def operate(field, shift, head_rows, tail_slots, weights, halo_rows):
     count = field.shape[1]
     width = field.shape[0]
-    summed = edge_pass(extend(field, halo_rows), head_rows, tail_slots, weights, True)
-    returned = trade(summed[:, count:].reshape(width, halo_rows.shape[0], halo_rows.shape[1]))
-    local = summed[:, :count].at[:, halo_rows.reshape(-1)].add(returned.reshape(width, -1))
-    return shift * field + local
-
-
-def two_products(residual, image):
-    return lax.psum(
-        (jnp.sum(residual * residual, axis=1), jnp.sum(residual * image, axis=1)), ("vx", "vy")
+    peers, cap = halo_rows.shape
+    summed, energy = edge_pass(extend(field, halo_rows), head_rows, tail_slots, weights, True)
+    squares = field * field
+    own = jnp.stack([jnp.sum(squares, axis=1), jnp.sum(shift * squares, axis=1) + energy[:, 0]], axis=1)
+    sent = jnp.concatenate(
+        [summed[:, count:].reshape(width, peers, cap), jnp.broadcast_to(own[:, None, :], (width, peers, 2))], axis=2
     )
+    got = trade(sent)
+    returned = got[:, :, :cap].reshape(width, -1)
+    norm, product = jnp.sum(got[:, :, cap:], axis=1).T
+    local = summed[:, :count].at[:, halo_rows.reshape(-1)].add(returned)
+    return shift * field + local, norm, product
 
 
 def body(right_side, shift, edge_ends, weights, halo_rows):
@@ -112,8 +120,7 @@
     quarter = [lax.dynamic_slice_in_dim(item, start, share, axis=1) for item in (head_rows, tail_slots, weights)]
     solution = jnp.zeros_like(right_side)
     residual = right_side
-    image = operate(residual, shift, head_rows, tail_slots, weights, halo_rows)
-    norm_now, product = two_products(residual, image)
+    image, norm_now, product = operate(residual, shift, head_rows, tail_slots, weights, halo_rows)
     alpha = norm_now / product
     direction = residual
     along = image
@@ -121,8 +128,7 @@
         solution = solution + alpha[:, None] * direction
         residual = residual - alpha[:, None] * along
         if step + 1 < ITERS:
-            image = operate(residual, shift, head_rows, tail_slots, weights, halo_rows)
-            norm_next, product = two_products(residual, image)
+            image, norm_next, product = operate(residual, shift, head_rows, tail_slots, weights, halo_rows)
             ratio = norm_next / norm_now
             alpha = norm_next / (product - ratio * norm_next / alpha)
             direction = residual + ratio[:, None] * direction

time: 224 us -> 185 us (0.83)
  blocking collectives: 49.4 us -> 13.9 us
  other arithmetic: 12.8 us -> 9.13 us
    psum x2 -> x0, blocking collectives: 35.5 us -> none  [two_products(): lax.psum((jnp.sum(residual * residual, axis=1), jnp.sum(residual * image,...]
    scatter-add x2 -> x1, other arithmetic: 7.19 us -> 3.51 us  [operate(): local = summed[:, :count].at[:, halo_rows.reshape(-1)].add(returned)]
    unnamed x27 -> x23, local copies, waits for them, and re-layouts: 7.64 us -> 7.18 us
where the time goes in v4:
time: 185 us; the launch traced here: 184 us
  Pallas kernels  91 us (49%)
  waiting for transfers between devices  34.6 us (19%)
  starting transfers between devices  20.7 us (11%)
  local copies, waits for them, and re-layouts  14.1 us (8%)
  blocking collectives  13.9 us (8%)
  other arithmetic  9.13 us (5%)
    pallas_call x3, Pallas kernels, edge_pass(): pl.pallas_call(flow_kernel(scatter), grid=(edges // tile,), in_specs=[ful...  91 us
    all_to_all x5, waiting for transfers between devices, trade(): lax.all_to_all(blocks, ('vx', 'vy'), split_axis=1, concat_axis=1, tiled=T...  34.6 us
    all_to_all x5, starting transfers between devices, trade(): lax.all_to_all(blocks, ('vx', 'vy'), split_axis=1, concat_axis=1, tiled=T...  20.7 us
    all_gather x1, blocking collectives, gathered(): return lax.all_gather(extend(field, halo_rows), 'col', axis=0, tiled=True)  8.63 us
    unnamed x23, local copies, waits for them, and re-layouts  7.18 us
    all_gather x1, blocking collectives, body(): resistance = lax.all_gather(total, 'col', axis=0, tiled=True)  5.25 us
  transfers between devices with their start and end apart: 5, of which 5 were waited for; matrix products, arithmetic and copies ran while one was open for 0% of the time, Pallas kernels for 0%

profile of v4, /device:TPU:0, one launch (start us, length us, event | category | flops | bytes accessed | tf_op | source)
XLA Modules:
  0.0 184.4 jit_solution(9619751059679274633)
XLA Ops:
  0.6 0.7 compare_select_fusion.1
  1.4 1.1 copy.64
  2.5 1.0 gather_fusion
  3.6 0.1 copy.65
  3.7 0.8 reshape.155
  4.5 7.2 %all-to-all-start = ((f32[8,1,2048]{2,1,0:T(1,128)}), f32[8,1,2048]{2,1,0:T(1,128)S(1)}, u32[]{:S(2)}, u32[]{:S(2)}) async-start(f32[8,1,2048]{2,1,0:T(1,128)} %reshape.155), calls=%async_computation | async-start | bytes 131072 | tf_op jit(solution)/shard_map/all_to_all | solution.py:12
  11.7 0.1 fusion
  11.8 0.6 copy-done.5
  12.5 6.2 %all-to-all-done = f32[8,1,2048]{2,1,0:T(1,128)S(1)} async-done(((f32[8,1,2048]{2,1,0:T(1,128)}), f32[8,1,2048]{2,1,0:T(1,128)S(1)}, u32[]{:S(2)}, u32[]{:S(2)}) %all-to-all-start) | async-done | bytes 65568 | tf_op jit(solution)/shard_map/all_to_all | solution.py:12
  18.7 0.6 broadcast.39
  19.3 0.8 reduce.8
  20.2 0.1 reshape.156
  20.3 0.1 reshape.105
  20.4 0.8 copy-done.1
  21.2 0.8 copy-done
  22.1 41.8 %shard_map.68 = (f32[32,1536]{1,0:T(8,128)S(1)}, f32[32,1]{1,0:T(8,128)S(1)}) custom-call(f32[32,1536]{1,0:T(8,128)S(1)} %pad_maximum_fusion.xs_ref, s32[1,16384]{1,0:T(1,128)S(1)} %get-tuple-element.23.head_ref, s32[1,16384]{1,0:T(1,128)S(1)} %get-tuple-element.22.tail_ref, f32[1,16384]{1,0:T(1,128)S(1)} %bitcast.30), custom_call_target="tpu_custom_call" | custom-call | tf_op jit(solution)/shard_map/pallas_call | solution.py:75
  63.9 0.7 copy-done.4
  64.6 0.1 multiply_reduce_fusion.3
  64.7 0.1 copy.67
  64.8 0.1 copy.68
  65.1 0.8 pad_maximum_fusion.3
  65.9 3.4 %all-to-all-start.1 = ((f32[32,8,66]{2,0,1:T(8,128)}), f32[32,8,66]{2,0,1:T(8,128)S(1)}, u32[]{:S(2)}, u32[]{:S(2)}) async-start(f32[32,8,66]{2,0,1:T(8,128)} %pad_maximum_fusion.3), calls=%async_computation.1 | async-start | bytes 262144 | tf_op jit(solution)/shard_map/all_to_all | solution.py:12
  69.3 0.2 copy.72
  69.5 7.2 %all-to-all-done.1 = f32[32,8,66]{2,0,1:T(8,128)S(1)} async-done(((f32[32,8,66]{2,0,1:T(8,128)}), f32[32,8,66]{2,0,1:T(8,128)S(1)}, u32[]{:S(2)}, u32[]{:S(2)}) %all-to-all-start.1) | async-done | bytes 67616 | tf_op jit(solution)/shard_map/all_to_all | solution.py:12
  76.7 0.1 slice_reduce_fusion.1
  76.8 0.2 slice_reduce_fusion.4
  77.0 0.1 copy.71
  77.1 0.1 reshape.137
  77.2 0.1 copy.73
  77.3 3.5 %scatter_fusion = f32[32,1024]{0,1:T(8,128)S(1)} fusion(f32[32,1024]{0,1:T(8,128)S(1)} %copy.72, s32[512]{0:T(512)S(1)} %bitcast.44, f32[512,32]{1,0:T(8,128)S(1)} %copy.73), kind=kCustom, calls=%fused_computation.3 | custom fusion | flops 16384 | bytes 198656 | tf_op jit(solution)/shard_map/scatter-add | solution.py:110
  80.8 0.2 copy.74
  81.0 0.2 multiply_reduce_fusion.2
  81.2 0.2 copy.75
  81.4 1.0 gather_fusion.1
  82.5 0.1 copy.76
  82.6 0.8 reshape.157
  83.4 3.4 %all-to-all-start.2 = ((f32[8,1,2048]{2,1,0:T(1,128)}), f32[8,1,2048]{2,1,0:T(1,128)S(1)}, u32[]{:S(2)}, u32[]{:S(2)}) async-start(f32[8,1,2048]{2,1,0:T(1,128)} %reshape.157), calls=%async_computation.2 | async-start | bytes 131072 | tf_op jit(solution)/shard_map/all_to_all | solution.py:12
  86.7 0.1 copy.78
  86.8 0.1 copy.79
  86.9 6.8 %all-to-all-done.2 = f32[8,1,2048]{2,1,0:T(1,128)S(1)} async-done(((f32[8,1,2048]{2,1,0:T(1,128)}), f32[8,1,2048]{2,1,0:T(1,128)S(1)}, u32[]{:S(2)}, u32[]{:S(2)}) %all-to-all-start.2) | async-done | bytes 65568 | tf_op jit(solution)/shard_map/all_to_all | solution.py:12
  93.7 0.8 reduce.9
  94.5 0.1 reshape.158
  94.7 0.1 reshape.109
  94.8 41.8 %shard_map.69 = (f32[32,1536]{1,0:T(8,128)S(1)}, f32[32,1]{1,0:T(8,128)S(1)}) custom-call(f32[32,1536]{1,0:T(8,128)S(1)} %pad_maximum_fusion.1.xs_ref, s32[1,16384]{1,0:T(1,128)S(1)} %get-tuple-element.23.head_ref, s32[1,16384]{1,0:T(1,128)S(1)} %get-tuple-element.22.tail_ref, f32[1,16384]{1,0:T(1,128)S(1)} %bitcast.31), custom_call_target="tpu_custom_call" | custom-call | tf_op jit(solution)/shard_map/pallas_call | solution.py:75
  136.6 0.1 reshape.110
  136.9 0.8 pad_maximum_fusion.4
  137.6 3.4 %all-to-all-start.3 = ((f32[32,8,66]{2,0,1:T(8,128)}), f32[32,8,66]{2,0,1:T(8,128)S(1)}, u32[]{:S(2)}, u32[]{:S(2)}) async-start(f32[32,8,66]{2,0,1:T(8,128)} %pad_maximum_fusion.4), calls=%async_computation.3 | async-start | bytes 262144 | tf_op jit(solution)/shard_map/all_to_all | solution.py:12
  141.0 7.5 %all-to-all-done.3 = f32[32,8,66]{2,0,1:T(8,128)S(1)} async-done(((f32[32,8,66]{2,0,1:T(8,128)}), f32[32,8,66]{2,0,1:T(8,128)S(1)}, u32[]{:S(2)}, u32[]{:S(2)}) %all-to-all-start.3) | async-done | bytes 67616 | tf_op jit(solution)/shard_map/all_to_all | solution.py:12
  148.5 0.1 slice_reduce_fusion
  148.6 0.2 slice_reduce_fusion.2
  148.8 0.1 multiply_add_fusion
  148.9 0.2 copy.82
  149.1 1.0 gather_fusion.2
  150.1 0.1 copy.83
  150.3 0.8 reshape.159
  151.0 3.4 %all-to-all-start.4 = ((f32[8,1,2048]{2,1,0:T(1,128)}), f32[8,1,2048]{2,1,0:T(1,128)S(1)}, u32[]{:S(2)}, u32[]{:S(2)}) async-start(f32[8,1,2048]{2,1,0:T(1,128)} %reshape.159), calls=%async_computation.4 | async-start | bytes 131072 | tf_op jit(solution)/shard_map/all_to_all | solution.py:12
  154.4 6.9 %all-to-all-done.4 = f32[8,1,2048]{2,1,0:T(1,128)S(1)} async-done(((f32[8,1,2048]{2,1,0:T(1,128)}), f32[8,1,2048]{2,1,0:T(1,128)S(1)}, u32[]{:S(2)}, u32[]{:S(2)}) %all-to-all-start.4) | async-done | bytes 65568 | tf_op jit(solution)/shard_map/all_to_all | solution.py:12
  161.3 0.8 reduce.10
  162.2 0.1 reshape.160
  162.3 0.1 reshape.111
  162.5 8.6 %all_gather.6.xs_ref = f32[128,1536]{1,0:T(8,128)S(1)} all-gather(f32[32,1536]{1,0:T(8,128)S(1)} %pad_maximum_fusion.2), channel_id=1, replica_groups=mesh['vx'=2,'vy'=4,'col'=4] {'col'}, dimensions={0}, use_global_device_ids=true | all-gather | bytes 983040 | tf_op jit(solution)/shard_map/all_gather | solution.py:94
  171.1 7.4 %shard_map.70 = f32[1,4096]{1,0:T(1,128)S(1)} custom-call(f32[128,1536]{1,0:T(8,128)S(1)} %all_gather.6.xs_ref, s32[1,4096]{1,0:T(1,128)S(1)} %get-tuple-element.25.head_ref, s32[1,4096]{1,0:T(1,128)S(1)} %get-tuple-element.24.tail_ref, f32[1,4096]{1,0:T(1,128)S(1)} %bitcast.32), custom_call_target="tpu_custom_call" | custom-call | tf_op jit(solution)/shard_map/pallas_call | solution.py:75
  178.5 5.2 %all-gather = f32[1,16384]{1,0:T(1,128)S(1)} all-gather(f32[1,4096]{1,0:T(1,128)S(1)} %shard_map.70), channel_id=2, replica_groups=mesh['vx'=2,'vy'=4,'col'=4] {'col'}, dimensions={1}, use_global_device_ids=true | all-gather | bytes 81920 | tf_op jit(solution)/shard_map/all_gather | solution.py:138
  183.7 0.6 copy.89
  (36 shorter events, 0.9 us)
Async XLA Ops:
  3.7 8.0 %copy-start.3 = (s32[2,16384]{1,0:T(2,128)S(1)}, s32[2,16384]{1,0:T(2,128)}, u32[]{:S(2)}) copy-start(s32[2,16384]{1,0:T(2,128)} %param.7) | copy-start | bytes 393220
  4.5 14.2 %all-to-all-start = ((f32[8,1,2048]{2,1,0:T(1,128)}), f32[8,1,2048]{2,1,0:T(1,128)S(1)}, u32[]{:S(2)}, u32[]{:S(2)}) async-start(f32[8,1,2048]{2,1,0:T(1,128)} %reshape.155), calls=%async_computation | async-start | bytes 131072 | tf_op jit(solution)/shard_map/all_to_all | solution.py:12
  11.7 0.7 copy-start.5
  20.3 0.9 copy-start.1
  21.2 0.8 copy-start
  63.9 0.7 copy-start.4
  65.9 10.8 %all-to-all-start.1 = ((f32[32,8,66]{2,0,1:T(8,128)}), f32[32,8,66]{2,0,1:T(8,128)S(1)}, u32[]{:S(2)}, u32[]{:S(2)}) async-start(f32[32,8,66]{2,0,1:T(8,128)} %pad_maximum_fusion.3), calls=%async_computation.1 | async-start | bytes 262144 | tf_op jit(solution)/shard_map/all_to_all | solution.py:12
  83.4 10.3 %all-to-all-start.2 = ((f32[8,1,2048]{2,1,0:T(1,128)}), f32[8,1,2048]{2,1,0:T(1,128)S(1)}, u32[]{:S(2)}, u32[]{:S(2)}) async-start(f32[8,1,2048]{2,1,0:T(1,128)} %reshape.157), calls=%async_computation.2 | async-start | bytes 131072 | tf_op jit(solution)/shard_map/all_to_all | solution.py:12
  137.6 10.8 %all-to-all-start.3 = ((f32[32,8,66]{2,0,1:T(8,128)}), f32[32,8,66]{2,0,1:T(8,128)S(1)}, u32[]{:S(2)}, u32[]{:S(2)}) async-start(f32[32,8,66]{2,0,1:T(8,128)} %pad_maximum_fusion.4), calls=%async_computation.3 | async-start | bytes 262144 | tf_op jit(solution)/shard_map/all_to_all | solution.py:12
  148.9 13.6 %copy-start.2 = (f32[32,1024]{1,0:T(8,128)}, f32[32,1024]{1,0:T(8,128)S(1)}, u32[]{:S(2)}) copy-start(f32[32,1024]{1,0:T(8,128)S(1)} %multiply_add_fusion) | copy-start | bytes 393220
  151.0 10.3 %all-to-all-start.4 = ((f32[8,1,2048]{2,1,0:T(1,128)}), f32[8,1,2048]{2,1,0:T(1,128)S(1)}, u32[]{:S(2)}, u32[]{:S(2)}) async-start(f32[8,1,2048]{2,1,0:T(1,128)} %reshape.159), calls=%async_computation.4 | async-start | bytes 131072 | tf_op jit(solution)/shard_map/all_to_all | solution.py:12

commit v5 on v4

--- a/solution.py
+++ b/solution.py
@@ -21,7 +21,26 @@
 
 
 def edge_tile(rows):
-    return 1024 if rows <= 2048 else 256
+    return 2048 if rows <= 2048 else 256
+
+
+def incidence(head, tail, rows):
+    tile = head.shape[1]
+    if rows % 128:
+        index = lax.broadcasted_iota(jnp.int32, (rows, tile), 0)
+        ends = (index == head).astype(jnp.float32) - (index == tail).astype(jnp.float32)
+        return ends.astype(jnp.bfloat16)
+    lane = lax.broadcasted_iota(jnp.int32, (128, tile), 0)
+    low_head = (lane == (head & 127)).astype(jnp.bfloat16)
+    low_tail = (lane == (tail & 127)).astype(jnp.bfloat16)
+    high_head = head >> 7
+    high_tail = tail >> 7
+    blocks = []
+    for block in range(rows // 128):
+        on_head = (high_head == block).astype(jnp.bfloat16)
+        on_tail = (high_tail == block).astype(jnp.bfloat16)
+        blocks.append(low_head * on_head - low_tail * on_tail)
+    return jnp.concatenate(blocks, axis=0)
 
 
 def flow_kernel(scatter):
@@ -30,9 +49,7 @@
         step = pl.program_id(0)
         width, rows = xs_ref.shape
         tile = head_ref.shape[1]
-        index = lax.broadcasted_iota(jnp.int32, (rows, tile), 0)
-        ends = (index == head_ref[...]).astype(jnp.float32) - (index == tail_ref[...]).astype(jnp.float32)
-        ends = ends.astype(jnp.bfloat16)
+        ends = incidence(head_ref[...], tail_ref[...], rows)
         gap = jnp.dot(split3(xs_ref[...]), ends, preferred_element_type=jnp.float32)
         gap = gap[:width] + gap[width:2 * width] + gap[2 * width:]
         if not scatter:

time: 185 us -> 154 us (0.83)
  Pallas kernels: 91 us -> 60 us
    pallas_call x3, Pallas kernels: 91 us -> 60 us  [edge_pass(): pl.pallas_call(flow_kernel(scatter), grid=(edges // tile,), in_specs=[ful...]
where the time goes in v5:
time: 154 us; the launch traced here: 153 us
  Pallas kernels  60 us (39%)
  waiting for transfers between devices  34.4 us (22%)
  starting transfers between devices  20.9 us (14%)
  local copies, waits for them, and re-layouts  14.1 us (9%)
  blocking collectives  13.9 us (9%)
  other arithmetic  9.13 us (6%)
    pallas_call x3, Pallas kernels, edge_pass(): pl.pallas_call(flow_kernel(scatter), grid=(edges // tile,), in_specs=[ful...  60 us
    all_to_all x5, waiting for transfers between devices, trade(): lax.all_to_all(blocks, ('vx', 'vy'), split_axis=1, concat_axis=1, tiled=T...  34.4 us
    all_to_all x5, starting transfers between devices, trade(): lax.all_to_all(blocks, ('vx', 'vy'), split_axis=1, concat_axis=1, tiled=T...  20.9 us
    all_gather x1, blocking collectives, gathered(): return lax.all_gather(extend(field, halo_rows), 'col', axis=0, tiled=True)  8.63 us
    unnamed x23, local copies, waits for them, and re-layouts  7.18 us
    all_gather x1, blocking collectives, body(): resistance = lax.all_gather(total, 'col', axis=0, tiled=True)  5.25 us
    scatter-add x1, other arithmetic, operate(): local = summed[:, :count].at[:, halo_rows.reshape(-1)].add(returned)  3.51 us
    gather x6, local copies, waits for them, and re-layouts, extend(): mirrored = trade(field[:, halo_rows])  3.47 us
  transfers between devices with their start and end apart: 5, of which 5 were waited for; matrix products, arithmetic and copies ran while one was open for 0% of the time, Pallas kernels for 0%

profile of v5, /device:TPU:0, one launch (start us, length us, event | category | flops | bytes accessed | tf_op | source)
XLA Modules:
  0.0 153.4 jit_solution(5429643448297715737)
XLA Ops:
  0.6 0.7 compare_select_fusion.1
  1.4 1.1 copy.64
  2.5 1.0 gather_fusion
  3.6 0.1 copy.65
  3.7 0.8 reshape.155
  4.5 7.3 %all-to-all-start = ((f32[8,1,2048]{2,1,0:T(1,128)}), f32[8,1,2048]{2,1,0:T(1,128)S(1)}, u32[]{:S(2)}, u32[]{:S(2)}) async-start(f32[8,1,2048]{2,1,0:T(1,128)} %reshape.155), calls=%async_computation | async-start | bytes 131072 | tf_op jit(solution)/shard_map/all_to_all | solution.py:12
  11.7 0.1 fusion
  11.9 0.6 copy-done.5
  12.5 6.2 %all-to-all-done = f32[8,1,2048]{2,1,0:T(1,128)S(1)} async-done(((f32[8,1,2048]{2,1,0:T(1,128)}), f32[8,1,2048]{2,1,0:T(1,128)S(1)}, u32[]{:S(2)}, u32[]{:S(2)}) %all-to-all-start) | async-done | bytes 65568 | tf_op jit(solution)/shard_map/all_to_all | solution.py:12
  18.7 0.6 broadcast.39
  19.3 0.8 reduce.8
  20.2 0.1 reshape.156
  20.3 0.1 reshape.105
  20.4 0.8 copy-done.1
  21.3 0.8 copy-done
  22.1 27.3 %shard_map.68 = (f32[32,1536]{1,0:T(8,128)S(1)}, f32[32,1]{1,0:T(8,128)S(1)}) custom-call(f32[32,1536]{1,0:T(8,128)S(1)} %pad_maximum_fusion.xs_ref, s32[1,16384]{1,0:T(1,128)S(1)} %get-tuple-element.23.head_ref, s32[1,16384]{1,0:T(1,128)S(1)} %get-tuple-element.22.tail_ref, f32[1,16384]{1,0:T(1,128)S(1)} %bitcast.30), custom_call_target="tpu_custom_call" | custom-call | tf_op jit(solution)/shard_map/pallas_call | solution.py:92
  49.4 0.7 copy-done.4
  50.1 0.1 multiply_reduce_fusion.3
  50.2 0.1 copy.67
  50.3 0.1 copy.68
  50.6 0.8 pad_maximum_fusion.3
  51.4 3.4 %all-to-all-start.1 = ((f32[32,8,66]{2,0,1:T(8,128)}), f32[32,8,66]{2,0,1:T(8,128)S(1)}, u32[]{:S(2)}, u32[]{:S(2)}) async-start(f32[32,8,66]{2,0,1:T(8,128)} %pad_maximum_fusion.3), calls=%async_computation.1 | async-start | bytes 262144 | tf_op jit(solution)/shard_map/all_to_all | solution.py:12
  54.8 0.2 copy.72
  55.0 7.2 %all-to-all-done.1 = f32[32,8,66]{2,0,1:T(8,128)S(1)} async-done(((f32[32,8,66]{2,0,1:T(8,128)}), f32[32,8,66]{2,0,1:T(8,128)S(1)}, u32[]{:S(2)}, u32[]{:S(2)}) %all-to-all-start.1) | async-done | bytes 67616 | tf_op jit(solution)/shard_map/all_to_all | solution.py:12
  62.2 0.1 slice_reduce_fusion.1
  62.3 0.2 slice_reduce_fusion.4
  62.5 0.1 copy.71
  62.6 0.1 reshape.137
  62.7 0.1 copy.73
  62.8 3.5 %scatter_fusion = f32[32,1024]{0,1:T(8,128)S(1)} fusion(f32[32,1024]{0,1:T(8,128)S(1)} %copy.72, s32[512]{0:T(512)S(1)} %bitcast.44, f32[512,32]{1,0:T(8,128)S(1)} %copy.73), kind=kCustom, calls=%fused_computation.3 | custom fusion | flops 16384 | bytes 198656 | tf_op jit(solution)/shard_map/scatter-add | solution.py:127
  66.3 0.2 copy.74
  66.5 0.2 multiply_reduce_fusion.2
  66.7 0.2 copy.75
  66.9 1.0 gather_fusion.1
  68.0 0.1 copy.76
  68.1 0.8 reshape.157
  68.9 3.4 %all-to-all-start.2 = ((f32[8,1,2048]{2,1,0:T(1,128)}), f32[8,1,2048]{2,1,0:T(1,128)S(1)}, u32[]{:S(2)}, u32[]{:S(2)}) async-start(f32[8,1,2048]{2,1,0:T(1,128)} %reshape.157), calls=%async_computation.2 | async-start | bytes 131072 | tf_op jit(solution)/shard_map/all_to_all | solution.py:12
  72.2 0.1 copy.78
  72.3 0.1 copy.79
  72.4 6.8 %all-to-all-done.2 = f32[8,1,2048]{2,1,0:T(1,128)S(1)} async-done(((f32[8,1,2048]{2,1,0:T(1,128)}), f32[8,1,2048]{2,1,0:T(1,128)S(1)}, u32[]{:S(2)}, u32[]{:S(2)}) %all-to-all-start.2) | async-done | bytes 65568 | tf_op jit(solution)/shard_map/all_to_all | solution.py:12
  79.1 0.8 reduce.9
  80.0 0.1 reshape.158
  80.2 0.1 reshape.109
  80.3 27.3 %shard_map.69 = (f32[32,1536]{1,0:T(8,128)S(1)}, f32[32,1]{1,0:T(8,128)S(1)}) custom-call(f32[32,1536]{1,0:T(8,128)S(1)} %pad_maximum_fusion.1.xs_ref, s32[1,16384]{1,0:T(1,128)S(1)} %get-tuple-element.23.head_ref, s32[1,16384]{1,0:T(1,128)S(1)} %get-tuple-element.22.tail_ref, f32[1,16384]{1,0:T(1,128)S(1)} %bitcast.31), custom_call_target="tpu_custom_call" | custom-call | tf_op jit(solution)/shard_map/pallas_call | solution.py:92
  107.6 0.1 reshape.110
  107.8 0.8 pad_maximum_fusion.4
  108.6 3.4 %all-to-all-start.3 = ((f32[32,8,66]{2,0,1:T(8,128)}), f32[32,8,66]{2,0,1:T(8,128)S(1)}, u32[]{:S(2)}, u32[]{:S(2)}) async-start(f32[32,8,66]{2,0,1:T(8,128)} %pad_maximum_fusion.4), calls=%async_computation.3 | async-start | bytes 262144 | tf_op jit(solution)/shard_map/all_to_all | solution.py:12
  112.0 7.5 %all-to-all-done.3 = f32[32,8,66]{2,0,1:T(8,128)S(1)} async-done(((f32[32,8,66]{2,0,1:T(8,128)}), f32[32,8,66]{2,0,1:T(8,128)S(1)}, u32[]{:S(2)}, u32[]{:S(2)}) %all-to-all-start.3) | async-done | bytes 67616 | tf_op jit(solution)/shard_map/all_to_all | solution.py:12
  119.4 0.1 slice_reduce_fusion
  119.5 0.2 slice_reduce_fusion.2
  119.7 0.1 multiply_add_fusion
  119.8 0.2 copy.82
  120.0 1.0 gather_fusion.2
  121.1 0.1 copy.83
  121.2 0.8 reshape.159
  122.0 3.5 %all-to-all-start.4 = ((f32[8,1,2048]{2,1,0:T(1,128)}), f32[8,1,2048]{2,1,0:T(1,128)S(1)}, u32[]{:S(2)}, u32[]{:S(2)}) async-start(f32[8,1,2048]{2,1,0:T(1,128)} %reshape.159), calls=%async_computation.4 | async-start | bytes 131072 | tf_op jit(solution)/shard_map/all_to_all | solution.py:12
  125.6 6.7 %all-to-all-done.4 = f32[8,1,2048]{2,1,0:T(1,128)S(1)} async-done(((f32[8,1,2048]{2,1,0:T(1,128)}), f32[8,1,2048]{2,1,0:T(1,128)S(1)}, u32[]{:S(2)}, u32[]{:S(2)}) %all-to-all-start.4) | async-done | bytes 65568 | tf_op jit(solution)/shard_map/all_to_all | solution.py:12
  132.3 0.8 reduce.10
  133.1 0.1 reshape.160
  133.3 0.1 reshape.111
  133.4 8.6 %all_gather.6.xs_ref = f32[128,1536]{1,0:T(8,128)S(1)} all-gather(f32[32,1536]{1,0:T(8,128)S(1)} %pad_maximum_fusion.2), channel_id=1, replica_groups=mesh['vx'=2,'vy'=4,'col'=4] {'col'}, dimensions={0}, use_global_device_ids=true | all-gather | bytes 983040 | tf_op jit(solution)/shard_map/all_gather | solution.py:111
  142.0 5.5 %shard_map.70 = f32[1,4096]{1,0:T(1,128)S(1)} custom-call(f32[128,1536]{1,0:T(8,128)S(1)} %all_gather.6.xs_ref, s32[1,4096]{1,0:T(1,128)S(1)} %get-tuple-element.25.head_ref, s32[1,4096]{1,0:T(1,128)S(1)} %get-tuple-element.24.tail_ref, f32[1,4096]{1,0:T(1,128)S(1)} %bitcast.32), custom_call_target="tpu_custom_call" | custom-call | tf_op jit(solution)/shard_map/pallas_call | solution.py:92
  147.5 5.2 %all-gather = f32[1,16384]{1,0:T(1,128)S(1)} all-gather(f32[1,4096]{1,0:T(1,128)S(1)} %shard_map.70), channel_id=2, replica_groups=mesh['vx'=2,'vy'=4,'col'=4] {'col'}, dimensions={1}, use_global_device_ids=true | all-gather | bytes 81920 | tf_op jit(solution)/shard_map/all_gather | solution.py:155
  152.8 0.6 copy.89
  (36 shorter events, 0.9 us)
Async XLA Ops:
  3.7 8.0 %copy-start.3 = (s32[2,16384]{1,0:T(2,128)S(1)}, s32[2,16384]{1,0:T(2,128)}, u32[]{:S(2)}) copy-start(s32[2,16384]{1,0:T(2,128)} %param.7) | copy-start | bytes 393220
  4.5 14.2 %all-to-all-start = ((f32[8,1,2048]{2,1,0:T(1,128)}), f32[8,1,2048]{2,1,0:T(1,128)S(1)}, u32[]{:S(2)}, u32[]{:S(2)}) async-start(f32[8,1,2048]{2,1,0:T(1,128)} %reshape.155), calls=%async_computation | async-start | bytes 131072 | tf_op jit(solution)/shard_map/all_to_all | solution.py:12
  11.7 0.7 copy-start.5
  20.3 0.9 copy-start.1
  21.2 0.8 copy-start
  49.4 0.7 copy-start.4
  51.4 10.8 %all-to-all-start.1 = ((f32[32,8,66]{2,0,1:T(8,128)}), f32[32,8,66]{2,0,1:T(8,128)S(1)}, u32[]{:S(2)}, u32[]{:S(2)}) async-start(f32[32,8,66]{2,0,1:T(8,128)} %pad_maximum_fusion.3), calls=%async_computation.1 | async-start | bytes 262144 | tf_op jit(solution)/shard_map/all_to_all | solution.py:12
  68.9 10.3 %all-to-all-start.2 = ((f32[8,1,2048]{2,1,0:T(1,128)}), f32[8,1,2048]{2,1,0:T(1,128)S(1)}, u32[]{:S(2)}, u32[]{:S(2)}) async-start(f32[8,1,2048]{2,1,0:T(1,128)} %reshape.157), calls=%async_computation.2 | async-start | bytes 131072 | tf_op jit(solution)/shard_map/all_to_all | solution.py:12
  108.6 10.8 %all-to-all-start.3 = ((f32[32,8,66]{2,0,1:T(8,128)}), f32[32,8,66]{2,0,1:T(8,128)S(1)}, u32[]{:S(2)}, u32[]{:S(2)}) async-start(f32[32,8,66]{2,0,1:T(8,128)} %pad_maximum_fusion.4), calls=%async_computation.3 | async-start | bytes 262144 | tf_op jit(solution)/shard_map/all_to_all | solution.py:12
  119.8 13.6 %copy-start.2 = (f32[32,1024]{1,0:T(8,128)}, f32[32,1024]{1,0:T(8,128)S(1)}, u32[]{:S(2)}) copy-start(f32[32,1024]{1,0:T(8,128)S(1)} %multiply_add_fusion) | copy-start | bytes 393220
  122.0 10.3 %all-to-all-start.4 = ((f32[8,1,2048]{2,1,0:T(1,128)}), f32[8,1,2048]{2,1,0:T(1,128)S(1)}, u32[]{:S(2)}, u32[]{:S(2)}) async-start(f32[8,1,2048]{2,1,0:T(1,128)} %reshape.159), calls=%async_computation.4 | async-start | bytes 131072 | tf_op jit(solution)/shard_map/all_to_all | solution.py:12

commit v6 on v5

--- a/solution.py
+++ b/solution.py
@@ -107,15 +107,12 @@
     return jnp.concatenate([field, mirrored.reshape(field.shape[0], -1)], axis=1)
 
 
-def gathered(field, halo_rows):
-    return lax.all_gather(extend(field, halo_rows), "col", axis=0, tiled=True)
-
-
 def operate(field, shift, head_rows, tail_slots, weights, halo_rows):
     count = field.shape[1]
     width = field.shape[0]
     peers, cap = halo_rows.shape
-    summed, energy = edge_pass(extend(field, halo_rows), head_rows, tail_slots, weights, True)
+    extended = extend(field, halo_rows)
+    summed, energy = edge_pass(extended, head_rows, tail_slots, weights, True)
     squares = field * field
     own = jnp.stack([jnp.sum(squares, axis=1), jnp.sum(shift * squares, axis=1) + energy[:, 0]], axis=1)
     sent = jnp.concatenate(
@@ -125,7 +122,7 @@
     returned = got[:, :, :cap].reshape(width, -1)
     norm, product = jnp.sum(got[:, :, cap:], axis=1).T
     local = summed[:, :count].at[:, halo_rows.reshape(-1)].add(returned)
-    return shift * field + local, norm, product
+    return shift * field + local, norm, product, extended[:, count:]
 
 
 def body(right_side, shift, edge_ends, weights, halo_rows):
@@ -137,21 +134,26 @@
     quarter = [lax.dynamic_slice_in_dim(item, start, share, axis=1) for item in (head_rows, tail_slots, weights)]
     solution = jnp.zeros_like(right_side)
     residual = right_side
-    image, norm_now, product = operate(residual, shift, head_rows, tail_slots, weights, halo_rows)
+    image, norm_now, product, mirrored = operate(residual, shift, head_rows, tail_slots, weights, halo_rows)
     alpha = norm_now / product
     direction = residual
     along = image
+    far_solution = jnp.zeros_like(mirrored)
+    far_direction = mirrored
     for step in range(ITERS):
         solution = solution + alpha[:, None] * direction
+        far_solution = far_solution + alpha[:, None] * far_direction
         residual = residual - alpha[:, None] * along
         if step + 1 < ITERS:
-            image, norm_next, product = operate(residual, shift, head_rows, tail_slots, weights, halo_rows)
+            image, norm_next, product, mirrored = operate(residual, shift, head_rows, tail_slots, weights, halo_rows)
             ratio = norm_next / norm_now
             alpha = norm_next / (product - ratio * norm_next / alpha)
             direction = residual + ratio[:, None] * direction
+            far_direction = mirrored + ratio[:, None] * far_direction
             along = image + ratio[:, None] * along
             norm_now = norm_next
-    total = edge_pass(gathered(solution, halo_rows), *quarter, False)[0]
+    extended = jnp.concatenate([solution, far_solution], axis=1)
+    total = edge_pass(lax.all_gather(extended, "col", axis=0, tiled=True), *quarter, False)[0]
     resistance = lax.all_gather(total, "col", axis=0, tiled=True)
     return (solution, resistance)
 

time: 154 us -> 141 us (0.916)
  waiting for transfers between devices: 34.4 us -> 27.6 us
  starting transfers between devices: 20.9 us -> 17.3 us
  local copies, waits for them, and re-layouts: 14.1 us -> 12.3 us
    all_to_all x5 -> x4, waiting for transfers between devices: 34.4 us -> 27.6 us  [trade(): lax.all_to_all(blocks, ('vx', 'vy'), split_axis=1, concat_axis=1, tiled=T...]
    all_to_all x5 -> x4, starting transfers between devices: 20.9 us -> 17.3 us  [trade(): lax.all_to_all(blocks, ('vx', 'vy'), split_axis=1, concat_axis=1, tiled=T...]
    gather x6 -> x4, local copies, waits for them, and re-layouts: 3.47 us -> 2.31 us  [extend(): mirrored = trade(field[:, halo_rows])]
    unnamed x23 -> x20, local copies, waits for them, and re-layouts: 7.18 us -> 6.94 us
  transfers between devices with their start and end apart: 5 -> 4, of which waited for: 5 -> 4; matrix products, arithmetic and copies ran while one was open for 0% -> 0% of each run, Pallas kernels for 0% -> 0%
where the time goes in v6:
time: 141 us
  Pallas kernels  60 us (43%)
  waiting for transfers between devices  27.6 us (20%)
  starting transfers between devices  17.3 us (12%)
  blocking collectives  14 us (10%)
  local copies, waits for them, and re-layouts  12.3 us (9%)
  other arithmetic  8.37 us (6%)
    pallas_call x3, Pallas kernels, edge_pass(): pl.pallas_call(flow_kernel(scatter), grid=(edges // tile,), in_specs=[ful...  60 us
    all_to_all x4, waiting for transfers between devices, trade(): lax.all_to_all(blocks, ('vx', 'vy'), split_axis=1, concat_axis=1, tiled=T...  27.6 us
    all_to_all x4, starting transfers between devices, trade(): lax.all_to_all(blocks, ('vx', 'vy'), split_axis=1, concat_axis=1, tiled=T...  17.3 us
    all_gather x1, blocking collectives, body(): lax.all_gather(extended, 'col', axis=0, tiled=True)  8.79 us
    unnamed x20, local copies, waits for them, and re-layouts  6.94 us
    all_gather x1, blocking collectives, body(): resistance = lax.all_gather(total, 'col', axis=0, tiled=True)  5.25 us
    scatter-add x1, other arithmetic, operate(): local = summed[:, :count].at[:, halo_rows.reshape(-1)].add(returned)  3.51 us
  transfers between devices with their start and end apart: 4, of which 4 were waited for; matrix products, arithmetic and copies ran while one was open for 0% of the time, Pallas kernels for 0%

profile of v6, /device:TPU:0, one launch (start us, length us, event | category | flops | bytes accessed | tf_op | source)
XLA Modules:
  0.0 140.7 jit_solution(5730382921973589688)
XLA Ops:
  0.6 0.7 compare_select_fusion.1
  1.3 0.1 reshape.110
  1.4 1.1 copy.56
  2.5 1.0 gather_fusion
  3.6 0.1 copy.57
  3.7 0.8 reshape.141
  4.5 7.3 %all-to-all-start = ((f32[8,1,2048]{2,1,0:T(1,128)}), f32[8,1,2048]{2,1,0:T(1,128)S(1)}, u32[]{:S(2)}, u32[]{:S(2)}) async-start(f32[8,1,2048]{2,1,0:T(1,128)} %reshape.141), calls=%async_computation | async-start | bytes 131072 | tf_op jit(solution)/shard_map/all_to_all | solution.py:12
  11.7 0.1 fusion
  11.9 0.6 copy-done.5
  12.4 0.1 reshape.104
  12.5 6.2 %all-to-all-done = f32[8,1,2048]{2,1,0:T(1,128)S(1)} async-done(((f32[8,1,2048]{2,1,0:T(1,128)}), f32[8,1,2048]{2,1,0:T(1,128)S(1)}, u32[]{:S(2)}, u32[]{:S(2)}) %all-to-all-start) | async-done | bytes 65568 | tf_op jit(solution)/shard_map/all_to_all | solution.py:12
  18.7 0.6 broadcast.37
  19.3 0.8 reduce.8
  20.2 0.1 reshape.142
  20.2 0.1 copy.58
  20.3 0.1 reshape.102
  20.4 0.8 copy-done.1
  21.3 0.8 copy-done
  22.1 27.3 %shard_map.68 = (f32[32,1536]{1,0:T(8,128)S(1)}, f32[32,1]{1,0:T(8,128)S(1)}) custom-call(f32[32,1536]{1,0:T(8,128)S(1)} %pad_maximum_fusion.xs_ref, s32[1,16384]{1,0:T(1,128)S(1)} %get-tuple-element.23.head_ref, s32[1,16384]{1,0:T(1,128)S(1)} %get-tuple-element.22.tail_ref, f32[1,16384]{1,0:T(1,128)S(1)} %bitcast.24), custom_call_target="tpu_custom_call" | custom-call | tf_op jit(solution)/shard_map/pallas_call | solution.py:92
  49.4 0.7 copy-done.4
  50.1 0.1 multiply_reduce_fusion.3
  50.2 0.1 copy.59
  50.3 0.1 copy.60
  50.4 0.1 reshape.103
  50.5 0.1 pad_maximum_fusion.5
  50.6 0.8 pad_maximum_fusion.3
  51.4 3.4 %all-to-all-start.1 = ((f32[32,8,66]{2,0,1:T(8,128)}), f32[32,8,66]{2,0,1:T(8,128)S(1)}, u32[]{:S(2)}, u32[]{:S(2)}) async-start(f32[32,8,66]{2,0,1:T(8,128)} %pad_maximum_fusion.3), calls=%async_computation.1 | async-start | bytes 262144 | tf_op jit(solution)/shard_map/all_to_all | solution.py:12
  54.8 0.2 copy.64
  55.0 7.2 %all-to-all-done.1 = f32[32,8,66]{2,0,1:T(8,128)S(1)} async-done(((f32[32,8,66]{2,0,1:T(8,128)}), f32[32,8,66]{2,0,1:T(8,128)S(1)}, u32[]{:S(2)}, u32[]{:S(2)}) %all-to-all-start.1) | async-done | bytes 67616 | tf_op jit(solution)/shard_map/all_to_all | solution.py:12
  62.2 0.1 slice_reduce_fusion.1
  62.3 0.2 slice_reduce_fusion.4
  62.5 0.1 copy.63
  62.6 0.1 reshape.125
  62.7 0.1 copy.65
  62.8 3.5 %scatter_fusion = f32[32,1024]{0,1:T(8,128)S(1)} fusion(f32[32,1024]{0,1:T(8,128)S(1)} %copy.64, s32[512]{0:T(512)S(1)} %bitcast.36, f32[512,32]{1,0:T(8,128)S(1)} %copy.65), kind=kCustom, calls=%fused_computation.2 | custom fusion | flops 16384 | bytes 198656 | tf_op jit(solution)/shard_map/scatter-add | solution.py:124
  66.3 0.2 copy.66
  66.5 0.2 multiply_reduce_fusion.2
  66.7 0.2 copy.67
  66.9 1.0 gather_fusion.1
  68.0 0.1 copy.68
  68.1 0.8 reshape.143
  68.9 3.4 %all-to-all-start.2 = ((f32[8,1,2048]{2,1,0:T(1,128)}), f32[8,1,2048]{2,1,0:T(1,128)S(1)}, u32[]{:S(2)}, u32[]{:S(2)}) async-start(f32[8,1,2048]{2,1,0:T(1,128)} %reshape.143), calls=%async_computation.2 | async-start | bytes 131072 | tf_op jit(solution)/shard_map/all_to_all | solution.py:12
  72.2 0.1 copy.70
  72.3 0.1 copy.71
  72.4 6.7 %all-to-all-done.2 = f32[8,1,2048]{2,1,0:T(1,128)S(1)} async-done(((f32[8,1,2048]{2,1,0:T(1,128)}), f32[8,1,2048]{2,1,0:T(1,128)S(1)}, u32[]{:S(2)}, u32[]{:S(2)}) %all-to-all-start.2) | async-done | bytes 65568 | tf_op jit(solution)/shard_map/all_to_all | solution.py:12
  79.1 0.8 reduce.9
  80.0 0.1 reshape.144
  80.1 0.1 copy.69
  80.2 0.1 reshape.106
  80.3 27.3 %shard_map.69 = (f32[32,1536]{1,0:T(8,128)S(1)}, f32[32,1]{1,0:T(8,128)S(1)}) custom-call(f32[32,1536]{1,0:T(8,128)S(1)} %pad_maximum_fusion.1.xs_ref, s32[1,16384]{1,0:T(1,128)S(1)} %get-tuple-element.23.head_ref, s32[1,16384]{1,0:T(1,128)S(1)} %get-tuple-element.22.tail_ref, f32[1,16384]{1,0:T(1,128)S(1)} %bitcast.25), custom_call_target="tpu_custom_call" | custom-call | tf_op jit(solution)/shard_map/pallas_call | solution.py:92
  107.6 0.1 reshape.107
  107.7 0.1 pad_maximum_fusion.6
  107.8 0.8 pad_maximum_fusion.4
  108.6 3.4 %all-to-all-start.3 = ((f32[32,8,66]{2,0,1:T(8,128)}), f32[32,8,66]{2,0,1:T(8,128)S(1)}, u32[]{:S(2)}, u32[]{:S(2)}) async-start(f32[32,8,66]{2,0,1:T(8,128)} %pad_maximum_fusion.4), calls=%async_computation.3 | async-start | bytes 262144 | tf_op jit(solution)/shard_map/all_to_all | solution.py:12
  112.0 7.4 %all-to-all-done.3 = f32[32,8,66]{2,0,1:T(8,128)S(1)} async-done(((f32[32,8,66]{2,0,1:T(8,128)}), f32[32,8,66]{2,0,1:T(8,128)S(1)}, u32[]{:S(2)}, u32[]{:S(2)}) %all-to-all-start.3) | async-done | bytes 67616 | tf_op jit(solution)/shard_map/all_to_all | solution.py:12
  119.4 0.1 slice_reduce_fusion
  119.5 0.2 slice_reduce_fusion.2
  119.7 0.1 multiply_add_fusion.1
  119.8 0.1 multiply_add_fusion
  120.0 0.6 copy-done.2
  120.6 8.8 %all_gather.6.xs_ref = f32[128,1536]{1,0:T(8,128)S(1)} all-gather(f32[32,1536]{1,0:T(8,128)S(1)} %pad_maximum_fusion.2), channel_id=1, replica_groups=mesh['vx'=2,'vy'=4,'col'=4] {'col'}, dimensions={0}, use_global_device_ids=true | all-gather | bytes 983040 | tf_op jit(solution)/shard_map/all_gather | solution.py:156
  129.4 5.5 %shard_map.70 = f32[1,4096]{1,0:T(1,128)S(1)} custom-call(f32[128,1536]{1,0:T(8,128)S(1)} %all_gather.6.xs_ref, s32[1,4096]{1,0:T(1,128)S(1)} %get-tuple-element.25.head_ref, s32[1,4096]{1,0:T(1,128)S(1)} %get-tuple-element.24.tail_ref, f32[1,4096]{1,0:T(1,128)S(1)} %bitcast.26), custom_call_target="tpu_custom_call" | custom-call | tf_op jit(solution)/shard_map/pallas_call | solution.py:92
  134.8 5.2 %all-gather = f32[1,16384]{1,0:T(1,128)S(1)} all-gather(f32[1,4096]{1,0:T(1,128)S(1)} %shard_map.70), channel_id=2, replica_groups=mesh['vx'=2,'vy'=4,'col'=4] {'col'}, dimensions={1}, use_global_device_ids=true | all-gather | bytes 81920 | tf_op jit(solution)/shard_map/all_gather | solution.py:157
  140.1 0.6 copy.78
  (26 shorter events, 0.3 us)
Async XLA Ops:
  3.7 8.0 %copy-start.3 = (s32[2,16384]{1,0:T(2,128)S(1)}, s32[2,16384]{1,0:T(2,128)}, u32[]{:S(2)}) copy-start(s32[2,16384]{1,0:T(2,128)} %param.7) | copy-start | bytes 393220
  4.5 14.2 %all-to-all-start = ((f32[8,1,2048]{2,1,0:T(1,128)}), f32[8,1,2048]{2,1,0:T(1,128)S(1)}, u32[]{:S(2)}, u32[]{:S(2)}) async-start(f32[8,1,2048]{2,1,0:T(1,128)} %reshape.141), calls=%async_computation | async-start | bytes 131072 | tf_op jit(solution)/shard_map/all_to_all | solution.py:12
  11.7 0.7 copy-start.5
  20.3 0.9 copy-start.1
  21.2 0.8 copy-start
  49.4 0.7 copy-start.4
  51.4 10.8 %all-to-all-start.1 = ((f32[32,8,66]{2,0,1:T(8,128)}), f32[32,8,66]{2,0,1:T(8,128)S(1)}, u32[]{:S(2)}, u32[]{:S(2)}) async-start(f32[32,8,66]{2,0,1:T(8,128)} %pad_maximum_fusion.3), calls=%async_computation.1 | async-start | bytes 262144 | tf_op jit(solution)/shard_map/all_to_all | solution.py:12
  68.9 10.3 %all-to-all-start.2 = ((f32[8,1,2048]{2,1,0:T(1,128)}), f32[8,1,2048]{2,1,0:T(1,128)S(1)}, u32[]{:S(2)}, u32[]{:S(2)}) async-start(f32[8,1,2048]{2,1,0:T(1,128)} %reshape.143), calls=%async_computation.2 | async-start | bytes 131072 | tf_op jit(solution)/shard_map/all_to_all | solution.py:12
  108.6 10.8 %all-to-all-start.3 = ((f32[32,8,66]{2,0,1:T(8,128)}), f32[32,8,66]{2,0,1:T(8,128)S(1)}, u32[]{:S(2)}, u32[]{:S(2)}) async-start(f32[32,8,66]{2,0,1:T(8,128)} %pad_maximum_fusion.4), calls=%async_computation.3 | async-start | bytes 262144 | tf_op jit(solution)/shard_map/all_to_all | solution.py:12
  119.9 0.7 copy-start.2

commit v7 on v6

--- a/solution.py
+++ b/solution.py
@@ -24,33 +24,56 @@
     return 2048 if rows <= 2048 else 256
 
 
-def incidence(head, tail, rows):
+def incidence(head, tail, rows, local):
     tile = head.shape[1]
     if rows % 128:
-        index = lax.broadcasted_iota(jnp.int32, (rows, tile), 0)
-        ends = (index == head).astype(jnp.float32) - (index == tail).astype(jnp.float32)
-        return ends.astype(jnp.bfloat16)
+        def build(first, size):
+            index = lax.broadcasted_iota(jnp.int32, (size, tile), 0) + first
+            ends = (index == head).astype(jnp.float32) - (index == tail).astype(jnp.float32)
+            return ends.astype(jnp.bfloat16)
+
+        return build
     lane = lax.broadcasted_iota(jnp.int32, (128, tile), 0)
     low_head = (lane == (head & 127)).astype(jnp.bfloat16)
     low_tail = (lane == (tail & 127)).astype(jnp.bfloat16)
     high_head = head >> 7
     high_tail = tail >> 7
-    blocks = []
-    for block in range(rows // 128):
-        on_head = (high_head == block).astype(jnp.bfloat16)
-        on_tail = (high_tail == block).astype(jnp.bfloat16)
-        blocks.append(low_head * on_head - low_tail * on_tail)
-    return jnp.concatenate(blocks, axis=0)
-
-
-def flow_kernel(scatter):
+
+    def build(first, size):
+        blocks = []
+        for block in range(first // 128, (first + size) // 128):
+            off_tail = -(high_tail == block).astype(jnp.bfloat16)
+            if block * 128 < local:
+                on_head = (high_head == block).astype(jnp.bfloat16)
+                blocks.append(low_head * on_head + low_tail * off_tail)
+            else:
+                blocks.append(low_tail * off_tail)
+        return jnp.concatenate(blocks, axis=0) if len(blocks) > 1 else blocks[0]
+
+    return build
+
+
+def pieces(rows):
+    step = 256 if rows % 256 == 0 else (128 if rows % 128 == 0 else rows)
+    return [(first, step) for first in range(0, rows, step)]
+
+
+def flow_kernel(scatter, local):
     def kernel(xs_ref, head_ref, tail_ref, w_ref, *out_ref):
         out_ref, acc = (out_ref[:2], out_ref[2:]) if scatter else (out_ref[0], ())
         step = pl.program_id(0)
         width, rows = xs_ref.shape
-        tile = head_ref.shape[1]
-        ends = incidence(head_ref[...], tail_ref[...], rows)
-        gap = jnp.dot(split3(xs_ref[...]), ends, preferred_element_type=jnp.float32)
+        head = head_ref[...]
+        tail = tail_ref[...]
+        xs = split3(xs_ref[...])
+        parts = []
+        gap = None
+        build = incidence(head, tail, rows, local)
+        for first, size in pieces(rows):
+            ends = build(first, size)
+            parts.append(ends)
+            term = jnp.dot(xs[:, first:first + size], ends, preferred_element_type=jnp.float32)
+            gap = term if gap is None else gap + term
         gap = gap[:width] + gap[width:2 * width] + gap[2 * width:]
         if not scatter:
             out_ref[...] = jnp.sum(gap * gap, axis=0, keepdims=True)
@@ -63,9 +86,11 @@
         energy_ref[...] = jnp.where(step == 0, 0.0, energy_ref[...]) + energy
         flow = split3(weighted)
         dims = (((1,), (1,)), ((), ()))
-        total[...] = jnp.where(step == 0, 0.0, total[...]) + lax.dot_general(
-            flow, ends, dims, preferred_element_type=jnp.float32
-        )
+        for (first, size), ends in zip(pieces(rows), parts):
+            window = total[:, first:first + size]
+            total[:, first:first + size] = jnp.where(step == 0, 0.0, window) + lax.dot_general(
+                flow, ends, dims, preferred_element_type=jnp.float32
+            )
 
         @pl.when(step == pl.num_programs(0) - 1)
         def _():
@@ -75,7 +100,7 @@
     return kernel
 
 
-def edge_pass(extended, head_rows, tail_slots, weights, scatter):
+def edge_pass(extended, head_rows, tail_slots, weights, scatter, local):
     width, rows = extended.shape
     edges = head_rows.shape[1]
     tile = edge_tile(rows)
@@ -90,7 +115,7 @@
         out_spec = edge_spec
         scratch = []
     return pl.pallas_call(
-        flow_kernel(scatter),
+        flow_kernel(scatter, local),
         grid=(edges // tile,),
         in_specs=[full, edge_spec, edge_spec, edge_spec],
         out_specs=out_spec,
@@ -112,7 +137,7 @@
     width = field.shape[0]
     peers, cap = halo_rows.shape
     extended = extend(field, halo_rows)
-    summed, energy = edge_pass(extended, head_rows, tail_slots, weights, True)
+    summed, energy = edge_pass(extended, head_rows, tail_slots, weights, True, count)
     squares = field * field
     own = jnp.stack([jnp.sum(squares, axis=1), jnp.sum(shift * squares, axis=1) + energy[:, 0]], axis=1)
     sent = jnp.concatenate(
@@ -153,7 +178,7 @@
             along = image + ratio[:, None] * along
             norm_now = norm_next
     extended = jnp.concatenate([solution, far_solution], axis=1)
-    total = edge_pass(lax.all_gather(extended, "col", axis=0, tiled=True), *quarter, False)[0]
+    total = edge_pass(lax.all_gather(extended, "col", axis=0, tiled=True), *quarter, False, solution.shape[1])[0]
     resistance = lax.all_gather(total, "col", axis=0, tiled=True)
     return (solution, resistance)
 

time: 141 us -> 140 us (level)
  no operation moved by 1% of the time
where the time goes in v7:
time: 140 us
  Pallas kernels  58.8 us (42%)
  waiting for transfers between devices  27.6 us (20%)
  starting transfers between devices  17.3 us (12%)
  blocking collectives  14 us (10%)
  local copies, waits for them, and re-layouts  12.3 us (9%)
  other arithmetic  8.37 us (6%)
    pallas_call x3, Pallas kernels, edge_pass(): pl.pallas_call(flow_kernel(scatter, local), grid=(edges // tile,), in_spe...  58.8 us
    all_to_all x4, waiting for transfers between devices, trade(): lax.all_to_all(blocks, ('vx', 'vy'), split_axis=1, concat_axis=1, tiled=T...  27.6 us
    all_to_all x4, starting transfers between devices, trade(): lax.all_to_all(blocks, ('vx', 'vy'), split_axis=1, concat_axis=1, tiled=T...  17.3 us
    all_gather x1, blocking collectives, body(): lax.all_gather(extended, 'col', axis=0, tiled=True)  8.79 us
    unnamed x20, local copies, waits for them, and re-layouts  6.94 us
    all_gather x1, blocking collectives, body(): resistance = lax.all_gather(total, 'col', axis=0, tiled=True)  5.25 us
    scatter-add x1, other arithmetic, operate(): local = summed[:, :count].at[:, halo_rows.reshape(-1)].add(returned)  3.51 us
  transfers between devices with their start and end apart: 4, of which 4 were waited for; matrix products, arithmetic and copies ran while one was open for 0% of the time, Pallas kernels for 0%

profile of v7, /device:TPU:0, one launch (start us, length us, event | category | flops | bytes accessed | tf_op | source)
XLA Modules:
  0.0 139.5 jit_solution(11249921873087179644)
XLA Ops:
  0.6 0.7 compare_select_fusion.1
  1.3 0.1 reshape.110
  1.4 1.1 copy.56
  2.5 1.0 gather_fusion
  3.6 0.1 copy.57
  3.7 0.8 reshape.141
  4.5 7.3 %all-to-all-start = ((f32[8,1,2048]{2,1,0:T(1,128)}), f32[8,1,2048]{2,1,0:T(1,128)S(1)}, u32[]{:S(2)}, u32[]{:S(2)}) async-start(f32[8,1,2048]{2,1,0:T(1,128)} %reshape.141), calls=%async_computation | async-start | bytes 131072 | tf_op jit(solution)/shard_map/all_to_all | solution.py:12
  11.7 0.1 fusion
  11.8 0.6 copy-done.5
  12.4 0.1 reshape.104
  12.5 6.2 %all-to-all-done = f32[8,1,2048]{2,1,0:T(1,128)S(1)} async-done(((f32[8,1,2048]{2,1,0:T(1,128)}), f32[8,1,2048]{2,1,0:T(1,128)S(1)}, u32[]{:S(2)}, u32[]{:S(2)}) %all-to-all-start) | async-done | bytes 65568 | tf_op jit(solution)/shard_map/all_to_all | solution.py:12
  18.7 0.6 broadcast.37
  19.3 0.8 reduce.8
  20.2 0.1 reshape.142
  20.2 0.1 copy.58
  20.3 0.1 reshape.102
  20.4 0.8 copy-done.1
  21.2 0.8 copy-done
  22.1 26.6 %shard_map.68 = (f32[32,1536]{1,0:T(8,128)S(1)}, f32[32,1]{1,0:T(8,128)S(1)}) custom-call(f32[32,1536]{1,0:T(8,128)S(1)} %pad_maximum_fusion.xs_ref, s32[1,16384]{1,0:T(1,128)S(1)} %get-tuple-element.23.head_ref, s32[1,16384]{1,0:T(1,128)S(1)} %get-tuple-element.22.tail_ref, f32[1,16384]{1,0:T(1,128)S(1)} %bitcast.24), custom_call_target="tpu_custom_call" | custom-call | tf_op jit(solution)/shard_map/pallas_call | solution.py:117
  48.7 0.7 copy-done.4
  49.4 0.1 multiply_reduce_fusion.3
  49.6 0.1 copy.59
  49.6 0.1 copy.60
  49.7 0.1 reshape.103
  49.9 0.1 pad_maximum_fusion.5
  50.0 0.8 pad_maximum_fusion.3
  50.7 3.4 %all-to-all-start.1 = ((f32[32,8,66]{2,0,1:T(8,128)}), f32[32,8,66]{2,0,1:T(8,128)S(1)}, u32[]{:S(2)}, u32[]{:S(2)}) async-start(f32[32,8,66]{2,0,1:T(8,128)} %pad_maximum_fusion.3), calls=%async_computation.1 | async-start | bytes 262144 | tf_op jit(solution)/shard_map/all_to_all | solution.py:12
  54.1 0.2 copy.64
  54.3 7.2 %all-to-all-done.1 = f32[32,8,66]{2,0,1:T(8,128)S(1)} async-done(((f32[32,8,66]{2,0,1:T(8,128)}), f32[32,8,66]{2,0,1:T(8,128)S(1)}, u32[]{:S(2)}, u32[]{:S(2)}) %all-to-all-start.1) | async-done | bytes 67616 | tf_op jit(solution)/shard_map/all_to_all | solution.py:12
  61.6 0.1 slice_reduce_fusion.1
  61.7 0.2 slice_reduce_fusion.4
  61.8 0.1 copy.63
  61.9 0.1 reshape.125
  62.0 0.1 copy.65
  62.2 3.5 %scatter_fusion = f32[32,1024]{0,1:T(8,128)S(1)} fusion(f32[32,1024]{0,1:T(8,128)S(1)} %copy.64, s32[512]{0:T(512)S(1)} %bitcast.36, f32[512,32]{1,0:T(8,128)S(1)} %copy.65), kind=kCustom, calls=%fused_computation.2 | custom fusion | flops 16384 | bytes 198656 | tf_op jit(solution)/shard_map/scatter-add | solution.py:149
  65.7 0.2 copy.66
  65.9 0.2 multiply_reduce_fusion.2
  66.1 0.2 copy.67
  66.3 1.0 gather_fusion.1
  67.3 0.1 copy.68
  67.5 0.8 reshape.143
  68.2 3.4 %all-to-all-start.2 = ((f32[8,1,2048]{2,1,0:T(1,128)}), f32[8,1,2048]{2,1,0:T(1,128)S(1)}, u32[]{:S(2)}, u32[]{:S(2)}) async-start(f32[8,1,2048]{2,1,0:T(1,128)} %reshape.143), calls=%async_computation.2 | async-start | bytes 131072 | tf_op jit(solution)/shard_map/all_to_all | solution.py:12
  71.6 0.1 copy.70
  71.7 0.1 copy.71
  71.8 6.7 %all-to-all-done.2 = f32[8,1,2048]{2,1,0:T(1,128)S(1)} async-done(((f32[8,1,2048]{2,1,0:T(1,128)}), f32[8,1,2048]{2,1,0:T(1,128)S(1)}, u32[]{:S(2)}, u32[]{:S(2)}) %all-to-all-start.2) | async-done | bytes 65568 | tf_op jit(solution)/shard_map/all_to_all | solution.py:12
  78.5 0.8 reduce.9
  79.3 0.1 reshape.144
  79.4 0.1 copy.69
  79.5 0.1 reshape.106
  79.6 26.7 %shard_map.69 = (f32[32,1536]{1,0:T(8,128)S(1)}, f32[32,1]{1,0:T(8,128)S(1)}) custom-call(f32[32,1536]{1,0:T(8,128)S(1)} %pad_maximum_fusion.1.xs_ref, s32[1,16384]{1,0:T(1,128)S(1)} %get-tuple-element.23.head_ref, s32[1,16384]{1,0:T(1,128)S(1)} %get-tuple-element.22.tail_ref, f32[1,16384]{1,0:T(1,128)S(1)} %bitcast.25), custom_call_target="tpu_custom_call" | custom-call | tf_op jit(solution)/shard_map/pallas_call | solution.py:117
  106.3 0.1 reshape.107
  106.4 0.1 pad_maximum_fusion.6
  106.5 0.8 pad_maximum_fusion.4
  107.3 3.4 %all-to-all-start.3 = ((f32[32,8,66]{2,0,1:T(8,128)}), f32[32,8,66]{2,0,1:T(8,128)S(1)}, u32[]{:S(2)}, u32[]{:S(2)}) async-start(f32[32,8,66]{2,0,1:T(8,128)} %pad_maximum_fusion.4), calls=%async_computation.3 | async-start | bytes 262144 | tf_op jit(solution)/shard_map/all_to_all | solution.py:12
  110.7 7.4 %all-to-all-done.3 = f32[32,8,66]{2,0,1:T(8,128)S(1)} async-done(((f32[32,8,66]{2,0,1:T(8,128)}), f32[32,8,66]{2,0,1:T(8,128)S(1)}, u32[]{:S(2)}, u32[]{:S(2)}) %all-to-all-start.3) | async-done | bytes 67616 | tf_op jit(solution)/shard_map/all_to_all | solution.py:12
  118.1 0.1 slice_reduce_fusion
  118.2 0.2 slice_reduce_fusion.2
  118.4 0.1 multiply_add_fusion.1
  118.5 0.1 multiply_add_fusion
  118.7 0.6 copy-done.2
  119.3 8.8 %all_gather.6.xs_ref = f32[128,1536]{1,0:T(8,128)S(1)} all-gather(f32[32,1536]{1,0:T(8,128)S(1)} %pad_maximum_fusion.2), channel_id=1, replica_groups=mesh['vx'=2,'vy'=4,'col'=4] {'col'}, dimensions={0}, use_global_device_ids=true | all-gather | bytes 983040 | tf_op jit(solution)/shard_map/all_gather | solution.py:181
  128.1 5.5 %shard_map.70 = f32[1,4096]{1,0:T(1,128)S(1)} custom-call(f32[128,1536]{1,0:T(8,128)S(1)} %all_gather.6.xs_ref, s32[1,4096]{1,0:T(1,128)S(1)} %get-tuple-element.25.head_ref, s32[1,4096]{1,0:T(1,128)S(1)} %get-tuple-element.24.tail_ref, f32[1,4096]{1,0:T(1,128)S(1)} %bitcast.26), custom_call_target="tpu_custom_call" | custom-call | tf_op jit(solution)/shard_map/pallas_call | solution.py:117
  133.6 5.2 %all-gather = f32[1,16384]{1,0:T(1,128)S(1)} all-gather(f32[1,4096]{1,0:T(1,128)S(1)} %shard_map.70), channel_id=2, replica_groups=mesh['vx'=2,'vy'=4,'col'=4] {'col'}, dimensions={1}, use_global_device_ids=true | all-gather | bytes 81920 | tf_op jit(solution)/shard_map/all_gather | solution.py:182
  138.9 0.6 copy.78
  (26 shorter events, 0.3 us)
Async XLA Ops:
  3.7 8.0 %copy-start.3 = (s32[2,16384]{1,0:T(2,128)S(1)}, s32[2,16384]{1,0:T(2,128)}, u32[]{:S(2)}) copy-start(s32[2,16384]{1,0:T(2,128)} %param.7) | copy-start | bytes 393220
  4.5 14.2 %all-to-all-start = ((f32[8,1,2048]{2,1,0:T(1,128)}), f32[8,1,2048]{2,1,0:T(1,128)S(1)}, u32[]{:S(2)}, u32[]{:S(2)}) async-start(f32[8,1,2048]{2,1,0:T(1,128)} %reshape.141), calls=%async_computation | async-start | bytes 131072 | tf_op jit(solution)/shard_map/all_to_all | solution.py:12
  11.7 0.7 copy-start.5
  20.3 0.9 copy-start.1
  21.2 0.8 copy-start
  48.7 0.7 copy-start.4
  50.7 10.8 %all-to-all-start.1 = ((f32[32,8,66]{2,0,1:T(8,128)}), f32[32,8,66]{2,0,1:T(8,128)S(1)}, u32[]{:S(2)}, u32[]{:S(2)}) async-start(f32[32,8,66]{2,0,1:T(8,128)} %pad_maximum_fusion.3), calls=%async_computation.1 | async-start | bytes 262144 | tf_op jit(solution)/shard_map/all_to_all | solution.py:12
  68.2 10.3 %all-to-all-start.2 = ((f32[8,1,2048]{2,1,0:T(1,128)}), f32[8,1,2048]{2,1,0:T(1,128)S(1)}, u32[]{:S(2)}, u32[]{:S(2)}) async-start(f32[8,1,2048]{2,1,0:T(1,128)} %reshape.143), calls=%async_computation.2 | async-start | bytes 131072 | tf_op jit(solution)/shard_map/all_to_all | solution.py:12
  107.3 10.8 %all-to-all-start.3 = ((f32[32,8,66]{2,0,1:T(8,128)}), f32[32,8,66]{2,0,1:T(8,128)S(1)}, u32[]{:S(2)}, u32[]{:S(2)}) async-start(f32[32,8,66]{2,0,1:T(8,128)} %pad_maximum_fusion.4), calls=%async_computation.3 | async-start | bytes 262144 | tf_op jit(solution)/shard_map/all_to_all | solution.py:12
  118.6 0.7 copy-start.2

commit v8 on v7

--- a/solution.py
+++ b/solution.py
@@ -9,7 +9,18 @@
 
 
 def trade(blocks):
-    return lax.all_to_all(blocks, ("vx", "vy"), split_axis=1, concat_axis=1, tiled=True)
+    axes = ("vx", "vy")
+    count = blocks.shape[1]
+    if count > 8:
+        return lax.all_to_all(blocks, axes, split_axis=1, concat_axis=1, tiled=True)
+    me = lax.axis_index(axes)
+    got = [lax.dynamic_slice_in_dim(blocks, me, 1, axis=1)]
+    for shift in range(1, count):
+        send = lax.dynamic_slice_in_dim(blocks, (me + shift) % count, 1, axis=1)
+        got.append(lax.ppermute(send, axes, [(i, (i + shift) % count) for i in range(count)]))
+    stacked = jnp.concatenate(got, axis=1)
+    order = (me - jnp.arange(count)) % count
+    return jnp.take(stacked, order, axis=1)
 
 
 def split3(values):

time: 140 us -> 148 us (1.057)
  starting transfers between devices: 17.3 us -> 48.3 us
  waiting for transfers between devices: 27.6 us -> 8.47 us
  other arithmetic: 8.37 us -> 5.2 us
    ppermute x0 -> x28, starting transfers between devices: none -> 48.3 us  [trade(): lax.ppermute(send, axes, [(i, (i + shift) % count) for i in range(count)])]
    all_to_all x4 -> x0, waiting for transfers between devices: 27.6 us -> none  [trade(): lax.all_to_all(blocks, ('vx', 'vy'), split_axis=1, concat_axis=1, tiled=T...]
    all_to_all x4 -> x0, starting transfers between devices: 17.3 us -> none  [trade(): lax.all_to_all(blocks, ('vx', 'vy'), split_axis=1, concat_axis=1, tiled=T...]
    ppermute x0 -> x28, waiting for transfers between devices: none -> 8.47 us  [trade(): lax.ppermute(send, axes, [(i, (i + shift) % count) for i in range(count)])]
    unnamed x20 -> x58, local copies, waits for them, and re-layouts: 6.94 us -> 4.69 us
    gather x0 -> x4, local copies, waits for them, and re-layouts: none -> 2.22 us  [trade(): return jnp.take(stacked, order, axis=1)]
    all_to_all x2 -> x0, other arithmetic: 1.68 us -> none  [trade(): lax.all_to_all(blocks, ('vx', 'vy'), split_axis=1, concat_axis=1, tiled=T...]
  transfers between devices with their start and end apart: 4 -> 28, of which waited for: 4 -> 9; matrix products, arithmetic and copies ran while one was open for 0% -> 1% of each run, Pallas kernels for 0% -> 0%
where the time goes in v8:
time: 148 us
  Pallas kernels  58.9 us (40%)
  starting transfers between devices  48.3 us (33%)
  blocking collectives  14 us (9%)
  local copies, waits for them, and re-layouts  11.4 us (8%)
  waiting for transfers between devices  8.47 us (6%)
  other arithmetic  5.2 us (4%)
    pallas_call x3, Pallas kernels, edge_pass(): pl.pallas_call(flow_kernel(scatter, local), grid=(edges // tile,), in_spe...  58.9 us
    ppermute x28, starting transfers between devices, trade(): lax.ppermute(send, axes, [(i, (i + shift) % count) for i in range(count)])  48.3 us
    all_gather x1, blocking collectives, body(): lax.all_gather(extended, 'col', axis=0, tiled=True)  8.73 us
    ppermute x28, waiting for transfers between devices, trade(): lax.ppermute(send, axes, [(i, (i + shift) % count) for i in range(count)])  8.47 us
    all_gather x1, blocking collectives, body(): resistance = lax.all_gather(total, 'col', axis=0, tiled=True)  5.25 us
    unnamed x58, local copies, waits for them, and re-layouts  4.69 us
    scatter-add x1, other arithmetic, operate(): local = summed[:, :count].at[:, halo_rows.reshape(-1)].add(returned)  3.51 us
  transfers between devices with their start and end apart: 28, of which 9 were waited for; matrix products, arithmetic and copies ran while one was open for 1% of the time, Pallas kernels for 0%

profile of v8, /device:TPU:0, one launch (start us, length us, event | category | flops | bytes accessed | tf_op | source)
XLA Modules:
  0.0 147.6 jit_solution(16132157033598379784)
XLA Ops:
  0.7 0.7 copy-done.5
  1.5 0.2 copy.138
  1.8 1.0 gather_fusion
  2.9 3.0 %collective-permute-start = (f32[32,1,64]{2,0,1:T(8,128)S(1)}, f32[32,1,64]{2,0,1:T(8,128)S(1)}, u32[]{:S(2)}, u32[]{:S(2)}) collective-permute-start(f32[32,1,64]{2,0,1:T(8,128)S(1)} %bitcast.54), channel_id=1, source_target_pairs={{0,4},{4,8},{8,12},{12,16},{16,20},{20,24},{24,28},{28,0},{1,5},{5... | collective-permute-start | bytes 24584 | tf_op jit(solution)/shard_map/ppermute | solution.py:20
  6.0 2.6 %collective-permute-start.1 = (f32[32,1,64]{2,0,1:T(8,128)S(1)}, f32[32,1,64]{2,0,1:T(8,128)S(1)}, u32[]{:S(2)}, u32[]{:S(2)}) collective-permute-start(f32[32,1,64]{2,0,1:T(8,128)S(1)} %bitcast.53), channel_id=1, source_target_pairs={{0,8},{4,12},{8,16},{12,20},{16,24},{20,28},{24,0},{28,4},{1,9},{5... | collective-permute-start | bytes 24584 | tf_op jit(solution)/shard_map/ppermute | solution.py:20
  8.7 2.3 %collective-permute-start.2 = (f32[32,1,64]{2,0,1:T(8,128)S(1)}, f32[32,1,64]{2,0,1:T(8,128)S(1)}, u32[]{:S(2)}, u32[]{:S(2)}) collective-permute-start(f32[32,1,64]{2,0,1:T(8,128)S(1)} %bitcast.52), channel_id=1, source_target_pairs={{0,12},{4,16},{8,20},{12,24},{16,28},{20,0},{24,4},{28,8},{1,13},{... | collective-permute-start | bytes 24584 | tf_op jit(solution)/shard_map/ppermute | solution.py:20
  11.0 0.5 collective-permute-start.3
  11.7 1.6 %collective-permute-start.4 = (f32[32,1,64]{2,0,1:T(8,128)S(1)}, f32[32,1,64]{2,0,1:T(8,128)S(1)}, u32[]{:S(2)}, u32[]{:S(2)}) collective-permute-start(f32[32,1,64]{2,0,1:T(8,128)S(1)} %bitcast.50), channel_id=1, source_target_pairs={{0,20},{4,24},{8,28},{12,0},{16,4},{20,8},{24,12},{28,16},{1,21},{... | collective-permute-start | bytes 24584 | tf_op jit(solution)/shard_map/ppermute | solution.py:20
  13.5 0.1 fusion.17
  13.8 0.7 copy-done
  14.5 1.2 collective-permute-start.5
  15.7 2.2 %collective-permute-start.6 = (f32[32,1,64]{2,0,1:T(8,128)S(1)}, f32[32,1,64]{2,0,1:T(8,128)S(1)}, u32[]{:S(2)}, u32[]{:S(2)}) collective-permute-start(f32[32,1,64]{2,0,1:T(8,128)S(1)} %bitcast.56), channel_id=1, source_target_pairs={{0,28},{4,0},{8,4},{12,8},{16,12},{20,16},{24,20},{28,24},{1,29},{... | collective-permute-start | bytes 24584 | tf_op jit(solution)/shard_map/ppermute | solution.py:20
  18.0 1.1 collective-permute-done.5
  19.1 0.8 collective-permute-done.6
  19.9 0.6 gather_fusion.2
  20.7 26.7 %shard_map.68 = (f32[32,1536]{1,0:T(8,128)S(1)}, f32[32,1]{1,0:T(8,128)S(1)}) custom-call(f32[32,1536]{1,0:T(8,128)S(1)} %pad_maximum_fusion.xs_ref, s32[1,16384]{1,0:T(1,128)S(1)} %get-tuple-element.57.head_ref, s32[1,16384]{1,0:T(1,128)S(1)} %get-tuple-element.56.tail_ref, f32[1,16384]{1,0:T(1,128)S(1)} %bitcast.40), custom_call_target="tpu_custom_call" | custom-call | tf_op jit(solution)/shard_map/pallas_call | solution.py:128
  47.4 0.7 copy-done.4
  48.1 0.1 multiply_reduce_fusion.3
  48.6 0.1 fusion.8
  48.8 2.1 %collective-permute-start.7 = (f32[32,1,66]{2,0,1:T(8,128)S(1)}, f32[32,1,66]{2,0,1:T(8,128)S(1)}, u32[]{:S(2)}, u32[]{:S(2)}) collective-permute-start(f32[32,1,66]{2,0,1:T(8,128)S(1)} %get-tuple-element.41), channel_id=1, source_target_pairs={{0,4},{4,8},{8,12},{12,16},{16,20},{20,24},{24,28},{28,0},{1,5},{5... | collective-permute-start | bytes 25352 | tf_op jit(solution)/shard_map/ppermute | solution.py:20
  50.9 3.3 %collective-permute-start.8 = (f32[32,1,66]{2,0,1:T(8,128)S(1)}, f32[32,1,66]{2,0,1:T(8,128)S(1)}, u32[]{:S(2)}, u32[]{:S(2)}) collective-permute-start(f32[32,1,66]{2,0,1:T(8,128)S(1)} %get-tuple-element.42), channel_id=1, source_target_pairs={{0,8},{4,12},{8,16},{12,20},{16,24},{20,28},{24,0},{28,4},{1,9},{5... | collective-permute-start | bytes 25352 | tf_op jit(solution)/shard_map/ppermute | solution.py:20
  54.2 2.5 %collective-permute-start.9 = (f32[32,1,66]{2,0,1:T(8,128)S(1)}, f32[32,1,66]{2,0,1:T(8,128)S(1)}, u32[]{:S(2)}, u32[]{:S(2)}) collective-permute-start(f32[32,1,66]{2,0,1:T(8,128)S(1)} %get-tuple-element.43), channel_id=1, source_target_pairs={{0,12},{4,16},{8,20},{12,24},{16,28},{20,0},{24,4},{28,8},{1,13},{... | collective-permute-start | bytes 25352 | tf_op jit(solution)/shard_map/ppermute | solution.py:20
  56.7 1.7 %collective-permute-start.10 = (f32[32,1,66]{2,0,1:T(8,128)S(1)}, f32[32,1,66]{2,0,1:T(8,128)S(1)}, u32[]{:S(2)}, u32[]{:S(2)}) collective-permute-start(f32[32,1,66]{2,0,1:T(8,128)S(1)} %get-tuple-element.44), channel_id=1, source_target_pairs={{0,16},{4,20},{8,24},{12,28},{16,0},{20,4},{24,8},{28,12},{1,17},{... | collective-permute-start | bytes 25352 | tf_op jit(solution)/shard_map/ppermute | solution.py:20
  58.3 0.2 copy.152
  58.6 1.6 %collective-permute-start.13 = (f32[32,1,66]{2,0,1:T(8,128)S(1)}, f32[32,1,66]{2,0,1:T(8,128)S(1)}, u32[]{:S(2)}, u32[]{:S(2)}) collective-permute-start(f32[32,1,66]{2,0,1:T(8,128)S(1)} %get-tuple-element.39), channel_id=1, source_target_pairs={{0,28},{4,0},{8,4},{12,8},{16,12},{20,16},{24,20},{28,24},{1,29},{... | collective-permute-start | bytes 25352 | tf_op jit(solution)/shard_map/ppermute | solution.py:20
  60.3 0.1 collective-permute-done.10
  60.4 2.8 %collective-permute-done.12 = f32[32,1,66]{2,0,1:T(8,128)S(1)} collective-permute-done((f32[32,1,66]{2,0,1:T(8,128)S(1)}, f32[32,1,66]{2,0,1:T(8,128)S(1)}, u32[]{:S(2)}, u32[]{:S(2)}) %collective-permute-start.12) | collective-permute-done | bytes 8480 | tf_op jit(solution)/shard_map/ppermute | solution.py:20
  63.3 0.6 gather_fusion.3
  64.0 0.2 slice_reduce_fusion.4
  64.4 0.1 copy.153
  64.5 3.5 %scatter_fusion = f32[32,1024]{0,1:T(8,128)S(1)} fusion(f32[32,1024]{0,1:T(8,128)S(1)} %copy.152, s32[512]{0:T(512)S(1)} %bitcast.64, f32[512,32]{1,0:T(8,128)S(1)} %copy.153), kind=kCustom, calls=%fused_computation.6 | custom fusion | flops 16384 | bytes 198656 | tf_op jit(solution)/shard_map/scatter-add | solution.py:160
  68.0 0.2 copy.154
  68.2 0.2 multiply_reduce_fusion.2
  68.4 0.2 copy.155
  68.6 1.0 gather_fusion.1
  69.8 0.7 collective-permute-start.14
  70.7 3.3 %collective-permute-start.15 = (f32[32,1,64]{2,0,1:T(8,128)S(1)}, f32[32,1,64]{2,0,1:T(8,128)S(1)}, u32[]{:S(2)}, u32[]{:S(2)}) collective-permute-start(f32[32,1,64]{2,0,1:T(8,128)S(1)} %bitcast.62), channel_id=1, source_target_pairs={{0,8},{4,12},{8,16},{12,20},{16,24},{20,28},{24,0},{28,4},{1,9},{5... | collective-permute-start | bytes 24584 | tf_op jit(solution)/shard_map/ppermute | solution.py:20
  74.0 0.7 collective-permute-start.16
  74.8 1.7 %collective-permute-start.17 = (f32[32,1,64]{2,0,1:T(8,128)S(1)}, f32[32,1,64]{2,0,1:T(8,128)S(1)}, u32[]{:S(2)}, u32[]{:S(2)}) collective-permute-start(f32[32,1,64]{2,0,1:T(8,128)S(1)} %bitcast.59), channel_id=1, source_target_pairs={{0,16},{4,20},{8,24},{12,28},{16,0},{20,4},{24,8},{28,12},{1,17},{... | collective-permute-start | bytes 24584 | tf_op jit(solution)/shard_map/ppermute | solution.py:20
  76.6 1.1 collective-permute-start.18
  78.0 0.9 collective-permute-start.19
  78.9 2.7 %collective-permute-start.20 = (f32[32,1,64]{2,0,1:T(8,128)S(1)}, f32[32,1,64]{2,0,1:T(8,128)S(1)}, u32[]{:S(2)}, u32[]{:S(2)}) collective-permute-start(f32[32,1,64]{2,0,1:T(8,128)S(1)} %bitcast.55), channel_id=1, source_target_pairs={{0,28},{4,0},{8,4},{12,8},{16,12},{20,16},{24,20},{28,24},{1,29},{... | collective-permute-start | bytes 24584 | tf_op jit(solution)/shard_map/ppermute | solution.py:20
  81.6 0.5 collective-permute-done.18
  82.1 0.5 collective-permute-done.19
  82.6 0.4 collective-permute-done.20
  83.0 0.6 gather_fusion.4
  83.9 26.7 %shard_map.69 = (f32[32,1536]{1,0:T(8,128)S(1)}, f32[32,1]{1,0:T(8,128)S(1)}) custom-call(f32[32,1536]{1,0:T(8,128)S(1)} %pad_maximum_fusion.1.xs_ref, s32[1,16384]{1,0:T(1,128)S(1)} %get-tuple-element.57.head_ref, s32[1,16384]{1,0:T(1,128)S(1)} %get-tuple-element.56.tail_ref, f32[1,16384]{1,0:T(1,128)S(1)} %bitcast.41), custom_call_target="tpu_custom_call" | custom-call | tf_op jit(solution)/shard_map/pallas_call | solution.py:128
  110.8 0.1 fusion
  110.9 1.8 %collective-permute-start.21 = (f32[32,1,66]{2,0,1:T(8,128)S(1)}, f32[32,1,66]{2,0,1:T(8,128)S(1)}, u32[]{:S(2)}, u32[]{:S(2)}) collective-permute-start(f32[32,1,66]{2,0,1:T(8,128)S(1)} %get-tuple-element.25), channel_id=1, source_target_pairs={{0,4},{4,8},{8,12},{12,16},{16,20},{20,24},{24,28},{28,0},{1,5},{5... | collective-permute-start | bytes 25352 | tf_op jit(solution)/shard_map/ppermute | solution.py:20
  112.8 1.3 collective-permute-start.25
  114.2 2.5 %collective-permute-start.22 = (f32[32,1,66]{2,0,1:T(8,128)S(1)}, f32[32,1,66]{2,0,1:T(8,128)S(1)}, u32[]{:S(2)}, u32[]{:S(2)}) collective-permute-start(f32[32,1,66]{2,0,1:T(8,128)S(1)} %get-tuple-element.26), channel_id=1, source_target_pairs={{0,8},{4,12},{8,16},{12,20},{16,24},{20,28},{24,0},{28,4},{1,9},{5... | collective-permute-start | bytes 25352 | tf_op jit(solution)/shard_map/ppermute | solution.py:20
  116.7 3.8 %collective-permute-start.23 = (f32[32,1,66]{2,0,1:T(8,128)S(1)}, f32[32,1,66]{2,0,1:T(8,128)S(1)}, u32[]{:S(2)}, u32[]{:S(2)}) collective-permute-start(f32[32,1,66]{2,0,1:T(8,128)S(1)} %get-tuple-element.27), channel_id=1, source_target_pairs={{0,12},{4,16},{8,20},{12,24},{16,28},{20,0},{24,4},{28,8},{1,13},{... | collective-permute-start | bytes 25352 | tf_op jit(solution)/shard_map/ppermute | solution.py:20
  120.5 0.5 collective-permute-start.24
  121.0 0.3 collective-permute-start.26
  121.3 2.2 %collective-permute-start.27 = (f32[32,1,66]{2,0,1:T(8,128)S(1)}, f32[32,1,66]{2,0,1:T(8,128)S(1)}, u32[]{:S(2)}, u32[]{:S(2)}) collective-permute-start(f32[32,1,66]{2,0,1:T(8,128)S(1)} %get-tuple-element.23), channel_id=1, source_target_pairs={{0,28},{4,0},{8,4},{12,8},{16,12},{20,16},{24,20},{28,24},{1,29},{... | collective-permute-start | bytes 25352 | tf_op jit(solution)/shard_map/ppermute | solution.py:20
  123.4 0.8 collective-permute-done.24
  124.2 1.4 collective-permute-done.26
  125.6 0.6 gather_fusion.5
  126.4 0.2 slice_reduce_fusion.2
  126.8 0.6 copy-done.2
  127.5 8.7 %all_gather.6.xs_ref = f32[128,1536]{1,0:T(8,128)S(1)} all-gather(f32[32,1536]{1,0:T(8,128)S(1)} %pad_maximum_fusion.2), channel_id=1, replica_groups=mesh['vx'=2,'vy'=4,'col'=4] {'col'}, dimensions={0}, use_global_device_ids=true | all-gather | bytes 983040 | tf_op jit(solution)/shard_map/all_gather | solution.py:192
  136.2 5.5 %shard_map.70 = f32[1,4096]{1,0:T(1,128)S(1)} custom-call(f32[128,1536]{1,0:T(8,128)S(1)} %all_gather.6.xs_ref, s32[1,4096]{1,0:T(1,128)S(1)} %get-tuple-element.59.head_ref, s32[1,4096]{1,0:T(1,128)S(1)} %get-tuple-element.58.tail_ref, f32[1,4096]{1,0:T(1,128)S(1)} %bitcast.42), custom_call_target="tpu_custom_call" | custom-call | tf_op jit(solution)/shard_map/pallas_call | solution.py:128
  141.7 5.2 %all-gather = f32[1,16384]{1,0:T(1,128)S(1)} all-gather(f32[1,4096]{1,0:T(1,128)S(1)} %shard_map.70), channel_id=2, replica_groups=mesh['vx'=2,'vy'=4,'col'=4] {'col'}, dimensions={1}, use_global_device_ids=true | all-gather | bytes 81920 | tf_op jit(solution)/shard_map/all_gather | solution.py:193
  147.0 0.6 copy.214
  (124 shorter events, 3.8 us)
Async XLA Ops:
  0.6 0.9 copy-start.1
  0.7 0.7 copy-start.5
  2.9 11.5 %collective-permute-start = (f32[32,1,64]{2,0,1:T(8,128)S(1)}, f32[32,1,64]{2,0,1:T(8,128)S(1)}, u32[]{:S(2)}, u32[]{:S(2)}) collective-permute-start(f32[32,1,64]{2,0,1:T(8,128)S(1)} %bitcast.54), channel_id=1, source_target_pairs={{0,4},{4,8},{8,12},{12,16},{16,20},{20,24},{24,28},{28,0},{1,5},{5... | collective-permute-start | bytes 24584 | tf_op jit(solution)/shard_map/ppermute | solution.py:20
  6.0 7.4 %copy-start.3 = (s32[2,16384]{1,0:T(2,128)S(1)}, s32[2,16384]{1,0:T(2,128)}, u32[]{:S(2)}) copy-start(s32[2,16384]{1,0:T(2,128)} %param.11) | copy-start | bytes 393220
  6.0 9.7 %collective-permute-start.1 = (f32[32,1,64]{2,0,1:T(8,128)S(1)}, f32[32,1,64]{2,0,1:T(8,128)S(1)}, u32[]{:S(2)}, u32[]{:S(2)}) collective-permute-start(f32[32,1,64]{2,0,1:T(8,128)S(1)} %bitcast.53), channel_id=1, source_target_pairs={{0,8},{4,12},{8,16},{12,20},{16,24},{20,28},{24,0},{28,4},{1,9},{5... | collective-permute-start | bytes 24584 | tf_op jit(solution)/shard_map/ppermute | solution.py:20
  8.7 9.3 %collective-permute-start.2 = (f32[32,1,64]{2,0,1:T(8,128)S(1)}, f32[32,1,64]{2,0,1:T(8,128)S(1)}, u32[]{:S(2)}, u32[]{:S(2)}) collective-permute-start(f32[32,1,64]{2,0,1:T(8,128)S(1)} %bitcast.52), channel_id=1, source_target_pairs={{0,12},{4,16},{8,20},{12,24},{16,28},{20,0},{24,4},{28,8},{1,13},{... | collective-permute-start | bytes 24584 | tf_op jit(solution)/shard_map/ppermute | solution.py:20
  11.0 6.9 %collective-permute-start.3 = (f32[32,1,64]{2,0,1:T(8,128)S(1)}, f32[32,1,64]{2,0,1:T(8,128)S(1)}, u32[]{:S(2)}, u32[]{:S(2)}) collective-permute-start(f32[32,1,64]{2,0,1:T(8,128)S(1)} %bitcast.51), channel_id=1, source_target_pairs={{0,16},{4,20},{8,24},{12,28},{16,0},{20,4},{24,8},{28,12},{1,17},{... | collective-permute-start | bytes 24584 | tf_op jit(solution)/shard_map/ppermute | solution.py:20
  11.7 6.3 %collective-permute-start.4 = (f32[32,1,64]{2,0,1:T(8,128)S(1)}, f32[32,1,64]{2,0,1:T(8,128)S(1)}, u32[]{:S(2)}, u32[]{:S(2)}) collective-permute-start(f32[32,1,64]{2,0,1:T(8,128)S(1)} %bitcast.50), channel_id=1, source_target_pairs={{0,20},{4,24},{8,28},{12,0},{16,4},{20,8},{24,12},{28,16},{1,21},{... | collective-permute-start | bytes 24584 | tf_op jit(solution)/shard_map/ppermute | solution.py:20
  13.6 0.8 copy-start
  14.5 4.6 %collective-permute-start.5 = (f32[32,1,64]{2,0,1:T(8,128)S(1)}, f32[32,1,64]{2,0,1:T(8,128)S(1)}, u32[]{:S(2)}, u32[]{:S(2)}) collective-permute-start(f32[32,1,64]{2,0,1:T(8,128)S(1)} %bitcast.60), channel_id=1, source_target_pairs={{0,24},{4,28},{8,0},{12,4},{16,8},{20,12},{24,16},{28,20},{1,25},{... | collective-permute-start | bytes 24584 | tf_op jit(solution)/shard_map/ppermute | solution.py:20
  15.7 4.2 %collective-permute-start.6 = (f32[32,1,64]{2,0,1:T(8,128)S(1)}, f32[32,1,64]{2,0,1:T(8,128)S(1)}, u32[]{:S(2)}, u32[]{:S(2)}) collective-permute-start(f32[32,1,64]{2,0,1:T(8,128)S(1)} %bitcast.56), channel_id=1, source_target_pairs={{0,28},{4,0},{8,4},{12,8},{16,12},{20,16},{24,20},{28,24},{1,29},{... | collective-permute-start | bytes 24584 | tf_op jit(solution)/shard_map/ppermute | solution.py:20
  47.4 0.7 copy-start.4
  48.8 9.8 %collective-permute-start.7 = (f32[32,1,66]{2,0,1:T(8,128)S(1)}, f32[32,1,66]{2,0,1:T(8,128)S(1)}, u32[]{:S(2)}, u32[]{:S(2)}) collective-permute-start(f32[32,1,66]{2,0,1:T(8,128)S(1)} %get-tuple-element.41), channel_id=1, source_target_pairs={{0,4},{4,8},{8,12},{12,16},{16,20},{20,24},{24,28},{28,0},{1,5},{5... | collective-permute-start | bytes 25352 | tf_op jit(solution)/shard_map/ppermute | solution.py:20
  50.9 9.5 %collective-permute-start.11 = (f32[32,1,66]{2,0,1:T(8,128)S(1)}, f32[32,1,66]{2,0,1:T(8,128)S(1)}, u32[]{:S(2)}, u32[]{:S(2)}) collective-permute-start(f32[32,1,66]{2,0,1:T(8,128)S(1)} %get-tuple-element.46), channel_id=1, source_target_pairs={{0,20},{4,24},{8,28},{12,0},{16,4},{20,8},{24,12},{28,16},{1,21},{... | collective-permute-start | bytes 25352 | tf_op jit(solution)/shard_map/ppermute | solution.py:20
  50.9 7.7 %collective-permute-start.8 = (f32[32,1,66]{2,0,1:T(8,128)S(1)}, f32[32,1,66]{2,0,1:T(8,128)S(1)}, u32[]{:S(2)}, u32[]{:S(2)}) collective-permute-start(f32[32,1,66]{2,0,1:T(8,128)S(1)} %get-tuple-element.42), channel_id=1, source_target_pairs={{0,8},{4,12},{8,16},{12,20},{16,24},{20,28},{24,0},{28,4},{1,9},{5... | collective-permute-start | bytes 25352 | tf_op jit(solution)/shard_map/ppermute | solution.py:20
  54.2 6.1 %collective-permute-start.9 = (f32[32,1,66]{2,0,1:T(8,128)S(1)}, f32[32,1,66]{2,0,1:T(8,128)S(1)}, u32[]{:S(2)}, u32[]{:S(2)}) collective-permute-start(f32[32,1,66]{2,0,1:T(8,128)S(1)} %get-tuple-element.43), channel_id=1, source_target_pairs={{0,12},{4,16},{8,20},{12,24},{16,28},{20,0},{24,4},{28,8},{1,13},{... | collective-permute-start | bytes 25352 | tf_op jit(solution)/shard_map/ppermute | solution.py:20
  56.7 3.7 %collective-permute-start.10 = (f32[32,1,66]{2,0,1:T(8,128)S(1)}, f32[32,1,66]{2,0,1:T(8,128)S(1)}, u32[]{:S(2)}, u32[]{:S(2)}) collective-permute-start(f32[32,1,66]{2,0,1:T(8,128)S(1)} %get-tuple-element.44), channel_id=1, source_target_pairs={{0,16},{4,20},{8,24},{12,28},{16,0},{20,4},{24,8},{28,12},{1,17},{... | collective-permute-start | bytes 25352 | tf_op jit(solution)/shard_map/ppermute | solution.py:20
  58.6 4.7 %collective-permute-start.12 = (f32[32,1,66]{2,0,1:T(8,128)S(1)}, f32[32,1,66]{2,0,1:T(8,128)S(1)}, u32[]{:S(2)}, u32[]{:S(2)}) collective-permute-start(f32[32,1,66]{2,0,1:T(8,128)S(1)} %get-tuple-element.45), channel_id=1, source_target_pairs={{0,24},{4,28},{8,0},{12,4},{16,8},{20,12},{24,16},{28,20},{1,25},{... | collective-permute-start | bytes 25352 | tf_op jit(solution)/shard_map/ppermute | solution.py:20
  58.6 4.6 %collective-permute-start.13 = (f32[32,1,66]{2,0,1:T(8,128)S(1)}, f32[32,1,66]{2,0,1:T(8,128)S(1)}, u32[]{:S(2)}, u32[]{:S(2)}) collective-permute-start(f32[32,1,66]{2,0,1:T(8,128)S(1)} %get-tuple-element.39), channel_id=1, source_target_pairs={{0,28},{4,0},{8,4},{12,8},{16,12},{20,16},{24,20},{28,24},{1,29},{... | collective-permute-start | bytes 25352 | tf_op jit(solution)/shard_map/ppermute | solution.py:20
  69.8 8.1 %collective-permute-start.14 = (f32[32,1,64]{2,0,1:T(8,128)S(1)}, f32[32,1,64]{2,0,1:T(8,128)S(1)}, u32[]{:S(2)}, u32[]{:S(2)}) collective-permute-start(f32[32,1,64]{2,0,1:T(8,128)S(1)} %bitcast.63), channel_id=1, source_target_pairs={{0,4},{4,8},{8,12},{12,16},{16,20},{20,24},{24,28},{28,0},{1,5},{5... | collective-permute-start | bytes 24584 | tf_op jit(solution)/shard_map/ppermute | solution.py:20
  70.7 8.3 %collective-permute-start.15 = (f32[32,1,64]{2,0,1:T(8,128)S(1)}, f32[32,1,64]{2,0,1:T(8,128)S(1)}, u32[]{:S(2)}, u32[]{:S(2)}) collective-permute-start(f32[32,1,64]{2,0,1:T(8,128)S(1)} %bitcast.62), channel_id=1, source_target_pairs={{0,8},{4,12},{8,16},{12,20},{16,24},{20,28},{24,0},{28,4},{1,9},{5... | collective-permute-start | bytes 24584 | tf_op jit(solution)/shard_map/ppermute | solution.py:20
  74.0 7.6 %collective-permute-start.16 = (f32[32,1,64]{2,0,1:T(8,128)S(1)}, f32[32,1,64]{2,0,1:T(8,128)S(1)}, u32[]{:S(2)}, u32[]{:S(2)}) collective-permute-start(f32[32,1,64]{2,0,1:T(8,128)S(1)} %bitcast.61), channel_id=1, source_target_pairs={{0,12},{4,16},{8,20},{12,24},{16,28},{20,0},{24,4},{28,8},{1,13},{... | collective-permute-start | bytes 24584 | tf_op jit(solution)/shard_map/ppermute | solution.py:20
  74.8 6.8 %collective-permute-start.17 = (f32[32,1,64]{2,0,1:T(8,128)S(1)}, f32[32,1,64]{2,0,1:T(8,128)S(1)}, u32[]{:S(2)}, u32[]{:S(2)}) collective-permute-start(f32[32,1,64]{2,0,1:T(8,128)S(1)} %bitcast.59), channel_id=1, source_target_pairs={{0,16},{4,20},{8,24},{12,28},{16,0},{20,4},{24,8},{28,12},{1,17},{... | collective-permute-start | bytes 24584 | tf_op jit(solution)/shard_map/ppermute | solution.py:20
  76.6 5.5 %collective-permute-start.18 = (f32[32,1,64]{2,0,1:T(8,128)S(1)}, f32[32,1,64]{2,0,1:T(8,128)S(1)}, u32[]{:S(2)}, u32[]{:S(2)}) collective-permute-start(f32[32,1,64]{2,0,1:T(8,128)S(1)} %bitcast.58), channel_id=1, source_target_pairs={{0,20},{4,24},{8,28},{12,0},{16,4},{20,8},{24,12},{28,16},{1,21},{... | collective-permute-start | bytes 24584 | tf_op jit(solution)/shard_map/ppermute | solution.py:20
  78.0 4.7 %collective-permute-start.19 = (f32[32,1,64]{2,0,1:T(8,128)S(1)}, f32[32,1,64]{2,0,1:T(8,128)S(1)}, u32[]{:S(2)}, u32[]{:S(2)}) collective-permute-start(f32[32,1,64]{2,0,1:T(8,128)S(1)} %bitcast.57), channel_id=1, source_target_pairs={{0,24},{4,28},{8,0},{12,4},{16,8},{20,12},{24,16},{28,20},{1,25},{... | collective-permute-start | bytes 24584 | tf_op jit(solution)/shard_map/ppermute | solution.py:20
  78.9 4.1 %collective-permute-start.20 = (f32[32,1,64]{2,0,1:T(8,128)S(1)}, f32[32,1,64]{2,0,1:T(8,128)S(1)}, u32[]{:S(2)}, u32[]{:S(2)}) collective-permute-start(f32[32,1,64]{2,0,1:T(8,128)S(1)} %bitcast.55), channel_id=1, source_target_pairs={{0,28},{4,0},{8,4},{12,8},{16,12},{20,16},{24,20},{28,24},{1,29},{... | collective-permute-start | bytes 24584 | tf_op jit(solution)/shard_map/ppermute | solution.py:20
  110.9 10.1 %collective-permute-start.21 = (f32[32,1,66]{2,0,1:T(8,128)S(1)}, f32[32,1,66]{2,0,1:T(8,128)S(1)}, u32[]{:S(2)}, u32[]{:S(2)}) collective-permute-start(f32[32,1,66]{2,0,1:T(8,128)S(1)} %get-tuple-element.25), channel_id=1, source_target_pairs={{0,4},{4,8},{8,12},{12,16},{16,20},{20,24},{24,28},{28,0},{1,5},{5... | collective-permute-start | bytes 25352 | tf_op jit(solution)/shard_map/ppermute | solution.py:20
  112.8 11.4 %collective-permute-start.25 = (f32[32,1,66]{2,0,1:T(8,128)S(1)}, f32[32,1,66]{2,0,1:T(8,128)S(1)}, u32[]{:S(2)}, u32[]{:S(2)}) collective-permute-start(f32[32,1,66]{2,0,1:T(8,128)S(1)} %get-tuple-element.30), channel_id=1, source_target_pairs={{0,20},{4,24},{8,28},{12,0},{16,4},{20,8},{24,12},{28,16},{1,21},{... | collective-permute-start | bytes 25352 | tf_op jit(solution)/shard_map/ppermute | solution.py:20
  114.2 7.1 %collective-permute-start.22 = (f32[32,1,66]{2,0,1:T(8,128)S(1)}, f32[32,1,66]{2,0,1:T(8,128)S(1)}, u32[]{:S(2)}, u32[]{:S(2)}) collective-permute-start(f32[32,1,66]{2,0,1:T(8,128)S(1)} %get-tuple-element.26), channel_id=1, source_target_pairs={{0,8},{4,12},{8,16},{12,20},{16,24},{20,28},{24,0},{28,4},{1,9},{5... | collective-permute-start | bytes 25352 | tf_op jit(solution)/shard_map/ppermute | solution.py:20
  116.7 6.7 %collective-permute-start.23 = (f32[32,1,66]{2,0,1:T(8,128)S(1)}, f32[32,1,66]{2,0,1:T(8,128)S(1)}, u32[]{:S(2)}, u32[]{:S(2)}) collective-permute-start(f32[32,1,66]{2,0,1:T(8,128)S(1)} %get-tuple-element.27), channel_id=1, source_target_pairs={{0,12},{4,16},{8,20},{12,24},{16,28},{20,0},{24,4},{28,8},{1,13},{... | collective-permute-start | bytes 25352 | tf_op jit(solution)/shard_map/ppermute | solution.py:20
  120.5 3.7 %collective-permute-start.24 = (f32[32,1,66]{2,0,1:T(8,128)S(1)}, f32[32,1,66]{2,0,1:T(8,128)S(1)}, u32[]{:S(2)}, u32[]{:S(2)}) collective-permute-start(f32[32,1,66]{2,0,1:T(8,128)S(1)} %get-tuple-element.28), channel_id=1, source_target_pairs={{0,16},{4,20},{8,24},{12,28},{16,0},{20,4},{24,8},{28,12},{1,17},{... | collective-permute-start | bytes 25352 | tf_op jit(solution)/shard_map/ppermute | solution.py:20
  121.0 4.6 %collective-permute-start.26 = (f32[32,1,66]{2,0,1:T(8,128)S(1)}, f32[32,1,66]{2,0,1:T(8,128)S(1)}, u32[]{:S(2)}, u32[]{:S(2)}) collective-permute-start(f32[32,1,66]{2,0,1:T(8,128)S(1)} %get-tuple-element.29), channel_id=1, source_target_pairs={{0,24},{4,28},{8,0},{12,4},{16,8},{20,12},{24,16},{28,20},{1,25},{... | collective-permute-start | bytes 25352 | tf_op jit(solution)/shard_map/ppermute | solution.py:20
  121.3 4.4 %collective-permute-start.27 = (f32[32,1,66]{2,0,1:T(8,128)S(1)}, f32[32,1,66]{2,0,1:T(8,128)S(1)}, u32[]{:S(2)}, u32[]{:S(2)}) collective-permute-start(f32[32,1,66]{2,0,1:T(8,128)S(1)} %get-tuple-element.23), channel_id=1, source_target_pairs={{0,28},{4,0},{8,4},{12,8},{16,12},{20,16},{24,20},{28,24},{1,29},{... | collective-permute-start | bytes 25352 | tf_op jit(solution)/shard_map/ppermute | solution.py:20
  126.8 0.7 copy-start.2

commit v9 on v7

--- a/solution.py
+++ b/solution.py
@@ -58,7 +58,9 @@
     return [(first, step) for first in range(0, rows, step)]
 
 
-def flow_kernel(scatter, local):
+def flow_kernel(mode, local):
+    scatter = mode == "scatter"
+
     def kernel(xs_ref, head_ref, tail_ref, w_ref, *out_ref):
         out_ref, acc = (out_ref[:2], out_ref[2:]) if scatter else (out_ref[0], ())
         step = pl.program_id(0)
@@ -75,14 +77,17 @@
             term = jnp.dot(xs[:, first:first + size], ends, preferred_element_type=jnp.float32)
             gap = term if gap is None else gap + term
         gap = gap[:width] + gap[width:2 * width] + gap[2 * width:]
-        if not scatter:
+        if mode == "gap":
             out_ref[...] = jnp.sum(gap * gap, axis=0, keepdims=True)
+            return
+        weighted = gap * w_ref[...]
+        energy = jnp.sum(gap * weighted, axis=1, keepdims=True)
+        if mode == "energy":
+            out_ref[...] = jnp.where(step == 0, 0.0, out_ref[...]) + energy
             return
         (total,) = acc
         energy_ref = out_ref[1]
         out_ref = out_ref[0]
-        weighted = gap * w_ref[...]
-        energy = jnp.sum(gap * weighted, axis=1, keepdims=True)
         energy_ref[...] = jnp.where(step == 0, 0.0, energy_ref[...]) + energy
         flow = split3(weighted)
         dims = (((1,), (1,)), ((), ()))
@@ -100,22 +105,26 @@
     return kernel
 
 
-def edge_pass(extended, head_rows, tail_slots, weights, scatter, local):
+def edge_pass(extended, head_rows, tail_slots, weights, mode, local):
     width, rows = extended.shape
     edges = head_rows.shape[1]
     tile = edge_tile(rows)
     edge_spec = pl.BlockSpec((1, tile), lambda i: (0, i))
     full = pl.BlockSpec((width, rows), lambda i: (0, 0))
-    if scatter:
+    if mode == "scatter":
         out_shape = (jax.ShapeDtypeStruct((width, rows), jnp.float32), jax.ShapeDtypeStruct((width, 1), jnp.float32))
         out_spec = (pl.BlockSpec((width, rows), lambda i: (0, 0)), pl.BlockSpec((width, 1), lambda i: (0, 0)))
         scratch = [pltpu.VMEM((3 * width, rows), jnp.float32)]
+    elif mode == "energy":
+        out_shape = jax.ShapeDtypeStruct((width, 1), jnp.float32)
+        out_spec = pl.BlockSpec((width, 1), lambda i: (0, 0))
+        scratch = []
     else:
         out_shape = jax.ShapeDtypeStruct((1, edges), jnp.float32)
         out_spec = edge_spec
         scratch = []
     return pl.pallas_call(
-        flow_kernel(scatter, local),
+        flow_kernel(mode, local),
         grid=(edges // tile,),
         in_specs=[full, edge_spec, edge_spec, edge_spec],
         out_specs=out_spec,
@@ -132,13 +141,19 @@
     return jnp.concatenate([field, mirrored.reshape(field.shape[0], -1)], axis=1)
 
 
-def operate(field, shift, head_rows, tail_slots, weights, halo_rows):
+def operate(field, shift, head_rows, tail_slots, weights, halo_rows, full=True):
     count = field.shape[1]
     width = field.shape[0]
     peers, cap = halo_rows.shape
     extended = extend(field, halo_rows)
-    summed, energy = edge_pass(extended, head_rows, tail_slots, weights, True, count)
     squares = field * field
+    if not full:
+        energy = edge_pass(extended, head_rows, tail_slots, weights, "energy", count)
+        own = jnp.stack([jnp.sum(squares, axis=1), jnp.sum(shift * squares, axis=1) + energy[:, 0]], axis=1)
+        got = trade(jnp.broadcast_to(own[:, None, :], (width, peers, 2)))
+        norm, product = jnp.sum(got, axis=1).T
+        return None, norm, product, extended[:, count:]
+    summed, energy = edge_pass(extended, head_rows, tail_slots, weights, "scatter", count)
     own = jnp.stack([jnp.sum(squares, axis=1), jnp.sum(shift * squares, axis=1) + energy[:, 0]], axis=1)
     sent = jnp.concatenate(
         [summed[:, count:].reshape(width, peers, cap), jnp.broadcast_to(own[:, None, :], (width, peers, 2))], axis=2
@@ -168,17 +183,19 @@
     for step in range(ITERS):
         solution = solution + alpha[:, None] * direction
         far_solution = far_solution + alpha[:, None] * far_direction
-        residual = residual - alpha[:, None] * along
+        residual = None if along is None else residual - alpha[:, None] * along
         if step + 1 < ITERS:
-            image, norm_next, product, mirrored = operate(residual, shift, head_rows, tail_slots, weights, halo_rows)
+            image, norm_next, product, mirrored = operate(
+                residual, shift, head_rows, tail_slots, weights, halo_rows, step + 2 < ITERS
+            )
             ratio = norm_next / norm_now
             alpha = norm_next / (product - ratio * norm_next / alpha)
             direction = residual + ratio[:, None] * direction
             far_direction = mirrored + ratio[:, None] * far_direction
-            along = image + ratio[:, None] * along
+            along = None if image is None else image + ratio[:, None] * along
             norm_now = norm_next
     extended = jnp.concatenate([solution, far_solution], axis=1)
-    total = edge_pass(lax.all_gather(extended, "col", axis=0, tiled=True), *quarter, False, solution.shape[1])[0]
+    total = edge_pass(lax.all_gather(extended, "col", axis=0, tiled=True), *quarter, "gap", solution.shape[1])[0]
     resistance = lax.all_gather(total, "col", axis=0, tiled=True)
     return (solution, resistance)
 

time: 140 us -> 123 us (0.88)
  Pallas kernels: 58.8 us -> 43.9 us
    pallas_call x3, Pallas kernels: 58.8 us -> 43.9 us  [edge_pass(): pl.pallas_call(flow_kernel(mode, local), grid=(edges // tile,), in_specs=...]
where the time goes in v9:
time: 123 us
  Pallas kernels  43.9 us (36%)
  waiting for transfers between devices  26.7 us (22%)
  starting transfers between devices  17.3 us (14%)
  blocking collectives  13.9 us (11%)
  local copies, waits for them, and re-layouts  12.6 us (10%)
  other arithmetic  7.46 us (6%)
    pallas_call x3, Pallas kernels, edge_pass(): pl.pallas_call(flow_kernel(mode, local), grid=(edges // tile,), in_specs=...  43.9 us
    all_to_all x4, waiting for transfers between devices, trade(): lax.all_to_all(blocks, ('vx', 'vy'), split_axis=1, concat_axis=1, tiled=T...  26.7 us
    all_to_all x4, starting transfers between devices, trade(): lax.all_to_all(blocks, ('vx', 'vy'), split_axis=1, concat_axis=1, tiled=T...  17.3 us
    all_gather x1, blocking collectives, body(): lax.all_gather(extended, 'col', axis=0, tiled=True)  8.61 us
    unnamed x20, local copies, waits for them, and re-layouts  6.94 us
    all_gather x1, blocking collectives, body(): resistance = lax.all_gather(total, 'col', axis=0, tiled=True)  5.25 us
    scatter-add x1, other arithmetic, operate(): local = summed[:, :count].at[:, halo_rows.reshape(-1)].add(returned)  3.51 us
  transfers between devices with their start and end apart: 4, of which 4 were waited for; matrix products, arithmetic and copies ran while one was open for 0% of the time, Pallas kernels for 0%

profile of v9, /device:TPU:0, one launch (start us, length us, event | category | flops | bytes accessed | tf_op | source)
XLA Modules:
  0.0 122.8 jit_solution(18251940201727194118)
XLA Ops:
  0.6 0.7 compare_select_fusion.1
  1.3 0.1 reshape.106
  1.4 1.1 copy.66
  2.5 1.0 gather_fusion
  3.6 0.1 copy.67
  3.7 0.0 copy-start.3
  3.7 0.8 reshape.135
  4.5 7.3 %all-to-all-start = ((f32[8,1,2048]{2,1,0:T(1,128)}), f32[8,1,2048]{2,1,0:T(1,128)S(1)}, u32[]{:S(2)}, u32[]{:S(2)}) async-start(f32[8,1,2048]{2,1,0:T(1,128)} %reshape.135), calls=%async_computation | async-start | bytes 131072 | tf_op jit(solution)/shard_map/all_to_all | solution.py:12
  11.7 0.0 copy-start.5
  11.7 0.1 fusion.3
  11.8 0.6 copy-done.5
  12.4 0.1 reshape.101
  12.5 6.2 %all-to-all-done = f32[8,1,2048]{2,1,0:T(1,128)S(1)} async-done(((f32[8,1,2048]{2,1,0:T(1,128)}), f32[8,1,2048]{2,1,0:T(1,128)S(1)}, u32[]{:S(2)}, u32[]{:S(2)}) %all-to-all-start) | async-done | bytes 65568 | tf_op jit(solution)/shard_map/all_to_all | solution.py:12
  18.7 0.6 broadcast.35
  19.3 0.8 reduce.4
  20.2 0.1 reshape.136
  20.2 0.1 copy.68
  20.3 0.1 reshape.99
  20.4 0.8 copy-done.1
  21.2 0.8 copy-done
  22.1 26.6 %shard_map.68 = (f32[32,1536]{1,0:T(8,128)S(1)}, f32[32,1]{1,0:T(8,128)S(1)}) custom-call(f32[32,1536]{1,0:T(8,128)S(1)} %pad_maximum_fusion.xs_ref, s32[1,16384]{1,0:T(1,128)S(1)} %get-tuple-element.17.head_ref, s32[1,16384]{1,0:T(1,128)S(1)} %get-tuple-element.16.tail_ref, f32[1,16384]{1,0:T(1,128)S(1)} %bitcast.39), custom_call_target="tpu_custom_call" | custom-call | tf_op jit(solution)/shard_map/pallas_call | solution.py:126
  48.7 0.0 copy-start.4
  48.8 0.7 copy-done.4
  49.4 0.1 multiply_reduce_fusion.3
  49.6 0.1 copy.69
  49.6 0.1 copy.70
  49.7 0.1 reshape.100
  49.9 0.1 pad_maximum_fusion.4
  50.0 0.8 pad_maximum_fusion.3
  50.7 3.4 %all-to-all-start.1 = ((f32[32,8,66]{2,0,1:T(8,128)}), f32[32,8,66]{2,0,1:T(8,128)S(1)}, u32[]{:S(2)}, u32[]{:S(2)}) async-start(f32[32,8,66]{2,0,1:T(8,128)} %pad_maximum_fusion.3), calls=%async_computation.1 | async-start | bytes 262144 | tf_op jit(solution)/shard_map/all_to_all | solution.py:12
  54.1 0.2 copy.74
  54.3 7.2 %all-to-all-done.1 = f32[32,8,66]{2,0,1:T(8,128)S(1)} async-done(((f32[32,8,66]{2,0,1:T(8,128)}), f32[32,8,66]{2,0,1:T(8,128)S(1)}, u32[]{:S(2)}, u32[]{:S(2)}) %all-to-all-start.1) | async-done | bytes 67616 | tf_op jit(solution)/shard_map/all_to_all | solution.py:12
  61.6 0.1 slice_reduce_fusion
  61.7 0.2 slice_reduce_fusion.1
  61.8 0.1 copy.73
  61.9 0.1 reshape.121
  62.0 0.1 copy.75
  62.2 3.5 %scatter_fusion = f32[32,1024]{0,1:T(8,128)S(1)} fusion(f32[32,1024]{0,1:T(8,128)S(1)} %copy.74, s32[512]{0:T(512)S(1)} %bitcast.50, f32[512,32]{1,0:T(8,128)S(1)} %copy.75), kind=kCustom, calls=%fused_computation.2 | custom fusion | flops 16384 | bytes 198656 | tf_op jit(solution)/shard_map/scatter-add | solution.py:164
  65.7 0.2 copy.76
  65.9 0.2 multiply_reduce_fusion.2
  66.1 0.2 copy.77
  66.3 1.0 gather_fusion.1
  67.3 0.1 copy.78
  67.5 0.8 reshape.137
  68.2 3.4 %all-to-all-start.2 = ((f32[8,1,2048]{2,1,0:T(1,128)}), f32[8,1,2048]{2,1,0:T(1,128)S(1)}, u32[]{:S(2)}, u32[]{:S(2)}) async-start(f32[8,1,2048]{2,1,0:T(1,128)} %reshape.137), calls=%async_computation.2 | async-start | bytes 131072 | tf_op jit(solution)/shard_map/all_to_all | solution.py:12
  71.6 0.1 copy.80
  71.7 6.8 %all-to-all-done.2 = f32[8,1,2048]{2,1,0:T(1,128)S(1)} async-done(((f32[8,1,2048]{2,1,0:T(1,128)}), f32[8,1,2048]{2,1,0:T(1,128)S(1)}, u32[]{:S(2)}, u32[]{:S(2)}) %all-to-all-start.2) | async-done | bytes 65568 | tf_op jit(solution)/shard_map/all_to_all | solution.py:12
  78.5 0.8 reduce.5
  79.4 0.1 reshape.138
  79.4 0.1 copy.79
  79.5 0.1 reshape.103
  79.6 11.7 %shard_map.69 = f32[32,1]{1,0:T(8,128)S(1)} custom-call(f32[32,1536]{1,0:T(8,128)S(1)} %pad_maximum_fusion.1.xs_ref, s32[1,16384]{1,0:T(1,128)S(1)} %get-tuple-element.17.head_ref, s32[1,16384]{1,0:T(1,128)S(1)} %get-tuple-element.16.tail_ref, f32[1,16384]{1,0:T(1,128)S(1)} %bitcast.40), custom_call_target="tpu_custom_call" | custom-call | tf_op jit(solution)/shard_map/pallas_call | solution.py:126
  91.4 0.1 copy.81
  91.5 0.6 broadcast_in_dim.11
  92.1 3.3 %all-to-all-start.3 = ((f32[32,8,2]{0,2,1:T(2,128)}), f32[32,8,2]{0,2,1:T(2,128)S(1)}, u32[]{:S(2)}, u32[]{:S(2)}) async-start(f32[32,8,2]{0,2,1:T(2,128)} %broadcast_in_dim.11), calls=%async_computation.3 | async-start | bytes 16384 | tf_op jit(solution)/shard_map/all_to_all | solution.py:12
  95.5 6.4 %all-to-all-done.3 = f32[32,8,2]{0,2,1:T(2,128)S(1)} async-done(((f32[32,8,2]{0,2,1:T(2,128)}), f32[32,8,2]{0,2,1:T(2,128)S(1)}, u32[]{:S(2)}, u32[]{:S(2)}) %all-to-all-start.3) | async-done | bytes 2080 | tf_op jit(solution)/shard_map/all_to_all | solution.py:12
  101.9 0.1 multiply_add_fusion.1
  102.0 0.1 multiply_add_fusion
  102.1 0.0 copy-start.2
  102.2 0.6 copy-done.2
  102.8 8.6 %all_gather.6.xs_ref = f32[128,1536]{1,0:T(8,128)S(1)} all-gather(f32[32,1536]{1,0:T(8,128)S(1)} %pad_maximum_fusion.2), channel_id=1, replica_groups=mesh['vx'=2,'vy'=4,'col'=4] {'col'}, dimensions={0}, use_global_device_ids=true | all-gather | bytes 983040 | tf_op jit(solution)/shard_map/all_gather | solution.py:198
  111.4 5.5 %shard_map.70 = f32[1,4096]{1,0:T(1,128)S(1)} custom-call(f32[128,1536]{1,0:T(8,128)S(1)} %all_gather.6.xs_ref, s32[1,4096]{1,0:T(1,128)S(1)} %get-tuple-element.19.head_ref, s32[1,4096]{1,0:T(1,128)S(1)} %get-tuple-element.18.tail_ref, f32[1,4096]{1,0:T(1,128)S(1)} %bitcast.41), custom_call_target="tpu_custom_call" | custom-call | tf_op jit(solution)/shard_map/pallas_call | solution.py:126
  116.9 5.2 %all-gather = f32[1,16384]{1,0:T(1,128)S(1)} all-gather(f32[1,4096]{1,0:T(1,128)S(1)} %shard_map.70), channel_id=2, replica_groups=mesh['vx'=2,'vy'=4,'col'=4] {'col'}, dimensions={1}, use_global_device_ids=true | all-gather | bytes 81920 | tf_op jit(solution)/shard_map/all_gather | solution.py:199
  122.2 0.6 copy.85
  (21 shorter events, 0.2 us)
Async XLA Ops:
  3.7 8.0 %copy-start.3 = (s32[2,16384]{1,0:T(2,128)S(1)}, s32[2,16384]{1,0:T(2,128)}, u32[]{:S(2)}) copy-start(s32[2,16384]{1,0:T(2,128)} %param.7) | copy-start | bytes 393220
  4.5 14.2 %all-to-all-start = ((f32[8,1,2048]{2,1,0:T(1,128)}), f32[8,1,2048]{2,1,0:T(1,128)S(1)}, u32[]{:S(2)}, u32[]{:S(2)}) async-start(f32[8,1,2048]{2,1,0:T(1,128)} %reshape.135), calls=%async_computation | async-start | bytes 131072 | tf_op jit(solution)/shard_map/all_to_all | solution.py:12
  11.7 0.7 copy-start.5
  20.3 0.9 copy-start.1
  21.2 0.8 copy-start
  48.7 0.7 copy-start.4
  50.7 10.8 %all-to-all-start.1 = ((f32[32,8,66]{2,0,1:T(8,128)}), f32[32,8,66]{2,0,1:T(8,128)S(1)}, u32[]{:S(2)}, u32[]{:S(2)}) async-start(f32[32,8,66]{2,0,1:T(8,128)} %pad_maximum_fusion.3), calls=%async_computation.1 | async-start | bytes 262144 | tf_op jit(solution)/shard_map/all_to_all | solution.py:12
  68.2 10.3 %all-to-all-start.2 = ((f32[8,1,2048]{2,1,0:T(1,128)}), f32[8,1,2048]{2,1,0:T(1,128)S(1)}, u32[]{:S(2)}, u32[]{:S(2)}) async-start(f32[8,1,2048]{2,1,0:T(1,128)} %reshape.137), calls=%async_computation.2 | async-start | bytes 131072 | tf_op jit(solution)/shard_map/all_to_all | solution.py:12
  92.1 9.8 %all-to-all-start.3 = ((f32[32,8,2]{0,2,1:T(2,128)}), f32[32,8,2]{0,2,1:T(2,128)S(1)}, u32[]{:S(2)}, u32[]{:S(2)}) async-start(f32[32,8,2]{0,2,1:T(2,128)} %broadcast_in_dim.11), calls=%async_computation.3 | async-start | bytes 16384 | tf_op jit(solution)/shard_map/all_to_all | solution.py:12
  102.1 0.7 copy-start.2

commit v10 on v9

--- a/solution.py
+++ b/solution.py
@@ -150,9 +150,7 @@
     if not full:
         energy = edge_pass(extended, head_rows, tail_slots, weights, "energy", count)
         own = jnp.stack([jnp.sum(squares, axis=1), jnp.sum(shift * squares, axis=1) + energy[:, 0]], axis=1)
-        got = trade(jnp.broadcast_to(own[:, None, :], (width, peers, 2)))
-        norm, product = jnp.sum(got, axis=1).T
-        return None, norm, product, extended[:, count:]
+        return None, own, None, extended
     summed, energy = edge_pass(extended, head_rows, tail_slots, weights, "scatter", count)
     own = jnp.stack([jnp.sum(squares, axis=1), jnp.sum(shift * squares, axis=1) + energy[:, 0]], axis=1)
     sent = jnp.concatenate(
@@ -162,7 +160,7 @@
     returned = got[:, :, :cap].reshape(width, -1)
     norm, product = jnp.sum(got[:, :, cap:], axis=1).T
     local = summed[:, :count].at[:, halo_rows.reshape(-1)].add(returned)
-    return shift * field + local, norm, product, extended[:, count:]
+    return shift * field + local, norm, product, extended
 
 
 def body(right_side, shift, edge_ends, weights, halo_rows):
@@ -172,30 +170,30 @@
     share = edge_ends.shape[1] // lax.axis_size("col")
     start = lax.axis_index("col") * share
     quarter = [lax.dynamic_slice_in_dim(item, start, share, axis=1) for item in (head_rows, tail_slots, weights)]
-    solution = jnp.zeros_like(right_side)
     residual = right_side
-    image, norm_now, product, mirrored = operate(residual, shift, head_rows, tail_slots, weights, halo_rows)
+    image, norm_now, product, first_ext = operate(residual, shift, head_rows, tail_slots, weights, halo_rows)
+    first_all = lax.all_gather(first_ext, "col", axis=0, tiled=True)
     alpha = norm_now / product
-    direction = residual
-    along = image
-    far_solution = jnp.zeros_like(mirrored)
-    far_direction = mirrored
-    for step in range(ITERS):
-        solution = solution + alpha[:, None] * direction
-        far_solution = far_solution + alpha[:, None] * far_direction
-        residual = None if along is None else residual - alpha[:, None] * along
-        if step + 1 < ITERS:
-            image, norm_next, product, mirrored = operate(
-                residual, shift, head_rows, tail_slots, weights, halo_rows, step + 2 < ITERS
-            )
-            ratio = norm_next / norm_now
-            alpha = norm_next / (product - ratio * norm_next / alpha)
-            direction = residual + ratio[:, None] * direction
-            far_direction = mirrored + ratio[:, None] * far_direction
-            along = None if image is None else image + ratio[:, None] * along
-            norm_now = norm_next
-    extended = jnp.concatenate([solution, far_solution], axis=1)
-    total = edge_pass(lax.all_gather(extended, "col", axis=0, tiled=True), *quarter, "gap", solution.shape[1])[0]
+    residual = residual - alpha[:, None] * image
+    _, own, _, second_ext = operate(residual, shift, head_rows, tail_slots, weights, halo_rows, False)
+    second_all = lax.all_gather(second_ext, "col", axis=0, tiled=True)
+    stats = jnp.concatenate([own, alpha[:, None], norm_now[:, None]], axis=1)
+    stats = lax.all_gather(stats, ("vx", "vy", "col"), axis=0, tiled=False)
+    parts = lax.axis_size(("vx", "vy"))
+    stats = stats.reshape(parts, -1, stats.shape[-1])
+    norm_next = jnp.sum(stats[:, :, 0], axis=0)
+    product = jnp.sum(stats[:, :, 1], axis=0)
+    alpha_all = stats[0, :, 2]
+    ratio = norm_next / stats[0, :, 3]
+    alpha_next = norm_next / (product - ratio * norm_next / alpha_all)
+    lead = alpha_all + alpha_next * ratio
+    width = right_side.shape[0]
+    mine = lax.axis_index("col") * width
+    own_lead = lax.dynamic_slice_in_dim(lead, mine, width)
+    own_next = lax.dynamic_slice_in_dim(alpha_next, mine, width)
+    solution = own_lead[:, None] * right_side + own_next[:, None] * residual
+    extended = lead[:, None] * first_all + alpha_next[:, None] * second_all
+    total = edge_pass(extended, *quarter, "gap", right_side.shape[1])[0]
     resistance = lax.all_gather(total, "col", axis=0, tiled=True)
     return (solution, resistance)
 

time: 123 us -> 153 us (1.24)
  blocking collectives: 13.9 us -> 59.6 us
  waiting for transfers between devices: 26.7 us -> 12.9 us
  local copies, waits for them, and re-layouts: 12.6 us -> 10 us
    all_gather x1 -> x3, blocking collectives: 8.61 us -> 54.4 us  [the longest x1 38.2 us: body(): stats = lax.all_gather(stats, ('vx', 'vy', 'col'), axis=0, tiled=False)]
    all_to_all x4 -> x3, waiting for transfers between devices: 26.7 us -> 12.9 us  [trade(): lax.all_to_all(blocks, ('vx', 'vy'), split_axis=1, concat_axis=1, tiled=T...]
    unnamed x20 -> x19, local copies, waits for them, and re-layouts: 6.94 us -> 4.95 us
    all_to_all x4 -> x3, starting transfers between devices: 17.3 us -> 16.7 us  [trade(): lax.all_to_all(blocks, ('vx', 'vy'), split_axis=1, concat_axis=1, tiled=T...]
  transfers between devices with their start and end apart: 4 -> 3, of which waited for: 4 -> 2; matrix products, arithmetic and copies ran while one was open for 0% -> 0% of each run, Pallas kernels for 0% -> 0%
where the time goes in v10:
time: 153 us
  blocking collectives  59.6 us (39%)
  Pallas kernels  44 us (29%)
  starting transfers between devices  16.7 us (11%)
  waiting for transfers between devices  12.9 us (8%)
  local copies, waits for them, and re-layouts  10 us (7%)
  other arithmetic  8.38 us (5%)
    pallas_call x3, Pallas kernels, edge_pass(): pl.pallas_call(flow_kernel(mode, local), grid=(edges // tile,), in_specs=...  44 us
    all_gather x1, blocking collectives, body(): stats = lax.all_gather(stats, ('vx', 'vy', 'col'), axis=0, tiled=False)  38.2 us
    all_to_all x3, starting transfers between devices, trade(): lax.all_to_all(blocks, ('vx', 'vy'), split_axis=1, concat_axis=1, tiled=T...  16.7 us
    all_to_all x3, waiting for transfers between devices, trade(): lax.all_to_all(blocks, ('vx', 'vy'), split_axis=1, concat_axis=1, tiled=T...  12.9 us
    all_gather x1, blocking collectives, body(): first_all = lax.all_gather(first_ext, 'col', axis=0, tiled=True)  8.63 us
    all_gather x1, blocking collectives, body(): second_all = lax.all_gather(second_ext, 'col', axis=0, tiled=True)  7.61 us
    all_gather x1, blocking collectives, body(): resistance = lax.all_gather(total, 'col', axis=0, tiled=True)  5.25 us
    unnamed x19, local copies, waits for them, and re-layouts  4.95 us
  transfers between devices with their start and end apart: 3, of which 2 were waited for; matrix products, arithmetic and copies ran while one was open for 0% of the time, Pallas kernels for 0%

profile of v10, /device:TPU:0, one launch (start us, length us, event | category | flops | bytes accessed | tf_op | source)
XLA Modules:
  0.0 152.5 jit_solution(5206039709810518641)
XLA Ops:
  0.6 0.7 compare_select_fusion.1
  1.3 0.1 reshape.117
  1.4 1.1 copy.89
  2.5 1.0 gather_fusion
  3.6 0.1 copy.90
  3.7 0.0 copy-start.2
  3.7 0.8 reshape.152
  4.5 7.4 %all-to-all-start = ((f32[8,1,2048]{2,1,0:T(1,128)}), f32[8,1,2048]{2,1,0:T(1,128)S(1)}, u32[]{:S(2)}, u32[]{:S(2)}) async-start(f32[8,1,2048]{2,1,0:T(1,128)} %reshape.152), calls=%async_computation | async-start | bytes 131072 | tf_op jit(solution)/shard_map/all_to_all | solution.py:12
  11.9 0.0 copy-done.4
  11.9 0.1 reshape.111
  12.0 0.0 copy-start.1
  12.0 0.1 fusion.1
  12.1 0.7 copy-done
  12.8 0.1 copy-done.1
  12.9 5.9 %all-to-all-done = f32[8,1,2048]{2,1,0:T(1,128)S(1)} async-done(((f32[8,1,2048]{2,1,0:T(1,128)}), f32[8,1,2048]{2,1,0:T(1,128)S(1)}, u32[]{:S(2)}, u32[]{:S(2)}) %all-to-all-start) | async-done | bytes 65568 | tf_op jit(solution)/shard_map/all_to_all | solution.py:12
  18.8 0.6 broadcast.37
  19.4 0.8 reduce.8
  20.3 0.1 reshape.153
  20.4 0.1 copy.91
  20.5 0.1 reshape.109
  20.6 26.7 %shard_map.68 = (f32[32,1536]{1,0:T(8,128)S(1)}, f32[32,1]{1,0:T(8,128)S(1)}) custom-call(f32[32,1536]{1,0:T(8,128)S(1)} %constant_dynamic-update-slice_fusion.xs_ref, s32[1,16384]{1,0:T(1,128)S(1)} %get-tuple-element.20.head_ref, s32[1,16384]{1,0:T(1,128)S(1)} %get-tuple-element.19.tail_ref, f32[1,16384]{1,0:T(1,128)S(1)} %bitcast.42), custom_call_target="tpu_custom_call" | custom-call | tf_op jit(solution)/shard_map/pallas_call | solution.py:126
  47.2 0.0 copy-start.3
  47.3 0.7 copy-done.3
  47.9 0.1 multiply_reduce_fusion.3
  48.1 0.1 copy.92
  48.2 0.1 copy.93
  48.2 0.1 reshape.110
  48.4 0.1 pad_maximum_fusion.2
  48.5 0.8 pad_maximum_fusion.1
  49.2 3.4 %all-to-all-start.1 = ((f32[32,8,66]{2,0,1:T(8,128)}), f32[32,8,66]{2,0,1:T(8,128)S(1)}, u32[]{:S(2)}, u32[]{:S(2)}) async-start(f32[32,8,66]{2,0,1:T(8,128)} %pad_maximum_fusion.1), calls=%async_computation.1 | async-start | bytes 262144 | tf_op jit(solution)/shard_map/all_to_all | solution.py:12
  52.6 8.6 %all_gather.17 = f32[128,1536]{1,0:T(8,128)S(1)} all-gather(f32[32,1536]{1,0:T(8,128)S(1)} %constant_dynamic-update-slice_fusion.xs_ref), channel_id=1, replica_groups=mesh['vx'=2,'vy'=4,'col'=4] {'col'}, dimensions={0}, use_global_device_ids=true | all-gather | bytes 983040 | tf_op jit(solution)/shard_map/all_gather | solution.py:175
  61.2 0.2 copy.97
  61.4 0.0 all-to-all-done.1
  61.4 0.1 slice_reduce_fusion
  61.6 0.2 slice_reduce_fusion.1
  61.8 0.1 copy.96
  61.9 0.1 reshape.132
  62.0 0.1 copy.98
  62.1 3.5 %scatter_fusion = f32[32,1024]{0,1:T(8,128)S(1)} fusion(f32[32,1024]{0,1:T(8,128)S(1)} %copy.97, s32[512]{0:T(512)S(1)} %bitcast.53, f32[512,32]{1,0:T(8,128)S(1)} %copy.98), kind=kCustom, calls=%fused_computation.2 | custom fusion | flops 16384 | bytes 198656 | tf_op jit(solution)/shard_map/scatter-add | solution.py:162
  65.6 0.2 copy.99
  65.8 0.2 multiply_reduce_fusion.2
  66.0 0.1 copy.103
  66.1 0.2 copy.100
  66.3 1.0 gather_fusion.1
  67.3 0.1 copy.101
  67.5 0.8 reshape.154
  68.2 5.9 %all-to-all-start.2 = ((f32[8,1,2048]{2,1,0:T(1,128)}), f32[8,1,2048]{2,1,0:T(1,128)S(1)}, u32[]{:S(2)}, u32[]{:S(2)}) async-start(f32[8,1,2048]{2,1,0:T(1,128)} %reshape.154), calls=%async_computation.2 | async-start | bytes 131072 | tf_op jit(solution)/shard_map/all_to_all | solution.py:12
  74.1 7.0 %all-to-all-done.2 = f32[8,1,2048]{2,1,0:T(1,128)S(1)} async-done(((f32[8,1,2048]{2,1,0:T(1,128)}), f32[8,1,2048]{2,1,0:T(1,128)S(1)}, u32[]{:S(2)}, u32[]{:S(2)}) %all-to-all-start.2) | async-done | bytes 65568 | tf_op jit(solution)/shard_map/all_to_all | solution.py:12
  81.1 0.8 reduce.9
  82.0 0.1 reshape.155
  82.1 0.1 copy.102
  82.1 0.1 reshape.113
  82.3 11.7 %shard_map.69 = f32[32,1]{1,0:T(8,128)S(1)} custom-call(f32[32,1536]{1,0:T(8,128)S(1)} %pad_maximum_fusion.xs_ref, s32[1,16384]{1,0:T(1,128)S(1)} %get-tuple-element.20.head_ref, s32[1,16384]{1,0:T(1,128)S(1)} %get-tuple-element.19.tail_ref, f32[1,16384]{1,0:T(1,128)S(1)} %bitcast.43), custom_call_target="tpu_custom_call" | custom-call | tf_op jit(solution)/shard_map/pallas_call | solution.py:126
  94.0 7.6 %all_gather.18 = f32[128,1536]{1,0:T(8,128)S(1)} all-gather(f32[32,1536]{1,0:T(8,128)S(1)} %pad_maximum_fusion.xs_ref), channel_id=1, replica_groups=mesh['vx'=2,'vy'=4,'col'=4] {'col'}, dimensions={0}, use_global_device_ids=true | all-gather | bytes 983040 | tf_op jit(solution)/shard_map/all_gather | solution.py:179
  101.6 0.1 copy.104
  101.7 38.2 %all-gather.2 = f32[32,32,4]{1,2,0:T(4,128)S(1)} all-gather(f32[1,32,4]{1,2,0:T(4,128)S(1)} %maximum_bitcast_fusion), channel_id=2, replica_groups=mesh['vx'=2,'vy'=4,'col'=4] {'vx','vy','col'}, dimensions={0}, use_global_device_ids=true | all-gather | bytes 16896 | tf_op jit(solution)/shard_map/all_gather | solution.py:181
  139.9 0.1 reshape.114
  140.0 0.1 dynamic_slice.15
  140.1 0.1 dynamic_slice.16
  140.1 0.2 multiply_add_fusion.xs_ref
  140.3 5.6 %shard_map.70 = f32[1,4096]{1,0:T(1,128)S(1)} custom-call(f32[128,1536]{1,0:T(8,128)S(1)} %multiply_add_fusion.xs_ref, s32[1,4096]{1,0:T(1,128)S(1)} %get-tuple-element.22.head_ref, s32[1,4096]{1,0:T(1,128)S(1)} %get-tuple-element.21.tail_ref, f32[1,4096]{1,0:T(1,128)S(1)} %bitcast.44), custom_call_target="tpu_custom_call" | custom-call | tf_op jit(solution)/shard_map/pallas_call | solution.py:126
  145.9 5.2 %all-gather.1 = f32[1,16384]{1,0:T(1,128)S(1)} all-gather(f32[1,4096]{1,0:T(1,128)S(1)} %shard_map.70), channel_id=3, replica_groups=mesh['vx'=2,'vy'=4,'col'=4] {'col'}, dimensions={1}, use_global_device_ids=true | all-gather | bytes 81920 | tf_op jit(solution)/shard_map/all_gather | solution.py:197
  151.1 0.7 multiply_add_fusion.1
  151.9 0.6 copy.110
  (22 shorter events, 0.2 us)
Async XLA Ops:
  3.7 8.2 %copy-start.2 = (s32[2,16384]{1,0:T(2,128)S(1)}, s32[2,16384]{1,0:T(2,128)}, u32[]{:S(2)}) copy-start(s32[2,16384]{1,0:T(2,128)} %param.7) | copy-start | bytes 393220
  4.5 7.4 %copy-start.4 = (s32[8,64]{1,0:T(8,128)S(1)}, s32[8,64]{1,0:T(8,128)}, u32[]{:S(2)}) copy-start(s32[8,64]{1,0:T(8,128)} %param.9) | copy-start | bytes 6148
  4.5 14.4 %all-to-all-start = ((f32[8,1,2048]{2,1,0:T(1,128)}), f32[8,1,2048]{2,1,0:T(1,128)S(1)}, u32[]{:S(2)}, u32[]{:S(2)}) async-start(f32[8,1,2048]{2,1,0:T(1,128)} %reshape.152), calls=%async_computation | async-start | bytes 131072 | tf_op jit(solution)/shard_map/all_to_all | solution.py:12
  11.9 0.8 copy-start
  12.0 0.9 copy-start.1
  47.2 0.7 copy-start.3
  49.2 12.2 %all-to-all-start.1 = ((f32[32,8,66]{2,0,1:T(8,128)}), f32[32,8,66]{2,0,1:T(8,128)S(1)}, u32[]{:S(2)}, u32[]{:S(2)}) async-start(f32[32,8,66]{2,0,1:T(8,128)} %pad_maximum_fusion.1), calls=%async_computation.1 | async-start | bytes 262144 | tf_op jit(solution)/shard_map/all_to_all | solution.py:12
  68.2 12.9 %all-to-all-start.2 = ((f32[8,1,2048]{2,1,0:T(1,128)}), f32[8,1,2048]{2,1,0:T(1,128)S(1)}, u32[]{:S(2)}, u32[]{:S(2)}) async-start(f32[8,1,2048]{2,1,0:T(1,128)} %reshape.154), calls=%async_computation.2 | async-start | bytes 131072 | tf_op jit(solution)/shard_map/all_to_all | solution.py:12

commit v11 on v9

--- a/solution.py
+++ b/solution.py
@@ -136,8 +136,15 @@
     )(extended, head_rows, tail_slots, weights)
 
 
+def picker(halo_rows, count):
+    flat = halo_rows.reshape(-1, 1)
+    return (flat == lax.broadcasted_iota(jnp.int32, (flat.shape[0], count), 1)).astype(jnp.float32)
+
+
 def extend(field, halo_rows):
-    mirrored = trade(field[:, halo_rows])
+    peers, cap = halo_rows.shape
+    chosen = jnp.dot(field, picker(halo_rows, field.shape[1]).T, precision=lax.Precision.HIGHEST)
+    mirrored = trade(chosen.reshape(field.shape[0], peers, cap))
     return jnp.concatenate([field, mirrored.reshape(field.shape[0], -1)], axis=1)
 
 
@@ -161,7 +168,7 @@
     got = trade(sent)
     returned = got[:, :, :cap].reshape(width, -1)
     norm, product = jnp.sum(got[:, :, cap:], axis=1).T
-    local = summed[:, :count].at[:, halo_rows.reshape(-1)].add(returned)
+    local = summed[:, :count] + jnp.dot(returned, picker(halo_rows, count), precision=lax.Precision.HIGHEST)
     return shift * field + local, norm, product, extended[:, count:]
 
 

time: 123 us -> 115 us (0.935)
  blocking collectives: 13.9 us -> 23.8 us
  waiting for transfers between devices: 26.7 us -> 19.8 us
  local copies, waits for them, and re-layouts: 12.6 us -> 5.81 us
  other arithmetic: 7.46 us -> 2.28 us
  matrix products: 0 us -> 4.31 us
  starting transfers between devices: 17.3 us -> 13.9 us
    all_to_all x0 -> x1, blocking collectives: none -> 9.91 us  [trade(): lax.all_to_all(blocks, ('vx', 'vy'), split_axis=1, concat_axis=1, tiled=T...]
    all_to_all x4 -> x3, waiting for transfers between devices: 26.7 us -> 19.8 us  [trade(): lax.all_to_all(blocks, ('vx', 'vy'), split_axis=1, concat_axis=1, tiled=T...]
    unnamed x20 -> x15, local copies, waits for them, and re-layouts: 6.94 us -> 2.34 us
    dot_general x0 -> x3, matrix products: none -> 4.31 us  [the longest x2 3.29 us: extend(): jnp.dot(field, picker(halo_rows, field.shape[1]).T, precision=lax.Precisi...]
    scatter-add x1 -> x0, other arithmetic: 3.51 us -> none  [operate(): local = summed[:, :count].at[:, halo_rows.reshape(-1)].add(returned)]
    all_to_all x4 -> x3, starting transfers between devices: 17.3 us -> 13.9 us  [trade(): lax.all_to_all(blocks, ('vx', 'vy'), split_axis=1, concat_axis=1, tiled=T...]
    gather x4 -> x0, local copies, waits for them, and re-layouts: 2.31 us -> none  [extend(): mirrored = trade(field[:, halo_rows])]
  transfers between devices with their start and end apart: 4 -> 3, of which waited for: 4 -> 3; matrix products, arithmetic and copies ran while one was open for 0% -> 0% of each run, Pallas kernels for 0% -> 0%
where the time goes in v11:
time: 115 us
  Pallas kernels  43.9 us (38%)
  blocking collectives  23.8 us (21%)
  waiting for transfers between devices  19.8 us (17%)
  starting transfers between devices  13.9 us (12%)
  local copies, waits for them, and re-layouts  5.81 us (5%)
  matrix products  4.31 us (4%)
  other arithmetic  2.28 us (2%)
    pallas_call x3, Pallas kernels, edge_pass(): pl.pallas_call(flow_kernel(mode, local), grid=(edges // tile,), in_specs=...  43.9 us
    all_to_all x3, waiting for transfers between devices, trade(): lax.all_to_all(blocks, ('vx', 'vy'), split_axis=1, concat_axis=1, tiled=T...  19.8 us
    all_to_all x3, starting transfers between devices, trade(): lax.all_to_all(blocks, ('vx', 'vy'), split_axis=1, concat_axis=1, tiled=T...  13.9 us
    all_to_all x1, blocking collectives, trade(): lax.all_to_all(blocks, ('vx', 'vy'), split_axis=1, concat_axis=1, tiled=T...  9.91 us
    all_gather x1, blocking collectives, body(): lax.all_gather(extended, 'col', axis=0, tiled=True)  8.63 us
    all_gather x1, blocking collectives, body(): resistance = lax.all_gather(total, 'col', axis=0, tiled=True)  5.25 us
    dot_general x2, matrix products, extend(): jnp.dot(field, picker(halo_rows, field.shape[1]).T, precision=lax.Precisi...  3.29 us
    unnamed x15, local copies, waits for them, and re-layouts  2.34 us
  transfers between devices with their start and end apart: 3, of which 3 were waited for; matrix products, arithmetic and copies ran while one was open for 0% of the time, Pallas kernels for 0%

profile of v11, /device:TPU:0, one launch (start us, length us, event | category | flops | bytes accessed | tf_op | source)
XLA Modules:
  0.0 114.8 jit_solution(16877879149687170954)
XLA Ops:
  0.6 0.0 copy-start.3
  0.6 0.8 eq.6
  1.4 0.0 copy-start.1
  1.4 0.0 copy-start.4
  1.4 2.1 %fusion.7 = f32[32,512]{1,0:T(8,128)S(1)} fusion(f32[32,1024]{1,0:T(8,128)} %param.5, s32[512]{0:T(512)S(1)} %eq.6), kind=kOutput, calls=%fused_computation.8 | convolution fusion | flops 201850880 | bytes 198656 | tf_op jit(solution)/shard_map/dot_general | solution.py:146
  3.6 0.1 reshape.78
  3.7 0.8 reshape.87
  4.5 7.3 %all-to-all-start = ((f32[8,1,2048]{2,1,0:T(1,128)}), f32[8,1,2048]{2,1,0:T(1,128)S(1)}, u32[]{:S(2)}, u32[]{:S(2)}) async-start(f32[8,1,2048]{2,1,0:T(1,128)} %reshape.87), calls=%async_computation | async-start | bytes 131072 | tf_op jit(solution)/shard_map/all_to_all | solution.py:12
  11.7 0.0 copy-done.3
  11.7 0.0 copy-start
  11.8 0.1 fusion.14
  11.9 0.0 copy-done.1
  11.9 0.0 copy-done.4
  11.9 0.1 multiply_reduce_fusion.3
  12.0 0.1 copy.47
  12.1 0.1 copy.48
  12.2 6.5 %all-to-all-done = f32[8,1,2048]{2,1,0:T(1,128)S(1)} async-done(((f32[8,1,2048]{2,1,0:T(1,128)}), f32[8,1,2048]{2,1,0:T(1,128)S(1)}, u32[]{:S(2)}, u32[]{:S(2)}) %all-to-all-start) | async-done | bytes 65568 | tf_op jit(solution)/shard_map/all_to_all | solution.py:12
  18.7 0.5 broadcast.5
  19.2 0.8 reduce.4
  20.0 0.1 reshape.88
  20.1 0.1 copy.46
  20.2 0.1 reshape.79
  20.3 0.0 copy-done
  20.3 26.7 %shard_map.68 = (f32[32,1536]{1,0:T(8,128)S(1)}, f32[32,1]{1,0:T(8,128)S(1)}) custom-call(f32[32,1536]{1,0:T(8,128)S(1)} %pad_maximum_fusion.xs_ref, s32[1,16384]{1,0:T(1,128)S(1)} %get-tuple-element.15.head_ref, s32[1,16384]{1,0:T(1,128)S(1)} %get-tuple-element.14.tail_ref, f32[1,16384]{1,0:T(1,128)S(1)} %bitcast.38), custom_call_target="tpu_custom_call" | custom-call | tf_op jit(solution)/shard_map/pallas_call | solution.py:126
  47.0 0.1 reshape.80
  47.1 0.1 pad_maximum_fusion.4
  47.2 0.1 pad_maximum_fusion.3
  47.3 9.9 %all_to_all.20 = f32[32,8,66]{2,0,1:T(8,128)S(1)} all-to-all(f32[32,8,66]{2,0,1:T(8,128)S(1)} %pad_maximum_fusion.3), channel_id=1, replica_groups=mesh['vx'=2,'vy'=4,'col'=4] {'vx','vy'}, dimensions={1} | all-to-all | bytes 135168 | tf_op jit(solution)/shard_map/all_to_all | solution.py:12
  57.3 0.1 slice_reduce_fusion
  57.4 0.2 slice_reduce_fusion.1
  57.5 0.1 copy.51
  57.6 0.1 reshape.81
  57.7 1.0 multiply_reduce_fusion.2
  58.8 1.2 %fusion = f32[32,512]{1,0:T(8,128)S(1)} fusion(f32[32,1024]{1,0:T(8,128)S(1)} %get-tuple-element.16, s32[512]{0:T(512)S(1)} %eq.6), kind=kOutput, calls=%fused_computation.1 | convolution fusion | flops 201850880 | bytes 198656 | tf_op jit(solution)/shard_map/dot_general | solution.py:146
  59.9 0.1 reshape.82
  60.1 0.8 reshape.89
  60.8 3.4 %all-to-all-start.2 = ((f32[8,1,2048]{2,1,0:T(1,128)}), f32[8,1,2048]{2,1,0:T(1,128)S(1)}, u32[]{:S(2)}, u32[]{:S(2)}) async-start(f32[8,1,2048]{2,1,0:T(1,128)} %reshape.89), calls=%async_computation.2 | async-start | bytes 131072 | tf_op jit(solution)/shard_map/all_to_all | solution.py:12
  64.2 0.1 copy.54
  64.3 6.8 %all-to-all-done.2 = f32[8,1,2048]{2,1,0:T(1,128)S(1)} async-done(((f32[8,1,2048]{2,1,0:T(1,128)}), f32[8,1,2048]{2,1,0:T(1,128)S(1)}, u32[]{:S(2)}, u32[]{:S(2)}) %all-to-all-start.2) | async-done | bytes 65568 | tf_op jit(solution)/shard_map/all_to_all | solution.py:12
  71.1 0.8 reduce.5
  71.9 0.1 reshape.90
  72.0 0.1 copy.53
  72.1 0.1 reshape.83
  72.2 11.7 %shard_map.69 = f32[32,1]{1,0:T(8,128)S(1)} custom-call(f32[32,1536]{1,0:T(8,128)S(1)} %pad_maximum_fusion.1.xs_ref, s32[1,16384]{1,0:T(1,128)S(1)} %get-tuple-element.15.head_ref, s32[1,16384]{1,0:T(1,128)S(1)} %get-tuple-element.14.tail_ref, f32[1,16384]{1,0:T(1,128)S(1)} %bitcast.39), custom_call_target="tpu_custom_call" | custom-call | tf_op jit(solution)/shard_map/pallas_call | solution.py:126
  84.0 0.1 copy.55
  84.0 0.6 broadcast_in_dim.8
  84.7 3.3 %all-to-all-start.3 = ((f32[32,8,2]{0,2,1:T(2,128)}), f32[32,8,2]{0,2,1:T(2,128)S(1)}, u32[]{:S(2)}, u32[]{:S(2)}) async-start(f32[32,8,2]{0,2,1:T(2,128)} %broadcast_in_dim.8), calls=%async_computation.3 | async-start | bytes 16384 | tf_op jit(solution)/shard_map/all_to_all | solution.py:12
  88.0 6.4 %all-to-all-done.3 = f32[32,8,2]{0,2,1:T(2,128)S(1)} async-done(((f32[32,8,2]{0,2,1:T(2,128)}), f32[32,8,2]{0,2,1:T(2,128)S(1)}, u32[]{:S(2)}, u32[]{:S(2)}) %all-to-all-start.3) | async-done | bytes 2080 | tf_op jit(solution)/shard_map/all_to_all | solution.py:12
  94.5 0.1 multiply_add_fusion.1
  94.6 0.1 multiply_add_fusion
  94.7 0.0 copy-start.2
  94.7 8.6 %all_gather.6.xs_ref = f32[128,1536]{1,0:T(8,128)S(1)} all-gather(f32[32,1536]{1,0:T(8,128)S(1)} %pad_maximum_fusion.2), channel_id=1, replica_groups=mesh['vx'=2,'vy'=4,'col'=4] {'col'}, dimensions={0}, use_global_device_ids=true | all-gather | bytes 983040 | tf_op jit(solution)/shard_map/all_gather | solution.py:205
  103.3 5.5 %shard_map.70 = f32[1,4096]{1,0:T(1,128)S(1)} custom-call(f32[128,1536]{1,0:T(8,128)S(1)} %all_gather.6.xs_ref, s32[1,4096]{1,0:T(1,128)S(1)} %get-tuple-element.18.head_ref, s32[1,4096]{1,0:T(1,128)S(1)} %get-tuple-element.17.tail_ref, f32[1,4096]{1,0:T(1,128)S(1)} %bitcast.40), custom_call_target="tpu_custom_call" | custom-call | tf_op jit(solution)/shard_map/pallas_call | solution.py:126
  108.9 0.0 copy-done.2
  108.9 5.2 %all-gather = f32[1,16384]{1,0:T(1,128)S(1)} all-gather(f32[1,4096]{1,0:T(1,128)S(1)} %shard_map.70), channel_id=2, replica_groups=mesh['vx'=2,'vy'=4,'col'=4] {'col'}, dimensions={1}, use_global_device_ids=true | all-gather | bytes 81920 | tf_op jit(solution)/shard_map/all_gather | solution.py:206
  114.2 0.6 copy.62
  (16 shorter events, 0.2 us)
Async XLA Ops:
  0.6 11.1 %copy-start.3 = (s32[2,16384]{1,0:T(2,128)S(1)}, s32[2,16384]{1,0:T(2,128)}, u32[]{:S(2)}) copy-start(s32[2,16384]{1,0:T(2,128)} %param.7) | copy-start | bytes 393220
  1.4 10.4 %copy-start.1 = (f32[32,1024]{1,0:T(8,128)S(1)}, f32[32,1024]{1,0:T(8,128)}, u32[]{:S(2)}) copy-start(f32[32,1024]{1,0:T(8,128)} %param.5) | copy-start | bytes 393220
  1.4 10.4 %copy-start.4 = (f32[1024]{0:T(1024)S(1)}, f32[1024]{0:T(1024)}, u32[]{:S(2)}) copy-start(f32[1024]{0:T(1024)} %param.6) | copy-start | bytes 12292
  4.5 14.2 %all-to-all-start = ((f32[8,1,2048]{2,1,0:T(1,128)}), f32[8,1,2048]{2,1,0:T(1,128)S(1)}, u32[]{:S(2)}, u32[]{:S(2)}) async-start(f32[8,1,2048]{2,1,0:T(1,128)} %reshape.87), calls=%async_computation | async-start | bytes 131072 | tf_op jit(solution)/shard_map/all_to_all | solution.py:12
  11.7 8.6 %copy-start = (f32[16384]{0:T(1024)S(1)}, f32[16384]{0:T(1024)}, u32[]{:S(2)}) copy-start(f32[16384]{0:T(1024)} %param.8) | copy-start | bytes 196612
  60.8 10.3 %all-to-all-start.2 = ((f32[8,1,2048]{2,1,0:T(1,128)}), f32[8,1,2048]{2,1,0:T(1,128)S(1)}, u32[]{:S(2)}, u32[]{:S(2)}) async-start(f32[8,1,2048]{2,1,0:T(1,128)} %reshape.89), calls=%async_computation.2 | async-start | bytes 131072 | tf_op jit(solution)/shard_map/all_to_all | solution.py:12
  84.7 9.8 %all-to-all-start.3 = ((f32[32,8,2]{0,2,1:T(2,128)}), f32[32,8,2]{0,2,1:T(2,128)S(1)}, u32[]{:S(2)}, u32[]{:S(2)}) async-start(f32[32,8,2]{0,2,1:T(2,128)} %broadcast_in_dim.8), calls=%async_computation.3 | async-start | bytes 16384 | tf_op jit(solution)/shard_map/all_to_all | solution.py:12
  94.7 14.2 %copy-start.2 = (f32[32,1024]{1,0:T(8,128)}, f32[32,1024]{1,0:T(8,128)S(1)}, u32[]{:S(2)}) copy-start(f32[32,1024]{1,0:T(8,128)S(1)} %multiply_add_fusion) | copy-start | bytes 393220

commit v12 on v11

--- a/solution.py
+++ b/solution.py
@@ -105,6 +105,105 @@
     return kernel
 
 
+def front_kernel(local):
+    def kernel(xs_ref, head_ref, tail_ref, w_ref, far_ref, energy_ref, flow_ref, total):
+        step = pl.program_id(0)
+        width, rows = xs_ref.shape
+        xs = split3(xs_ref[...])
+        build = incidence(head_ref[...], tail_ref[...], rows, local)
+        parts = []
+        gap = None
+        for first, size in pieces(rows):
+            ends = build(first, size)
+            parts.append((first, size, ends))
+            term = jnp.dot(xs[:, first:first + size], ends, preferred_element_type=jnp.float32)
+            gap = term if gap is None else gap + term
+        gap = gap[:width] + gap[width:2 * width] + gap[2 * width:]
+        weighted = gap * w_ref[...]
+        energy = jnp.sum(gap * weighted, axis=1, keepdims=True)
+        energy_ref[...] = jnp.where(step == 0, 0.0, energy_ref[...]) + energy
+        flow = split3(weighted)
+        flow_ref[...] = flow
+        dims = (((1,), (1,)), ((), ()))
+        for first, size, ends in parts:
+            if first < local:
+                continue
+            window = total[:, first - local:first - local + size]
+            total[:, first - local:first - local + size] = jnp.where(step == 0, 0.0, window) + lax.dot_general(
+                flow, ends, dims, preferred_element_type=jnp.float32
+            )
+
+        @pl.when(step == pl.num_programs(0) - 1)
+        def _():
+            sums = total[...]
+            far_ref[...] = sums[:width] + sums[width:2 * width] + sums[2 * width:]
+
+    return kernel
+
+
+def back_kernel(rows):
+    def kernel(flow_ref, head_ref, tail_ref, near_ref, total):
+        step = pl.program_id(0)
+        width, local = near_ref.shape
+        build = incidence(head_ref[...], tail_ref[...], rows, local)
+        flow = flow_ref[...]
+        dims = (((1,), (1,)), ((), ()))
+        for first, size in pieces(rows):
+            if first >= local:
+                continue
+            ends = build(first, size)
+            window = total[:, first:first + size]
+            total[:, first:first + size] = jnp.where(step == 0, 0.0, window) + lax.dot_general(
+                flow, ends, dims, preferred_element_type=jnp.float32
+            )
+
+        @pl.when(step == pl.num_programs(0) - 1)
+        def _():
+            sums = total[...]
+            near_ref[...] = sums[:width] + sums[width:2 * width] + sums[2 * width:]
+
+    return kernel
+
+
+def split_pass(extended, head_rows, tail_slots, weights, local):
+    width, rows = extended.shape
+    edges = head_rows.shape[1]
+    tile = edge_tile(rows)
+    edge_spec = pl.BlockSpec((1, tile), lambda i: (0, i))
+    flow_spec = pl.BlockSpec((3 * width, tile), lambda i: (0, i))
+    params = pltpu.CompilerParams(dimension_semantics=("arbitrary",), vmem_limit_bytes=48 * 1024 * 1024)
+    far, energy, flow = pl.pallas_call(
+        front_kernel(local),
+        grid=(edges // tile,),
+        in_specs=[pl.BlockSpec((width, rows), lambda i: (0, 0)), edge_spec, edge_spec, edge_spec],
+        out_specs=(
+            pl.BlockSpec((width, rows - local), lambda i: (0, 0)),
+            pl.BlockSpec((width, 1), lambda i: (0, 0)),
+            flow_spec,
+        ),
+        out_shape=(
+            jax.ShapeDtypeStruct((width, rows - local), jnp.float32),
+            jax.ShapeDtypeStruct((width, 1), jnp.float32),
+            jax.ShapeDtypeStruct((3 * width, edges), jnp.bfloat16),
+        ),
+        scratch_shapes=[pltpu.VMEM((3 * width, rows - local), jnp.float32)],
+        compiler_params=params,
+    )(extended, head_rows, tail_slots, weights)
+
+    def near():
+        return pl.pallas_call(
+            back_kernel(rows),
+            grid=(edges // tile,),
+            in_specs=[flow_spec, edge_spec, edge_spec],
+            out_specs=pl.BlockSpec((width, local), lambda i: (0, 0)),
+            out_shape=jax.ShapeDtypeStruct((width, local), jnp.float32),
+            scratch_shapes=[pltpu.VMEM((3 * width, local), jnp.float32)],
+            compiler_params=params,
+        )(flow, head_rows, tail_slots)
+
+    return far, energy, near
+
+
 def edge_pass(extended, head_rows, tail_slots, weights, mode, local):
     width, rows = extended.shape
     edges = head_rows.shape[1]
@@ -160,15 +259,15 @@
         got = trade(jnp.broadcast_to(own[:, None, :], (width, peers, 2)))
         norm, product = jnp.sum(got, axis=1).T
         return None, norm, product, extended[:, count:]
-    summed, energy = edge_pass(extended, head_rows, tail_slots, weights, "scatter", count)
+    far, energy, near = split_pass(extended, head_rows, tail_slots, weights, count)
     own = jnp.stack([jnp.sum(squares, axis=1), jnp.sum(shift * squares, axis=1) + energy[:, 0]], axis=1)
     sent = jnp.concatenate(
-        [summed[:, count:].reshape(width, peers, cap), jnp.broadcast_to(own[:, None, :], (width, peers, 2))], axis=2
+        [far.reshape(width, peers, cap), jnp.broadcast_to(own[:, None, :], (width, peers, 2))], axis=2
     )
     got = trade(sent)
     returned = got[:, :, :cap].reshape(width, -1)
     norm, product = jnp.sum(got[:, :, cap:], axis=1).T
-    local = summed[:, :count] + jnp.dot(returned, picker(halo_rows, count), precision=lax.Precision.HIGHEST)
+    local = near() + jnp.dot(returned, picker(halo_rows, count), precision=lax.Precision.HIGHEST)
     return shift * field + local, norm, product, extended[:, count:]
 
 

time: 115 us -> 119 us (1.035)
  blocking collectives: 23.8 us -> 13.9 us
  starting transfers between devices: 13.9 us -> 20.6 us
  local copies, waits for them, and re-layouts: 5.81 us -> 9.25 us
  other arithmetic: 2.28 us -> 4.57 us
  Pallas kernels: 43.9 us -> 45.7 us
  waiting for transfers between devices: 19.8 us -> 18 us
    pallas_call x0 -> x2, Pallas kernels: none -> 28.4 us  [the longest x1 16.5 us: split_pass(): pl.pallas_call(front_kernel(local), grid=(edges // tile,), in_specs=[pl.B...]
    pallas_call x3 -> x2, Pallas kernels: 43.9 us -> 17.3 us  [edge_pass(): pl.pallas_call(flow_kernel(mode, local), grid=(edges // tile,), in_specs=...]
    all_to_all x1 -> x0, blocking collectives: 9.91 us -> none  [trade(): lax.all_to_all(blocks, ('vx', 'vy'), split_axis=1, concat_axis=1, tiled=T...]
    all_to_all x3 -> x4, starting transfers between devices: 13.9 us -> 20.6 us  [trade(): lax.all_to_all(blocks, ('vx', 'vy'), split_axis=1, concat_axis=1, tiled=T...]
    all_to_all x3 -> x4, waiting for transfers between devices: 19.8 us -> 18 us  [trade(): lax.all_to_all(blocks, ('vx', 'vy'), split_axis=1, concat_axis=1, tiled=T...]
    reshape x2, local copies, waits for them, and re-layouts: 0.11 us -> 1.67 us  [operate(): far.reshape(width, peers, cap)]
  transfers between devices with their start and end apart: 3 -> 4, of which waited for: 3 -> 3; matrix products, arithmetic and copies ran while one was open for 0% -> 2% of each run, Pallas kernels for 0% -> 10%
where the time goes in v12:
time: 119 us; the launch traced here: 118 us
  Pallas kernels  45.7 us (38%)
  starting transfers between devices  20.6 us (17%)
  waiting for transfers between devices  18 us (15%)
  blocking collectives  13.9 us (12%)
  local copies, waits for them, and re-layouts  9.25 us (8%)
  matrix products  5.15 us (4%)
  other arithmetic  4.57 us (4%)
    all_to_all x4, starting transfers between devices, trade(): lax.all_to_all(blocks, ('vx', 'vy'), split_axis=1, concat_axis=1, tiled=T...  20.6 us
    all_to_all x4, waiting for transfers between devices, trade(): lax.all_to_all(blocks, ('vx', 'vy'), split_axis=1, concat_axis=1, tiled=T...  18 us
    pallas_call x2, Pallas kernels, edge_pass(): pl.pallas_call(flow_kernel(mode, local), grid=(edges // tile,), in_specs=...  17.3 us
    pallas_call x1, Pallas kernels, split_pass(): pl.pallas_call(front_kernel(local), grid=(edges // tile,), in_specs=[pl.B...  16.5 us
    pallas_call x1, Pallas kernels, near(): pl.pallas_call(back_kernel(rows), grid=(edges // tile,), in_specs=[flow_s...  11.9 us
    all_gather x1, blocking collectives, body(): lax.all_gather(extended, 'col', axis=0, tiled=True)  8.63 us
    all_gather x1, blocking collectives, body(): resistance = lax.all_gather(total, 'col', axis=0, tiled=True)  5.25 us
    dot_general x2, matrix products, extend(): jnp.dot(field, picker(halo_rows, field.shape[1]).T, precision=lax.Precisi...  3.23 us
  transfers between devices with their start and end apart: 4, of which 3 were waited for; matrix products, arithmetic and copies ran while one was open for 2% of the time, Pallas kernels for 10%

profile of v12, /device:TPU:0, one launch (start us, length us, event | category | flops | bytes accessed | tf_op | source)
XLA Modules:
  0.0 118.1 jit_solution(3211153043804416568)
XLA Ops:
  0.6 0.0 copy-start.1
  0.6 0.0 copy-start
  0.7 0.8 eq.6
  1.5 2.1 %fusion.7 = f32[32,512]{1,0:T(8,128)S(1)} fusion(f32[32,1024]{1,0:T(8,128)} %param.5, s32[512]{0:T(512)S(1)} %eq.6), kind=kOutput, calls=%fused_computation.8 | convolution fusion | flops 201850880 | bytes 198656 | tf_op jit(solution)/shard_map/dot_general | solution.py:245
  3.5 0.1 reshape.78
  3.7 0.8 reshape.87
  4.4 7.3 %all-to-all-start = ((f32[8,1,2048]{2,1,0:T(1,128)}), f32[8,1,2048]{2,1,0:T(1,128)S(1)}, u32[]{:S(2)}, u32[]{:S(2)}) async-start(f32[8,1,2048]{2,1,0:T(1,128)} %reshape.87), calls=%async_computation | async-start | bytes 131072 | tf_op jit(solution)/shard_map/all_to_all | solution.py:12
  11.7 1.1 fusion.14
  12.8 1.0 multiply_reduce_fusion.3
  13.8 0.1 copy.47
  13.9 0.1 copy.48
  14.0 4.7 %all-to-all-done = f32[8,1,2048]{2,1,0:T(1,128)S(1)} async-done(((f32[8,1,2048]{2,1,0:T(1,128)}), f32[8,1,2048]{2,1,0:T(1,128)S(1)}, u32[]{:S(2)}, u32[]{:S(2)}) %all-to-all-start) | async-done | bytes 65568 | tf_op jit(solution)/shard_map/all_to_all | solution.py:12
  18.7 0.5 broadcast.5
  19.2 0.7 reduce.4
  19.9 0.1 reshape.88
  20.0 0.1 copy.46
  20.1 0.1 reshape.79
  20.2 0.0 copy-done.1
  20.2 0.0 copy-done
  20.2 16.5 %shard_map.68 = (f32[32,512]{1,0:T(8,128)S(1)}, f32[32,1]{1,0:T(8,128)S(1)}, bf16[96,16384]{1,0:T(8,128)(2,1)S(1)}) custom-call(f32[32,1536]{1,0:T(8,128)S(1)} %pad_maximum_fusion.xs_ref, s32[1,16384]{1,0:T(1,128)S(1)} %get-tuple-element.17.head_ref, s32[1,16384]{1,0:T(1,128)S(1)} %get-tuple-element.16.tail_ref, f32[1,16384]{1,0:T(1,128)S(1)} %bitcast.38), custom_call_target="tpu_custom_call" | custom-call | tf_op jit(solution)/shard_map/pallas_call | solution.py:175
  36.7 0.7 reshape.80
  37.4 0.9 copy.49
  38.4 0.1 pad_maximum_fusion.4
  38.5 0.8 pad_maximum_fusion.3
  39.2 0.0 copy-start.4
  39.2 4.1 %all-to-all-start.1 = ((f32[32,8,66]{2,0,1:T(8,128)}), f32[32,8,66]{2,0,1:T(8,128)}, u32[]{:S(2)}, u32[]{:S(2)}) async-start(f32[32,8,66]{2,0,1:T(8,128)} %pad_maximum_fusion.3), calls=%async_computation.1 | async-start | bytes 262144 | tf_op jit(solution)/shard_map/all_to_all | solution.py:12
  43.4 11.9 %shard_map.69 = f32[32,1024]{1,0:T(8,128)S(1)} custom-call(bf16[96,16384]{1,0:T(8,128)(2,1)S(1)} %get-tuple-element.7.flow_ref, s32[1,16384]{1,0:T(1,128)S(1)} %get-tuple-element.17.head_ref, s32[1,16384]{1,0:T(1,128)S(1)} %get-tuple-element.16.tail_ref), custom_call_target="tpu_custom_call" | custom-call | tf_op jit(solution)/shard_map/pallas_call | solution.py:194
  55.3 0.0 all-to-all-done.1
  55.3 1.0 copy.51
  56.3 0.1 reshape.81
  56.4 1.0 slice_reduce_fusion
  57.4 0.0 copy-start.2
  57.4 0.2 slice_reduce_fusion.1
  57.6 0.0 copy-done.4
  57.6 1.9 %multiply_reduce_fusion.2 = (f32[32]{0:T(128)S(1)}, f32[32]{0:T(128)S(1)}, f32[32,1024]{1,0:T(8,128)S(1)}) fusion(f32[1024]{0:T(1024)S(1)} %copy-done.4, f32[32,1024]{1,0:T(8,128)} %param.5, f32[32,1024]{1,0:T(8,128)S(1)} %shard_map.69, f32[32,512]{1,0:T(8,128)S(1)} %reshape.81, s32[512]{0:T(512)S(1)} %eq.6, f32[32]{0:T(128)S(1)} %div.31), kind=kOutput, calls=%fused_computation.20 | convolution fusion | flops 202145728 | bytes 465280 | tf_op jit(solution)/shard_map/dot_general | solution.py:270
  59.5 1.2 fusion
  60.7 0.1 reshape.82
  60.8 0.8 reshape.89
  61.6 5.9 %all-to-all-start.2 = ((f32[8,1,2048]{2,1,0:T(1,128)}), f32[8,1,2048]{2,1,0:T(1,128)S(1)}, u32[]{:S(2)}, u32[]{:S(2)}) async-start(f32[8,1,2048]{2,1,0:T(1,128)} %reshape.89), calls=%async_computation.2 | async-start | bytes 131072 | tf_op jit(solution)/shard_map/all_to_all | solution.py:12
  67.5 0.1 copy.54
  67.6 6.9 %all-to-all-done.2 = f32[8,1,2048]{2,1,0:T(1,128)S(1)} async-done(((f32[8,1,2048]{2,1,0:T(1,128)}), f32[8,1,2048]{2,1,0:T(1,128)S(1)}, u32[]{:S(2)}, u32[]{:S(2)}) %all-to-all-start.2) | async-done | bytes 65568 | tf_op jit(solution)/shard_map/all_to_all | solution.py:12
  74.5 0.7 reduce.5
  75.2 0.1 reshape.90
  75.3 0.1 copy.53
  75.4 0.1 reshape.83
  75.5 11.7 %shard_map.70 = f32[32,1]{1,0:T(8,128)S(1)} custom-call(f32[32,1536]{1,0:T(8,128)S(1)} %pad_maximum_fusion.1.xs_ref, s32[1,16384]{1,0:T(1,128)S(1)} %get-tuple-element.17.head_ref, s32[1,16384]{1,0:T(1,128)S(1)} %get-tuple-element.16.tail_ref, f32[1,16384]{1,0:T(1,128)S(1)} %bitcast.39), custom_call_target="tpu_custom_call" | custom-call | tf_op jit(solution)/shard_map/pallas_call | solution.py:225
  87.2 0.1 copy.55
  87.3 0.6 broadcast_in_dim.8
  87.9 3.3 %all-to-all-start.3 = ((f32[32,8,2]{0,2,1:T(2,128)}), f32[32,8,2]{0,2,1:T(2,128)S(1)}, u32[]{:S(2)}, u32[]{:S(2)}) async-start(f32[32,8,2]{0,2,1:T(2,128)} %broadcast_in_dim.8), calls=%async_computation.3 | async-start | bytes 16384 | tf_op jit(solution)/shard_map/all_to_all | solution.py:12
  91.3 6.4 %all-to-all-done.3 = f32[32,8,2]{0,2,1:T(2,128)S(1)} async-done(((f32[32,8,2]{0,2,1:T(2,128)}), f32[32,8,2]{0,2,1:T(2,128)S(1)}, u32[]{:S(2)}, u32[]{:S(2)}) %all-to-all-start.3) | async-done | bytes 2080 | tf_op jit(solution)/shard_map/all_to_all | solution.py:12
  97.8 0.0 copy-done.2
  97.8 0.1 multiply_add_fusion
  97.9 0.0 copy-start.3
  97.9 0.1 multiply_add_fusion.1
  98.0 8.6 %all_gather.6.xs_ref = f32[128,1536]{1,0:T(8,128)S(1)} all-gather(f32[32,1536]{1,0:T(8,128)S(1)} %pad_maximum_fusion.2), channel_id=1, replica_groups=mesh['vx'=2,'vy'=4,'col'=4] {'col'}, dimensions={0}, use_global_device_ids=true | all-gather | bytes 983040 | tf_op jit(solution)/shard_map/all_gather | solution.py:304
  106.6 5.5 %shard_map.71 = f32[1,4096]{1,0:T(1,128)S(1)} custom-call(f32[128,1536]{1,0:T(8,128)S(1)} %all_gather.6.xs_ref, s32[1,4096]{1,0:T(1,128)S(1)} %get-tuple-element.20.head_ref, s32[1,4096]{1,0:T(1,128)S(1)} %get-tuple-element.19.tail_ref, f32[1,4096]{1,0:T(1,128)S(1)} %bitcast.40), custom_call_target="tpu_custom_call" | custom-call | tf_op jit(solution)/shard_map/pallas_call | solution.py:225
  112.2 5.2 %all-gather = f32[1,16384]{1,0:T(1,128)S(1)} all-gather(f32[1,4096]{1,0:T(1,128)S(1)} %shard_map.71), channel_id=2, replica_groups=mesh['vx'=2,'vy'=4,'col'=4] {'col'}, dimensions={1}, use_global_device_ids=true | all-gather | bytes 81920 | tf_op jit(solution)/shard_map/all_gather | solution.py:305
  117.4 0.6 copy.62
  118.1 0.0 copy-done.3
  (14 shorter events, 0.2 us)
Async XLA Ops:
  0.6 19.5 %copy-start.1 = (f32[32,1024]{1,0:T(8,128)S(1)}, f32[32,1024]{1,0:T(8,128)}, u32[]{:S(2)}) copy-start(f32[32,1024]{1,0:T(8,128)} %param.5) | copy-start | bytes 393220
  0.6 19.5 %copy-start = (f32[16384]{0:T(1024)S(1)}, f32[16384]{0:T(1024)}, u32[]{:S(2)}) copy-start(f32[16384]{0:T(1024)} %param.8) | copy-start | bytes 196612
  4.4 14.2 %all-to-all-start = ((f32[8,1,2048]{2,1,0:T(1,128)}), f32[8,1,2048]{2,1,0:T(1,128)S(1)}, u32[]{:S(2)}, u32[]{:S(2)}) async-start(f32[8,1,2048]{2,1,0:T(1,128)} %reshape.87), calls=%async_computation | async-start | bytes 131072 | tf_op jit(solution)/shard_map/all_to_all | solution.py:12
  39.2 18.4 %copy-start.4 = (f32[1024]{0:T(1024)S(1)}, f32[1024]{0:T(1024)}, u32[]{:S(2)}) copy-start(f32[1024]{0:T(1024)} %param.6) | copy-start | bytes 12292
  39.2 16.0 %all-to-all-start.1 = ((f32[32,8,66]{2,0,1:T(8,128)}), f32[32,8,66]{2,0,1:T(8,128)}, u32[]{:S(2)}, u32[]{:S(2)}) async-start(f32[32,8,66]{2,0,1:T(8,128)} %pad_maximum_fusion.3), calls=%async_computation.1 | async-start | bytes 262144 | tf_op jit(solution)/shard_map/all_to_all | solution.py:12
  57.4 40.4 %copy-start.2 = (f32[32,1024]{1,0:T(8,128)S(1)}, f32[32,1024]{1,0:T(8,128)}, u32[]{:S(2)}) copy-start(f32[32,1024]{1,0:T(8,128)} %param.5) | copy-start | bytes 393220
  61.6 12.9 %all-to-all-start.2 = ((f32[8,1,2048]{2,1,0:T(1,128)}), f32[8,1,2048]{2,1,0:T(1,128)S(1)}, u32[]{:S(2)}, u32[]{:S(2)}) async-start(f32[8,1,2048]{2,1,0:T(1,128)} %reshape.89), calls=%async_computation.2 | async-start | bytes 131072 | tf_op jit(solution)/shard_map/all_to_all | solution.py:12
  87.9 9.8 %all-to-all-start.3 = ((f32[32,8,2]{0,2,1:T(2,128)}), f32[32,8,2]{0,2,1:T(2,128)S(1)}, u32[]{:S(2)}, u32[]{:S(2)}) async-start(f32[32,8,2]{0,2,1:T(2,128)} %broadcast_in_dim.8), calls=%async_computation.3 | async-start | bytes 16384 | tf_op jit(solution)/shard_map/all_to_all | solution.py:12
  97.9 20.2 %copy-start.3 = (f32[32,1024]{1,0:T(8,128)}, f32[32,1024]{1,0:T(8,128)S(1)}, u32[]{:S(2)}) copy-start(f32[32,1024]{1,0:T(8,128)S(1)} %multiply_add_fusion) | copy-start | bytes 393220

commit v13 on v11

--- a/solution.py
+++ b/solution.py
@@ -33,19 +33,23 @@
             return ends.astype(jnp.bfloat16)
 
         return build
-    lane = lax.broadcasted_iota(jnp.int32, (128, tile), 0)
-    low_head = (lane == (head & 127)).astype(jnp.bfloat16)
-    low_tail = (lane == (tail & 127)).astype(jnp.bfloat16)
-    high_head = head >> 7
-    high_tail = tail >> 7
+    lane = lax.broadcasted_iota(jnp.int32, (128, tile), 0).astype(jnp.bfloat16)
+    one = jnp.ones((), jnp.bfloat16)
+    zero = jnp.zeros((), jnp.bfloat16)
+    low_head = jnp.where(lane == (head & 127).astype(jnp.bfloat16), one, zero)
+    low_tail = jnp.where(lane == (tail & 127).astype(jnp.bfloat16), one, zero)
+    count = -(-rows // 128)
+    slots = -(-count // 16) * 16
+    which = lax.broadcasted_iota(jnp.int32, (slots, tile), 0)
+    on_heads = jnp.where(which == (head >> 7), one, zero)
+    off_tails = jnp.where(which == (tail >> 7), -one, zero)
 
     def build(first, size):
         blocks = []
         for block in range(first // 128, (first + size) // 128):
-            off_tail = -(high_tail == block).astype(jnp.bfloat16)
+            off_tail = off_tails[block:block + 1]
             if block * 128 < local:
-                on_head = (high_head == block).astype(jnp.bfloat16)
-                blocks.append(low_head * on_head + low_tail * off_tail)
+                blocks.append(low_head * on_heads[block:block + 1] + low_tail * off_tail)
             else:
                 blocks.append(low_tail * off_tail)
         return jnp.concatenate(blocks, axis=0) if len(blocks) > 1 else blocks[0]

time: 115 us -> 113 us (0.983)
  Pallas kernels: 43.9 us -> 41.7 us
    pallas_call x3, Pallas kernels: 43.9 us -> 41.7 us  [edge_pass(): pl.pallas_call(flow_kernel(mode, local), grid=(edges // tile,), in_specs=...]
where the time goes in v13:
time: 113 us
  Pallas kernels  41.7 us (37%)
  blocking collectives  23.8 us (21%)
  waiting for transfers between devices  19.8 us (18%)
  starting transfers between devices  13.9 us (12%)
  local copies, waits for them, and re-layouts  5.81 us (5%)
  matrix products  4.31 us (4%)
  other arithmetic  2.28 us (2%)
    pallas_call x3, Pallas kernels, edge_pass(): pl.pallas_call(flow_kernel(mode, local), grid=(edges // tile,), in_specs=...  41.7 us
    all_to_all x3, waiting for transfers between devices, trade(): lax.all_to_all(blocks, ('vx', 'vy'), split_axis=1, concat_axis=1, tiled=T...  19.8 us
    all_to_all x3, starting transfers between devices, trade(): lax.all_to_all(blocks, ('vx', 'vy'), split_axis=1, concat_axis=1, tiled=T...  13.9 us
    all_to_all x1, blocking collectives, trade(): lax.all_to_all(blocks, ('vx', 'vy'), split_axis=1, concat_axis=1, tiled=T...  9.91 us
    all_gather x1, blocking collectives, body(): lax.all_gather(extended, 'col', axis=0, tiled=True)  8.63 us
    all_gather x1, blocking collectives, body(): resistance = lax.all_gather(total, 'col', axis=0, tiled=True)  5.25 us
    dot_general x2, matrix products, extend(): jnp.dot(field, picker(halo_rows, field.shape[1]).T, precision=lax.Precisi...  3.29 us
    unnamed x15, local copies, waits for them, and re-layouts  2.34 us
  transfers between devices with their start and end apart: 3, of which 3 were waited for; matrix products, arithmetic and copies ran while one was open for 0% of the time, Pallas kernels for 0%

profile of v13, /device:TPU:0, one launch (start us, length us, event | category | flops | bytes accessed | tf_op | source)
XLA Modules:
  0.0 112.6 jit_solution(7082348299047551683)
XLA Ops:
  0.6 0.0 copy-start.3
  0.6 0.8 eq.6
  1.4 0.0 copy-start.1
  1.4 0.0 copy-start.4
  1.4 2.1 %fusion.7 = f32[32,512]{1,0:T(8,128)S(1)} fusion(f32[32,1024]{1,0:T(8,128)} %param.5, s32[512]{0:T(512)S(1)} %eq.6), kind=kOutput, calls=%fused_computation.8 | convolution fusion | flops 201850880 | bytes 198656 | tf_op jit(solution)/shard_map/dot_general | solution.py:150
  3.6 0.1 reshape.78
  3.7 0.8 reshape.87
  4.5 7.3 %all-to-all-start = ((f32[8,1,2048]{2,1,0:T(1,128)}), f32[8,1,2048]{2,1,0:T(1,128)S(1)}, u32[]{:S(2)}, u32[]{:S(2)}) async-start(f32[8,1,2048]{2,1,0:T(1,128)} %reshape.87), calls=%async_computation | async-start | bytes 131072 | tf_op jit(solution)/shard_map/all_to_all | solution.py:12
  11.7 0.0 copy-done.3
  11.7 0.0 copy-start
  11.8 0.1 fusion.14
  11.9 0.0 copy-done.1
  11.9 0.0 copy-done.4
  11.9 0.1 multiply_reduce_fusion.3
  12.0 0.1 copy.47
  12.1 0.1 copy.48
  12.2 6.5 %all-to-all-done = f32[8,1,2048]{2,1,0:T(1,128)S(1)} async-done(((f32[8,1,2048]{2,1,0:T(1,128)}), f32[8,1,2048]{2,1,0:T(1,128)S(1)}, u32[]{:S(2)}, u32[]{:S(2)}) %all-to-all-start) | async-done | bytes 65568 | tf_op jit(solution)/shard_map/all_to_all | solution.py:12
  18.7 0.5 broadcast.5
  19.2 0.8 reduce.4
  20.0 0.1 reshape.88
  20.1 0.1 copy.46
  20.2 0.1 reshape.79
  20.3 0.0 copy-done
  20.3 25.6 %shard_map.68 = (f32[32,1536]{1,0:T(8,128)S(1)}, f32[32,1]{1,0:T(8,128)S(1)}) custom-call(f32[32,1536]{1,0:T(8,128)S(1)} %pad_maximum_fusion.xs_ref, s32[1,16384]{1,0:T(1,128)S(1)} %get-tuple-element.15.head_ref, s32[1,16384]{1,0:T(1,128)S(1)} %get-tuple-element.14.tail_ref, f32[1,16384]{1,0:T(1,128)S(1)} %bitcast.38), custom_call_target="tpu_custom_call" | custom-call | tf_op jit(solution)/shard_map/pallas_call | solution.py:130
  45.9 0.1 reshape.80
  46.1 0.1 pad_maximum_fusion.4
  46.2 0.1 pad_maximum_fusion.3
  46.3 9.9 %all_to_all.20 = f32[32,8,66]{2,0,1:T(8,128)S(1)} all-to-all(f32[32,8,66]{2,0,1:T(8,128)S(1)} %pad_maximum_fusion.3), channel_id=1, replica_groups=mesh['vx'=2,'vy'=4,'col'=4] {'vx','vy'}, dimensions={1} | all-to-all | bytes 135168 | tf_op jit(solution)/shard_map/all_to_all | solution.py:12
  56.2 0.1 slice_reduce_fusion
  56.3 0.2 slice_reduce_fusion.1
  56.5 0.1 copy.51
  56.6 0.1 reshape.81
  56.7 1.0 multiply_reduce_fusion.2
  57.7 1.2 %fusion = f32[32,512]{1,0:T(8,128)S(1)} fusion(f32[32,1024]{1,0:T(8,128)S(1)} %get-tuple-element.16, s32[512]{0:T(512)S(1)} %eq.6), kind=kOutput, calls=%fused_computation.1 | convolution fusion | flops 201850880 | bytes 198656 | tf_op jit(solution)/shard_map/dot_general | solution.py:150
  58.9 0.1 reshape.82
  59.0 0.8 reshape.89
  59.8 3.4 %all-to-all-start.2 = ((f32[8,1,2048]{2,1,0:T(1,128)}), f32[8,1,2048]{2,1,0:T(1,128)S(1)}, u32[]{:S(2)}, u32[]{:S(2)}) async-start(f32[8,1,2048]{2,1,0:T(1,128)} %reshape.89), calls=%async_computation.2 | async-start | bytes 131072 | tf_op jit(solution)/shard_map/all_to_all | solution.py:12
  63.1 0.1 copy.54
  63.2 6.8 %all-to-all-done.2 = f32[8,1,2048]{2,1,0:T(1,128)S(1)} async-done(((f32[8,1,2048]{2,1,0:T(1,128)}), f32[8,1,2048]{2,1,0:T(1,128)S(1)}, u32[]{:S(2)}, u32[]{:S(2)}) %all-to-all-start.2) | async-done | bytes 65568 | tf_op jit(solution)/shard_map/all_to_all | solution.py:12
  70.0 0.8 reduce.5
  70.9 0.1 reshape.90
  70.9 0.1 copy.53
  71.0 0.1 reshape.83
  71.1 10.8 %shard_map.69 = f32[32,1]{1,0:T(8,128)S(1)} custom-call(f32[32,1536]{1,0:T(8,128)S(1)} %pad_maximum_fusion.1.xs_ref, s32[1,16384]{1,0:T(1,128)S(1)} %get-tuple-element.15.head_ref, s32[1,16384]{1,0:T(1,128)S(1)} %get-tuple-element.14.tail_ref, f32[1,16384]{1,0:T(1,128)S(1)} %bitcast.39), custom_call_target="tpu_custom_call" | custom-call | tf_op jit(solution)/shard_map/pallas_call | solution.py:130
  81.9 0.1 copy.55
  82.0 0.6 broadcast_in_dim.8
  82.6 3.3 %all-to-all-start.3 = ((f32[32,8,2]{0,2,1:T(2,128)}), f32[32,8,2]{0,2,1:T(2,128)S(1)}, u32[]{:S(2)}, u32[]{:S(2)}) async-start(f32[32,8,2]{0,2,1:T(2,128)} %broadcast_in_dim.8), calls=%async_computation.3 | async-start | bytes 16384 | tf_op jit(solution)/shard_map/all_to_all | solution.py:12
  86.0 6.4 %all-to-all-done.3 = f32[32,8,2]{0,2,1:T(2,128)S(1)} async-done(((f32[32,8,2]{0,2,1:T(2,128)}), f32[32,8,2]{0,2,1:T(2,128)S(1)}, u32[]{:S(2)}, u32[]{:S(2)}) %all-to-all-start.3) | async-done | bytes 2080 | tf_op jit(solution)/shard_map/all_to_all | solution.py:12
  92.5 0.1 multiply_add_fusion.1
  92.6 0.1 multiply_add_fusion
  92.7 0.0 copy-start.2
  92.7 8.6 %all_gather.6.xs_ref = f32[128,1536]{1,0:T(8,128)S(1)} all-gather(f32[32,1536]{1,0:T(8,128)S(1)} %pad_maximum_fusion.2), channel_id=1, replica_groups=mesh['vx'=2,'vy'=4,'col'=4] {'col'}, dimensions={0}, use_global_device_ids=true | all-gather | bytes 983040 | tf_op jit(solution)/shard_map/all_gather | solution.py:209
  101.3 5.3 %shard_map.70 = f32[1,4096]{1,0:T(1,128)S(1)} custom-call(f32[128,1536]{1,0:T(8,128)S(1)} %all_gather.6.xs_ref, s32[1,4096]{1,0:T(1,128)S(1)} %get-tuple-element.18.head_ref, s32[1,4096]{1,0:T(1,128)S(1)} %get-tuple-element.17.tail_ref, f32[1,4096]{1,0:T(1,128)S(1)} %bitcast.40), custom_call_target="tpu_custom_call" | custom-call | tf_op jit(solution)/shard_map/pallas_call | solution.py:130
  106.7 0.0 copy-done.2
  106.7 5.2 %all-gather = f32[1,16384]{1,0:T(1,128)S(1)} all-gather(f32[1,4096]{1,0:T(1,128)S(1)} %shard_map.70), channel_id=2, replica_groups=mesh['vx'=2,'vy'=4,'col'=4] {'col'}, dimensions={1}, use_global_device_ids=true | all-gather | bytes 81920 | tf_op jit(solution)/shard_map/all_gather | solution.py:210
  111.9 0.6 copy.62
  (16 shorter events, 0.2 us)
Async XLA Ops:
  0.6 11.1 %copy-start.3 = (s32[2,16384]{1,0:T(2,128)S(1)}, s32[2,16384]{1,0:T(2,128)}, u32[]{:S(2)}) copy-start(s32[2,16384]{1,0:T(2,128)} %param.7) | copy-start | bytes 393220
  1.4 10.4 %copy-start.1 = (f32[32,1024]{1,0:T(8,128)S(1)}, f32[32,1024]{1,0:T(8,128)}, u32[]{:S(2)}) copy-start(f32[32,1024]{1,0:T(8,128)} %param.5) | copy-start | bytes 393220
  1.4 10.4 %copy-start.4 = (f32[1024]{0:T(1024)S(1)}, f32[1024]{0:T(1024)}, u32[]{:S(2)}) copy-start(f32[1024]{0:T(1024)} %param.6) | copy-start | bytes 12292
  4.5 14.2 %all-to-all-start = ((f32[8,1,2048]{2,1,0:T(1,128)}), f32[8,1,2048]{2,1,0:T(1,128)S(1)}, u32[]{:S(2)}, u32[]{:S(2)}) async-start(f32[8,1,2048]{2,1,0:T(1,128)} %reshape.87), calls=%async_computation | async-start | bytes 131072 | tf_op jit(solution)/shard_map/all_to_all | solution.py:12
  11.7 8.6 %copy-start = (f32[16384]{0:T(1024)S(1)}, f32[16384]{0:T(1024)}, u32[]{:S(2)}) copy-start(f32[16384]{0:T(1024)} %param.8) | copy-start | bytes 196612
  59.8 10.3 %all-to-all-start.2 = ((f32[8,1,2048]{2,1,0:T(1,128)}), f32[8,1,2048]{2,1,0:T(1,128)S(1)}, u32[]{:S(2)}, u32[]{:S(2)}) async-start(f32[8,1,2048]{2,1,0:T(1,128)} %reshape.89), calls=%async_computation.2 | async-start | bytes 131072 | tf_op jit(solution)/shard_map/all_to_all | solution.py:12
  82.6 9.8 %all-to-all-start.3 = ((f32[32,8,2]{0,2,1:T(2,128)}), f32[32,8,2]{0,2,1:T(2,128)S(1)}, u32[]{:S(2)}, u32[]{:S(2)}) async-start(f32[32,8,2]{0,2,1:T(2,128)} %broadcast_in_dim.8), calls=%async_computation.3 | async-start | bytes 16384 | tf_op jit(solution)/shard_map/all_to_all | solution.py:12
  92.7 14.0 %copy-start.2 = (f32[32,1024]{1,0:T(8,128)}, f32[32,1024]{1,0:T(8,128)S(1)}, u32[]{:S(2)}) copy-start(f32[32,1024]{1,0:T(8,128)S(1)} %multiply_add_fusion) | copy-start | bytes 393220

commit v14 on v13

--- a/solution.py
+++ b/solution.py
@@ -141,14 +141,14 @@
 
 
 def picker(halo_rows, count):
-    flat = halo_rows.reshape(-1, 1)
-    return (flat == lax.broadcasted_iota(jnp.int32, (flat.shape[0], count), 1)).astype(jnp.float32)
+    peers, cap = halo_rows.shape
+    index = lax.broadcasted_iota(jnp.int32, (peers, cap, count), 2)
+    return (halo_rows[:, :, None] == index).astype(jnp.float32)
 
 
 def extend(field, halo_rows):
-    peers, cap = halo_rows.shape
-    chosen = jnp.dot(field, picker(halo_rows, field.shape[1]).T, precision=lax.Precision.HIGHEST)
-    mirrored = trade(chosen.reshape(field.shape[0], peers, cap))
+    chosen = jnp.einsum("cv,psv->cps", field, picker(halo_rows, field.shape[1]), precision=lax.Precision.HIGHEST)
+    mirrored = trade(chosen)
     return jnp.concatenate([field, mirrored.reshape(field.shape[0], -1)], axis=1)
 
 
@@ -170,9 +170,11 @@
         [summed[:, count:].reshape(width, peers, cap), jnp.broadcast_to(own[:, None, :], (width, peers, 2))], axis=2
     )
     got = trade(sent)
-    returned = got[:, :, :cap].reshape(width, -1)
+    returned = got[:, :, :cap]
     norm, product = jnp.sum(got[:, :, cap:], axis=1).T
-    local = summed[:, :count] + jnp.dot(returned, picker(halo_rows, count), precision=lax.Precision.HIGHEST)
+    local = summed[:, :count] + jnp.einsum(
+        "cps,psv->cv", returned, picker(halo_rows, count), precision=lax.Precision.HIGHEST
+    )
     return shift * field + local, norm, product, extended[:, count:]
 
 

time: 113 us -> 113 us (level)
  local copies, waits for them, and re-layouts: 5.81 us -> 4.6 us
    unnamed x15 -> x17, local copies, waits for them, and re-layouts: 2.34 us -> 2.35 us
where the time goes in v14:
time: 113 us; the launch traced here: 112 us
  Pallas kernels  41.7 us (37%)
  blocking collectives  23.8 us (21%)
  waiting for transfers between devices  19.8 us (18%)
  starting transfers between devices  13.9 us (12%)
  matrix products  5.16 us (5%)
  local copies, waits for them, and re-layouts  4.6 us (4%)
  other arithmetic  2.28 us (2%)
    pallas_call x3, Pallas kernels, edge_pass(): pl.pallas_call(flow_kernel(mode, local), grid=(edges // tile,), in_specs=...  41.7 us
    all_to_all x3, waiting for transfers between devices, trade(): lax.all_to_all(blocks, ('vx', 'vy'), split_axis=1, concat_axis=1, tiled=T...  19.8 us
    all_to_all x3, starting transfers between devices, trade(): lax.all_to_all(blocks, ('vx', 'vy'), split_axis=1, concat_axis=1, tiled=T...  13.9 us
    all_to_all x1, blocking collectives, trade(): lax.all_to_all(blocks, ('vx', 'vy'), split_axis=1, concat_axis=1, tiled=T...  9.91 us
    all_gather x1, blocking collectives, body(): lax.all_gather(extended, 'col', axis=0, tiled=True)  8.63 us
    all_gather x1, blocking collectives, body(): resistance = lax.all_gather(total, 'col', axis=0, tiled=True)  5.25 us
    dot_general x2, matrix products, extend(): jnp.einsum('cv,psv->cps', field, picker(halo_rows, field.shape[1]), preci...  4.12 us
    unnamed x17, local copies, waits for them, and re-layouts  2.35 us
  transfers between devices with their start and end apart: 3, of which 3 were waited for; matrix products, arithmetic and copies ran while one was open for 0% of the time, Pallas kernels for 0%

profile of v14, /device:TPU:0, one launch (start us, length us, event | category | flops | bytes accessed | tf_op | source)
XLA Modules:
  0.0 112.2 jit_solution(1818240326681042066)
XLA Ops:
  0.6 0.0 copy-start.1
  0.6 0.0 copy-start.3
  0.6 0.0 copy-start.4
  0.7 2.6 %fusion.19 = f32[8,32,64]{2,1,0:T(8,128)S(1)} fusion(f32[32,1024]{1,0:T(8,128)} %param.5, s32[8,64]{1,0:T(8,128)} %param.9), kind=kOutput, calls=%fused_computation.40 | convolution fusion | flops 201850880 | bytes 198656 | tf_op jit(solution)/shard_map/cv,psv->cps/dot_general | solution.py:150
  3.2 0.8 reshape.75
  4.0 7.3 %all-to-all-start = ((f32[8,1,2048]{2,1,0:T(1,128)}), f32[8,1,2048]{2,1,0:T(1,128)S(1)}, u32[]{:S(2)}, u32[]{:S(2)}) async-start(f32[8,1,2048]{2,1,0:T(1,128)} %reshape.75), calls=%async_computation | async-start | bytes 131072 | tf_op jit(solution)/shard_map/all_to_all | solution.py:12
  11.2 0.0 copy-done.3
  11.2 0.0 copy-start
  11.3 0.1 fusion.18
  11.4 0.0 copy-done.1
  11.4 0.0 copy-done.4
  11.4 0.1 multiply_reduce_fusion.3
  11.5 0.1 copy.38
  11.6 0.1 copy.39
  11.7 6.5 %all-to-all-done = f32[8,1,2048]{2,1,0:T(1,128)S(1)} async-done(((f32[8,1,2048]{2,1,0:T(1,128)}), f32[8,1,2048]{2,1,0:T(1,128)S(1)}, u32[]{:S(2)}, u32[]{:S(2)}) %all-to-all-start) | async-done | bytes 65568 | tf_op jit(solution)/shard_map/all_to_all | solution.py:12
  18.2 0.5 broadcast.6
  18.7 0.8 reduce.4
  19.5 0.1 reshape.76
  19.6 0.1 copy.37
  19.7 0.1 reshape.66
  19.8 0.0 copy-done
  19.8 25.6 %shard_map.68 = (f32[32,1536]{1,0:T(8,128)S(1)}, f32[32,1]{1,0:T(8,128)S(1)}) custom-call(f32[32,1536]{1,0:T(8,128)S(1)} %pad_maximum_fusion.xs_ref, s32[1,16384]{1,0:T(1,128)S(1)} %get-tuple-element.15.head_ref, s32[1,16384]{1,0:T(1,128)S(1)} %get-tuple-element.14.tail_ref, f32[1,16384]{1,0:T(1,128)S(1)} %bitcast.54), custom_call_target="tpu_custom_call" | custom-call | tf_op jit(solution)/shard_map/pallas_call | solution.py:130
  45.4 0.0 copy-start.5
  45.5 0.1 reshape.67
  45.6 0.1 pad_maximum_fusion.4
  45.7 0.1 pad_maximum_fusion.3
  45.8 9.9 %all_to_all.20 = f32[32,8,66]{2,0,1:T(8,128)S(1)} all-to-all(f32[32,8,66]{2,0,1:T(8,128)S(1)} %pad_maximum_fusion.3), channel_id=1, replica_groups=mesh['vx'=2,'vy'=4,'col'=4] {'vx','vy'}, dimensions={1} | all-to-all | bytes 135168 | tf_op jit(solution)/shard_map/all_to_all | solution.py:12
  55.7 0.1 slice_reduce_fusion
  55.8 0.2 slice_reduce_fusion.1
  56.0 0.0 copy-done.5
  56.0 1.0 multiply_reduce_fusion.2
  57.1 1.6 %fusion.22 = f32[8,32,64]{2,1,0:T(8,128)S(1)} fusion(s32[8,64]{1,0:T(8,128)S(1)} %copy-done.5, f32[32,1024]{1,0:T(8,128)S(1)} %get-tuple-element.16), kind=kOutput, calls=%fused_computation.41 | convolution fusion | flops 201850880 | bytes 198656 | tf_op jit(solution)/shard_map/cv,psv->cps/dot_general | solution.py:150
  58.6 0.8 reshape.77
  59.4 3.4 %all-to-all-start.2 = ((f32[8,1,2048]{2,1,0:T(1,128)}), f32[8,1,2048]{2,1,0:T(1,128)S(1)}, u32[]{:S(2)}, u32[]{:S(2)}) async-start(f32[8,1,2048]{2,1,0:T(1,128)} %reshape.77), calls=%async_computation.2 | async-start | bytes 131072 | tf_op jit(solution)/shard_map/all_to_all | solution.py:12
  62.7 0.1 copy.42
  62.8 6.8 %all-to-all-done.2 = f32[8,1,2048]{2,1,0:T(1,128)S(1)} async-done(((f32[8,1,2048]{2,1,0:T(1,128)}), f32[8,1,2048]{2,1,0:T(1,128)S(1)}, u32[]{:S(2)}, u32[]{:S(2)}) %all-to-all-start.2) | async-done | bytes 65568 | tf_op jit(solution)/shard_map/all_to_all | solution.py:12
  69.7 0.8 reduce.5
  70.5 0.1 reshape.78
  70.6 0.1 copy.41
  70.6 0.1 reshape.68
  70.8 10.8 %shard_map.69 = f32[32,1]{1,0:T(8,128)S(1)} custom-call(f32[32,1536]{1,0:T(8,128)S(1)} %pad_maximum_fusion.1.xs_ref, s32[1,16384]{1,0:T(1,128)S(1)} %get-tuple-element.15.head_ref, s32[1,16384]{1,0:T(1,128)S(1)} %get-tuple-element.14.tail_ref, f32[1,16384]{1,0:T(1,128)S(1)} %bitcast.55), custom_call_target="tpu_custom_call" | custom-call | tf_op jit(solution)/shard_map/pallas_call | solution.py:130
  81.6 0.1 copy.43
  81.7 0.6 broadcast_in_dim.8
  82.3 3.3 %all-to-all-start.3 = ((f32[32,8,2]{0,2,1:T(2,128)}), f32[32,8,2]{0,2,1:T(2,128)S(1)}, u32[]{:S(2)}, u32[]{:S(2)}) async-start(f32[32,8,2]{0,2,1:T(2,128)} %broadcast_in_dim.8), calls=%async_computation.3 | async-start | bytes 16384 | tf_op jit(solution)/shard_map/all_to_all | solution.py:12
  85.6 6.4 %all-to-all-done.3 = f32[32,8,2]{0,2,1:T(2,128)S(1)} async-done(((f32[32,8,2]{0,2,1:T(2,128)}), f32[32,8,2]{0,2,1:T(2,128)S(1)}, u32[]{:S(2)}, u32[]{:S(2)}) %all-to-all-start.3) | async-done | bytes 2080 | tf_op jit(solution)/shard_map/all_to_all | solution.py:12
  92.1 0.1 multiply_add_fusion.1
  92.2 0.1 multiply_add_fusion
  92.3 0.0 copy-start.2
  92.3 8.6 %all_gather.6.xs_ref = f32[128,1536]{1,0:T(8,128)S(1)} all-gather(f32[32,1536]{1,0:T(8,128)S(1)} %pad_maximum_fusion.2), channel_id=1, replica_groups=mesh['vx'=2,'vy'=4,'col'=4] {'col'}, dimensions={0}, use_global_device_ids=true | all-gather | bytes 983040 | tf_op jit(solution)/shard_map/all_gather | solution.py:211
  101.0 5.3 %shard_map.70 = f32[1,4096]{1,0:T(1,128)S(1)} custom-call(f32[128,1536]{1,0:T(8,128)S(1)} %all_gather.6.xs_ref, s32[1,4096]{1,0:T(1,128)S(1)} %get-tuple-element.18.head_ref, s32[1,4096]{1,0:T(1,128)S(1)} %get-tuple-element.17.tail_ref, f32[1,4096]{1,0:T(1,128)S(1)} %bitcast.56), custom_call_target="tpu_custom_call" | custom-call | tf_op jit(solution)/shard_map/pallas_call | solution.py:130
  106.3 0.0 copy-done.2
  106.3 5.2 %all-gather = f32[1,16384]{1,0:T(1,128)S(1)} all-gather(f32[1,4096]{1,0:T(1,128)S(1)} %shard_map.70), channel_id=2, replica_groups=mesh['vx'=2,'vy'=4,'col'=4] {'col'}, dimensions={1}, use_global_device_ids=true | all-gather | bytes 81920 | tf_op jit(solution)/shard_map/all_gather | solution.py:212
  111.5 0.6 copy.45
  (14 shorter events, 0.2 us)
Async XLA Ops:
  0.6 10.7 %copy-start.1 = (f32[32,1024]{1,0:T(8,128)S(1)}, f32[32,1024]{1,0:T(8,128)}, u32[]{:S(2)}) copy-start(f32[32,1024]{1,0:T(8,128)} %param.5) | copy-start | bytes 393220
  0.6 10.6 %copy-start.3 = (s32[2,16384]{1,0:T(2,128)S(1)}, s32[2,16384]{1,0:T(2,128)}, u32[]{:S(2)}) copy-start(s32[2,16384]{1,0:T(2,128)} %param.7) | copy-start | bytes 393220
  0.6 10.7 %copy-start.4 = (f32[1024]{0:T(1024)S(1)}, f32[1024]{0:T(1024)}, u32[]{:S(2)}) copy-start(f32[1024]{0:T(1024)} %param.6) | copy-start | bytes 12292
  4.0 14.2 %all-to-all-start = ((f32[8,1,2048]{2,1,0:T(1,128)}), f32[8,1,2048]{2,1,0:T(1,128)S(1)}, u32[]{:S(2)}, u32[]{:S(2)}) async-start(f32[8,1,2048]{2,1,0:T(1,128)} %reshape.75), calls=%async_computation | async-start | bytes 131072 | tf_op jit(solution)/shard_map/all_to_all | solution.py:12
  11.2 8.6 %copy-start = (f32[16384]{0:T(1024)S(1)}, f32[16384]{0:T(1024)}, u32[]{:S(2)}) copy-start(f32[16384]{0:T(1024)} %param.8) | copy-start | bytes 196612
  45.4 10.6 %copy-start.5 = (s32[8,64]{1,0:T(8,128)S(1)}, s32[8,64]{1,0:T(8,128)}, u32[]{:S(2)}) copy-start(s32[8,64]{1,0:T(8,128)} %param.9) | copy-start | bytes 6148
  59.4 10.3 %all-to-all-start.2 = ((f32[8,1,2048]{2,1,0:T(1,128)}), f32[8,1,2048]{2,1,0:T(1,128)S(1)}, u32[]{:S(2)}, u32[]{:S(2)}) async-start(f32[8,1,2048]{2,1,0:T(1,128)} %reshape.77), calls=%async_computation.2 | async-start | bytes 131072 | tf_op jit(solution)/shard_map/all_to_all | solution.py:12
  82.3 9.8 %all-to-all-start.3 = ((f32[32,8,2]{0,2,1:T(2,128)}), f32[32,8,2]{0,2,1:T(2,128)S(1)}, u32[]{:S(2)}, u32[]{:S(2)}) async-start(f32[32,8,2]{0,2,1:T(2,128)} %broadcast_in_dim.8), calls=%async_computation.3 | async-start | bytes 16384 | tf_op jit(solution)/shard_map/all_to_all | solution.py:12
  92.3 14.0 %copy-start.2 = (f32[32,1024]{1,0:T(8,128)}, f32[32,1024]{1,0:T(8,128)S(1)}, u32[]{:S(2)}) copy-start(f32[32,1024]{1,0:T(8,128)S(1)} %multiply_add_fusion) | copy-start | bytes 393220

commit v15 on v14

--- a/solution.py
+++ b/solution.py
@@ -143,11 +143,25 @@
 def picker(halo_rows, count):
     peers, cap = halo_rows.shape
     index = lax.broadcasted_iota(jnp.int32, (peers, cap, count), 2)
-    return (halo_rows[:, :, None] == index).astype(jnp.float32)
+    return (halo_rows[:, :, None] == index).astype(jnp.bfloat16)
+
+
+def parts3(values):
+    first = lax.reduce_precision(values, exponent_bits=8, mantissa_bits=7)
+    rest = values - first
+    second = lax.reduce_precision(rest, exponent_bits=8, mantissa_bits=7)
+    third = rest - second
+    return jnp.concatenate([first, second, third], axis=0).astype(jnp.bfloat16)
+
+
+def pick(pattern, values, choice):
+    width = values.shape[0]
+    out = jnp.einsum(pattern, parts3(values), choice, preferred_element_type=jnp.float32)
+    return out[:width] + out[width:2 * width] + out[2 * width:]
 
 
 def extend(field, halo_rows):
-    chosen = jnp.einsum("cv,psv->cps", field, picker(halo_rows, field.shape[1]), precision=lax.Precision.HIGHEST)
+    chosen = pick("cv,psv->cps", field, picker(halo_rows, field.shape[1]))
     mirrored = trade(chosen)
     return jnp.concatenate([field, mirrored.reshape(field.shape[0], -1)], axis=1)
 
@@ -172,9 +186,7 @@
     got = trade(sent)
     returned = got[:, :, :cap]
     norm, product = jnp.sum(got[:, :, cap:], axis=1).T
-    local = summed[:, :count] + jnp.einsum(
-        "cps,psv->cv", returned, picker(halo_rows, count), precision=lax.Precision.HIGHEST
-    )
+    local = summed[:, :count] + pick("cps,psv->cv", returned, picker(halo_rows, count))
     return shift * field + local, norm, product, extended[:, count:]
 
 

time: 113 us -> 112 us (level)
  matrix products: 5.16 us -> 2.3 us
  other arithmetic: 2.28 us -> 4 us
    dot_general x3, matrix products: 5.16 us -> 2.3 us  [pick(): jnp.einsum(pattern, parts3(values), choice, preferred_element_type=jnp.fl...]
    another operation x0 -> x4, other arithmetic: none -> 1.4 us
where the time goes in v15:
time: 112 us
  Pallas kernels  41.7 us (37%)
  blocking collectives  23.8 us (21%)
  waiting for transfers between devices  20 us (18%)
  starting transfers between devices  14.1 us (13%)
  local copies, waits for them, and re-layouts  4.9 us (4%)
  other arithmetic  4 us (4%)
  matrix products  2.3 us (2%)
    pallas_call x3, Pallas kernels, edge_pass(): pl.pallas_call(flow_kernel(mode, local), grid=(edges // tile,), in_specs=...  41.7 us
    all_to_all x3, waiting for transfers between devices, trade(): lax.all_to_all(blocks, ('vx', 'vy'), split_axis=1, concat_axis=1, tiled=T...  20 us
    all_to_all x3, starting transfers between devices, trade(): lax.all_to_all(blocks, ('vx', 'vy'), split_axis=1, concat_axis=1, tiled=T...  14.1 us
    all_to_all x1, blocking collectives, trade(): lax.all_to_all(blocks, ('vx', 'vy'), split_axis=1, concat_axis=1, tiled=T...  9.91 us
    all_gather x1, blocking collectives, body(): lax.all_gather(extended, 'col', axis=0, tiled=True)  8.63 us
    all_gather x1, blocking collectives, body(): resistance = lax.all_gather(total, 'col', axis=0, tiled=True)  5.25 us
    unnamed x17, local copies, waits for them, and re-layouts  2.42 us
    dot_general x3, matrix products, pick(): jnp.einsum(pattern, parts3(values), choice, preferred_element_type=jnp.fl...  2.3 us
  transfers between devices with their start and end apart: 3, of which 3 were waited for; matrix products, arithmetic and copies ran while one was open for 0% of the time, Pallas kernels for 0%

profile of v15, /device:TPU:0, one launch (start us, length us, event | category | flops | bytes accessed | tf_op | source)
XLA Modules:
  0.0 111.7 jit_solution(5480415668132746033)
XLA Ops:
  0.6 1.1 reduce-precision_convert_fusion.5
  1.7 1.2 %fusion.2 = f32[96,8,64]{0,2,1:T(8,128)S(1)} fusion(s32[8,64]{1,0:T(8,128)} %param.9, bf16[32,1024]{1,0:T(8,128)(2,1)S(1)} %get-tuple-element.26, bf16[32,1024]{1,0:T(8,128)(2,1)S(1)} %get-tuple-element.29, bf16[32,1024]{1,0:T(8,128)(2,1)S(1)} %get-tuple-element.25), kind=kOutput, calls=%fused_computation.3 | convolution fusion | flops 101777408 | bytes 395264 | tf_op jit(solution)/shard_map/cv,psv->cps/dot_general | solution.py:159
  2.9 0.0 copy-start.3
  2.9 0.2 slice_add_fusion.2
  3.1 0.1 copy.58
  3.2 0.0 copy-start.1
  3.2 0.8 reshape.75
  4.0 0.0 copy-start
  4.0 7.4 %all-to-all-start = ((f32[8,1,2048]{2,1,0:T(1,128)}), f32[8,1,2048]{2,1,0:T(1,128)S(1)}, u32[]{:S(2)}, u32[]{:S(2)}) async-start(f32[8,1,2048]{2,1,0:T(1,128)} %reshape.75), calls=%async_computation | async-start | bytes 131072 | tf_op jit(solution)/shard_map/all_to_all | solution.py:12
  11.4 0.0 copy-done.3
  11.4 0.1 fusion.29
  11.5 0.1 copy.60
  11.6 0.1 copy.61
  11.7 6.7 %all-to-all-done = f32[8,1,2048]{2,1,0:T(1,128)S(1)} async-done(((f32[8,1,2048]{2,1,0:T(1,128)}), f32[8,1,2048]{2,1,0:T(1,128)S(1)}, u32[]{:S(2)}, u32[]{:S(2)}) %all-to-all-start) | async-done | bytes 65568 | tf_op jit(solution)/shard_map/all_to_all | solution.py:12
  18.4 0.5 broadcast.6
  18.9 0.8 reduce.4
  19.7 0.1 reshape.76
  19.8 0.1 copy.59
  19.9 0.1 reshape.66
  20.0 0.0 copy-done.1
  20.0 0.0 copy-done
  20.0 25.6 %shard_map.68 = (f32[32,1536]{1,0:T(8,128)S(1)}, f32[32,1]{1,0:T(8,128)S(1)}) custom-call(f32[32,1536]{1,0:T(8,128)S(1)} %pad_maximum_fusion.xs_ref, s32[1,16384]{1,0:T(1,128)S(1)} %get-tuple-element.24.head_ref, s32[1,16384]{1,0:T(1,128)S(1)} %get-tuple-element.23.tail_ref, f32[1,16384]{1,0:T(1,128)S(1)} %bitcast.37), custom_call_target="tpu_custom_call" | custom-call | tf_op jit(solution)/shard_map/pallas_call | solution.py:130
  45.6 0.1 reshape.67
  45.7 0.1 pad_maximum_fusion.5
  45.8 0.1 pad_maximum_fusion.4
  45.9 0.0 copy-start.5
  45.9 9.9 %all_to_all.20 = f32[32,8,66]{2,0,1:T(8,128)S(1)} all-to-all(f32[32,8,66]{2,0,1:T(8,128)S(1)} %copy.62), channel_id=1, replica_groups=mesh['vx'=2,'vy'=4,'col'=4] {'vx','vy'}, dimensions={1} | all-to-all | bytes 135168 | tf_op jit(solution)/shard_map/all_to_all | solution.py:12
  55.9 0.1 slice_reduce_fusion
  56.0 0.2 slice_reduce_fusion.1
  56.1 0.1 reduce-precision_convert_fusion.3
  56.3 0.0 copy-done.5
  56.3 0.0 copy-start.4
  56.3 0.6 fusion.3
  57.0 0.1 copy-done.4
  57.0 0.1 reduce-precision_convert_fusion.1
  57.1 0.2 reduce-precision_convert_fusion
  57.3 0.5 fusion
  57.8 0.2 slice_add_fusion
  58.0 0.1 copy.65
  58.1 0.8 reshape.77
  58.9 3.4 %all-to-all-start.2 = ((f32[8,1,2048]{2,1,0:T(1,128)}), f32[8,1,2048]{2,1,0:T(1,128)S(1)}, u32[]{:S(2)}, u32[]{:S(2)}) async-start(f32[8,1,2048]{2,1,0:T(1,128)} %reshape.77), calls=%async_computation.2 | async-start | bytes 131072 | tf_op jit(solution)/shard_map/all_to_all | solution.py:12
  62.2 0.1 copy.67
  62.3 6.8 %all-to-all-done.2 = f32[8,1,2048]{2,1,0:T(1,128)S(1)} async-done(((f32[8,1,2048]{2,1,0:T(1,128)}), f32[8,1,2048]{2,1,0:T(1,128)S(1)}, u32[]{:S(2)}, u32[]{:S(2)}) %all-to-all-start.2) | async-done | bytes 65568 | tf_op jit(solution)/shard_map/all_to_all | solution.py:12
  69.1 0.8 reduce.5
  70.0 0.1 reshape.78
  70.0 0.1 copy.66
  70.1 0.1 reshape.68
  70.2 10.8 %shard_map.69 = f32[32,1]{1,0:T(8,128)S(1)} custom-call(f32[32,1536]{1,0:T(8,128)S(1)} %pad_maximum_fusion.2.xs_ref, s32[1,16384]{1,0:T(1,128)S(1)} %get-tuple-element.24.head_ref, s32[1,16384]{1,0:T(1,128)S(1)} %get-tuple-element.23.tail_ref, f32[1,16384]{1,0:T(1,128)S(1)} %bitcast.38), custom_call_target="tpu_custom_call" | custom-call | tf_op jit(solution)/shard_map/pallas_call | solution.py:130
  81.0 0.1 copy.68
  81.1 0.6 broadcast_in_dim.8
  81.7 3.3 %all-to-all-start.3 = ((f32[32,8,2]{0,2,1:T(2,128)}), f32[32,8,2]{0,2,1:T(2,128)S(1)}, u32[]{:S(2)}, u32[]{:S(2)}) async-start(f32[32,8,2]{0,2,1:T(2,128)} %broadcast_in_dim.8), calls=%async_computation.3 | async-start | bytes 16384 | tf_op jit(solution)/shard_map/all_to_all | solution.py:12
  85.1 6.4 %all-to-all-done.3 = f32[32,8,2]{0,2,1:T(2,128)S(1)} async-done(((f32[32,8,2]{0,2,1:T(2,128)}), f32[32,8,2]{0,2,1:T(2,128)S(1)}, u32[]{:S(2)}, u32[]{:S(2)}) %all-to-all-start.3) | async-done | bytes 2080 | tf_op jit(solution)/shard_map/all_to_all | solution.py:12
  91.6 0.1 multiply_add_fusion.1
  91.7 0.1 multiply_add_fusion
  91.8 0.0 copy-start.2
  91.8 8.6 %all_gather.6.xs_ref = f32[128,1536]{1,0:T(8,128)S(1)} all-gather(f32[32,1536]{1,0:T(8,128)S(1)} %pad_maximum_fusion.3), channel_id=1, replica_groups=mesh['vx'=2,'vy'=4,'col'=4] {'col'}, dimensions={0}, use_global_device_ids=true | all-gather | bytes 983040 | tf_op jit(solution)/shard_map/all_gather | solution.py:223
  100.4 5.3 %shard_map.70 = f32[1,4096]{1,0:T(1,128)S(1)} custom-call(f32[128,1536]{1,0:T(8,128)S(1)} %all_gather.6.xs_ref, s32[1,4096]{1,0:T(1,128)S(1)} %get-tuple-element.31.head_ref, s32[1,4096]{1,0:T(1,128)S(1)} %get-tuple-element.30.tail_ref, f32[1,4096]{1,0:T(1,128)S(1)} %bitcast.39), custom_call_target="tpu_custom_call" | custom-call | tf_op jit(solution)/shard_map/pallas_call | solution.py:130
  105.8 0.0 copy-done.2
  105.8 5.2 %all-gather = f32[1,16384]{1,0:T(1,128)S(1)} all-gather(f32[1,4096]{1,0:T(1,128)S(1)} %shard_map.70), channel_id=2, replica_groups=mesh['vx'=2,'vy'=4,'col'=4] {'col'}, dimensions={1}, use_global_device_ids=true | all-gather | bytes 81920 | tf_op jit(solution)/shard_map/all_gather | solution.py:224
  111.0 0.6 copy.79
  (15 shorter events, 0.2 us)
Async XLA Ops:
  2.9 8.5 %copy-start.3 = (s32[2,16384]{1,0:T(2,128)S(1)}, s32[2,16384]{1,0:T(2,128)}, u32[]{:S(2)}) copy-start(s32[2,16384]{1,0:T(2,128)} %param.7) | copy-start | bytes 393220
  3.2 16.7 %copy-start.1 = (f32[32,1024]{1,0:T(8,128)S(1)}, f32[32,1024]{1,0:T(8,128)}, u32[]{:S(2)}) copy-start(f32[32,1024]{1,0:T(8,128)} %param.5) | copy-start | bytes 393220
  4.0 16.0 %copy-start = (f32[16384]{0:T(1024)S(1)}, f32[16384]{0:T(1024)}, u32[]{:S(2)}) copy-start(f32[16384]{0:T(1024)} %param.8) | copy-start | bytes 196612
  4.0 14.4 %all-to-all-start = ((f32[8,1,2048]{2,1,0:T(1,128)}), f32[8,1,2048]{2,1,0:T(1,128)S(1)}, u32[]{:S(2)}, u32[]{:S(2)}) async-start(f32[8,1,2048]{2,1,0:T(1,128)} %reshape.75), calls=%async_computation | async-start | bytes 131072 | tf_op jit(solution)/shard_map/all_to_all | solution.py:12
  45.9 10.4 %copy-start.5 = (s32[8,64]{1,0:T(8,128)S(1)}, s32[8,64]{1,0:T(8,128)}, u32[]{:S(2)}) copy-start(s32[8,64]{1,0:T(8,128)} %param.9) | copy-start | bytes 6148
  56.3 0.7 copy-start.4
  58.9 10.3 %all-to-all-start.2 = ((f32[8,1,2048]{2,1,0:T(1,128)}), f32[8,1,2048]{2,1,0:T(1,128)S(1)}, u32[]{:S(2)}, u32[]{:S(2)}) async-start(f32[8,1,2048]{2,1,0:T(1,128)} %reshape.77), calls=%async_computation.2 | async-start | bytes 131072 | tf_op jit(solution)/shard_map/all_to_all | solution.py:12
  81.7 9.8 %all-to-all-start.3 = ((f32[32,8,2]{0,2,1:T(2,128)}), f32[32,8,2]{0,2,1:T(2,128)S(1)}, u32[]{:S(2)}, u32[]{:S(2)}) async-start(f32[32,8,2]{0,2,1:T(2,128)} %broadcast_in_dim.8), calls=%async_computation.3 | async-start | bytes 16384 | tf_op jit(solution)/shard_map/all_to_all | solution.py:12
  91.8 14.0 %copy-start.2 = (f32[32,1024]{1,0:T(8,128)}, f32[32,1024]{1,0:T(8,128)S(1)}, u32[]{:S(2)}) copy-start(f32[32,1024]{1,0:T(8,128)S(1)} %multiply_add_fusion) | copy-start | bytes 393220

commit v16 on v15

--- a/solution.py
+++ b/solution.py
@@ -113,6 +113,8 @@
     width, rows = extended.shape
     edges = head_rows.shape[1]
     tile = edge_tile(rows)
+    if mode == "gap" and rows <= 2048 and edges % 4096 == 0:
+        tile = 4096
     edge_spec = pl.BlockSpec((1, tile), lambda i: (0, i))
     full = pl.BlockSpec((width, rows), lambda i: (0, 0))
     if mode == "scatter":

time: 112 us -> 112 us (level)
  no operation moved by 1% of the time
where the time goes in v16:
time: 112 us; the launch traced here: 111 us
  Pallas kernels  41.5 us (37%)
  blocking collectives  23.8 us (21%)
  waiting for transfers between devices  20 us (18%)
  starting transfers between devices  14.1 us (13%)
  local copies, waits for them, and re-layouts  4.9 us (4%)
  other arithmetic  4 us (4%)
  matrix products  2.3 us (2%)
    pallas_call x3, Pallas kernels, edge_pass(): pl.pallas_call(flow_kernel(mode, local), grid=(edges // tile,), in_specs=...  41.5 us
    all_to_all x3, waiting for transfers between devices, trade(): lax.all_to_all(blocks, ('vx', 'vy'), split_axis=1, concat_axis=1, tiled=T...  20 us
    all_to_all x3, starting transfers between devices, trade(): lax.all_to_all(blocks, ('vx', 'vy'), split_axis=1, concat_axis=1, tiled=T...  14.1 us
    all_to_all x1, blocking collectives, trade(): lax.all_to_all(blocks, ('vx', 'vy'), split_axis=1, concat_axis=1, tiled=T...  9.91 us
    all_gather x1, blocking collectives, body(): lax.all_gather(extended, 'col', axis=0, tiled=True)  8.63 us
    all_gather x1, blocking collectives, body(): resistance = lax.all_gather(total, 'col', axis=0, tiled=True)  5.25 us
    unnamed x17, local copies, waits for them, and re-layouts  2.42 us
    dot_general x3, matrix products, pick(): jnp.einsum(pattern, parts3(values), choice, preferred_element_type=jnp.fl...  2.3 us
  transfers between devices with their start and end apart: 3, of which 3 were waited for; matrix products, arithmetic and copies ran while one was open for 0% of the time, Pallas kernels for 0%

profile of v16, /device:TPU:0, one launch (start us, length us, event | category | flops | bytes accessed | tf_op | source)
XLA Modules:
  0.0 111.4 jit_solution(10256025825102903036)
XLA Ops:
  0.6 1.1 reduce-precision_convert_fusion.5
  1.7 1.2 %fusion.2 = f32[96,8,64]{0,2,1:T(8,128)S(1)} fusion(s32[8,64]{1,0:T(8,128)} %param.9, bf16[32,1024]{1,0:T(8,128)(2,1)S(1)} %get-tuple-element.26, bf16[32,1024]{1,0:T(8,128)(2,1)S(1)} %get-tuple-element.29, bf16[32,1024]{1,0:T(8,128)(2,1)S(1)} %get-tuple-element.25), kind=kOutput, calls=%fused_computation.3 | convolution fusion | flops 101777408 | bytes 395264 | tf_op jit(solution)/shard_map/cv,psv->cps/dot_general | solution.py:161
  2.9 0.0 copy-start.3
  2.9 0.2 slice_add_fusion.2
  3.1 0.1 copy.58
  3.2 0.0 copy-start.1
  3.2 0.8 reshape.75
  4.0 0.0 copy-start
  4.0 7.4 %all-to-all-start = ((f32[8,1,2048]{2,1,0:T(1,128)}), f32[8,1,2048]{2,1,0:T(1,128)S(1)}, u32[]{:S(2)}, u32[]{:S(2)}) async-start(f32[8,1,2048]{2,1,0:T(1,128)} %reshape.75), calls=%async_computation | async-start | bytes 131072 | tf_op jit(solution)/shard_map/all_to_all | solution.py:12
  11.4 0.0 copy-done.3
  11.4 0.1 fusion.29
  11.5 0.1 copy.60
  11.6 0.1 copy.61
  11.7 6.7 %all-to-all-done = f32[8,1,2048]{2,1,0:T(1,128)S(1)} async-done(((f32[8,1,2048]{2,1,0:T(1,128)}), f32[8,1,2048]{2,1,0:T(1,128)S(1)}, u32[]{:S(2)}, u32[]{:S(2)}) %all-to-all-start) | async-done | bytes 65568 | tf_op jit(solution)/shard_map/all_to_all | solution.py:12
  18.4 0.5 broadcast.6
  18.9 0.8 reduce.4
  19.7 0.1 reshape.76
  19.8 0.1 copy.59
  19.9 0.1 reshape.66
  20.0 0.0 copy-done.1
  20.0 0.0 copy-done
  20.0 25.6 %shard_map.68 = (f32[32,1536]{1,0:T(8,128)S(1)}, f32[32,1]{1,0:T(8,128)S(1)}) custom-call(f32[32,1536]{1,0:T(8,128)S(1)} %pad_maximum_fusion.xs_ref, s32[1,16384]{1,0:T(1,128)S(1)} %get-tuple-element.24.head_ref, s32[1,16384]{1,0:T(1,128)S(1)} %get-tuple-element.23.tail_ref, f32[1,16384]{1,0:T(1,128)S(1)} %bitcast.37), custom_call_target="tpu_custom_call" | custom-call | tf_op jit(solution)/shard_map/pallas_call | solution.py:132
  45.6 0.1 reshape.67
  45.7 0.1 pad_maximum_fusion.5
  45.8 0.1 pad_maximum_fusion.4
  45.9 0.0 copy-start.5
  45.9 9.9 %all_to_all.20 = f32[32,8,66]{2,0,1:T(8,128)S(1)} all-to-all(f32[32,8,66]{2,0,1:T(8,128)S(1)} %copy.62), channel_id=1, replica_groups=mesh['vx'=2,'vy'=4,'col'=4] {'vx','vy'}, dimensions={1} | all-to-all | bytes 135168 | tf_op jit(solution)/shard_map/all_to_all | solution.py:12
  55.9 0.1 slice_reduce_fusion
  56.0 0.2 slice_reduce_fusion.1
  56.1 0.1 reduce-precision_convert_fusion.3
  56.3 0.0 copy-done.5
  56.3 0.0 copy-start.4
  56.3 0.6 fusion.3
  57.0 0.1 copy-done.4
  57.0 0.1 reduce-precision_convert_fusion.1
  57.1 0.2 reduce-precision_convert_fusion
  57.3 0.5 fusion
  57.8 0.2 slice_add_fusion
  58.0 0.1 copy.65
  58.1 0.8 reshape.77
  58.9 3.4 %all-to-all-start.2 = ((f32[8,1,2048]{2,1,0:T(1,128)}), f32[8,1,2048]{2,1,0:T(1,128)S(1)}, u32[]{:S(2)}, u32[]{:S(2)}) async-start(f32[8,1,2048]{2,1,0:T(1,128)} %reshape.77), calls=%async_computation.2 | async-start | bytes 131072 | tf_op jit(solution)/shard_map/all_to_all | solution.py:12
  62.2 0.1 copy.67
  62.3 6.8 %all-to-all-done.2 = f32[8,1,2048]{2,1,0:T(1,128)S(1)} async-done(((f32[8,1,2048]{2,1,0:T(1,128)}), f32[8,1,2048]{2,1,0:T(1,128)S(1)}, u32[]{:S(2)}, u32[]{:S(2)}) %all-to-all-start.2) | async-done | bytes 65568 | tf_op jit(solution)/shard_map/all_to_all | solution.py:12
  69.1 0.8 reduce.5
  70.0 0.1 reshape.78
  70.0 0.1 copy.66
  70.1 0.1 reshape.68
  70.2 10.8 %shard_map.69 = f32[32,1]{1,0:T(8,128)S(1)} custom-call(f32[32,1536]{1,0:T(8,128)S(1)} %pad_maximum_fusion.2.xs_ref, s32[1,16384]{1,0:T(1,128)S(1)} %get-tuple-element.24.head_ref, s32[1,16384]{1,0:T(1,128)S(1)} %get-tuple-element.23.tail_ref, f32[1,16384]{1,0:T(1,128)S(1)} %bitcast.38), custom_call_target="tpu_custom_call" | custom-call | tf_op jit(solution)/shard_map/pallas_call | solution.py:132
  81.0 0.1 copy.68
  81.1 0.6 broadcast_in_dim.8
  81.7 3.3 %all-to-all-start.3 = ((f32[32,8,2]{0,2,1:T(2,128)}), f32[32,8,2]{0,2,1:T(2,128)S(1)}, u32[]{:S(2)}, u32[]{:S(2)}) async-start(f32[32,8,2]{0,2,1:T(2,128)} %broadcast_in_dim.8), calls=%async_computation.3 | async-start | bytes 16384 | tf_op jit(solution)/shard_map/all_to_all | solution.py:12
  85.1 6.4 %all-to-all-done.3 = f32[32,8,2]{0,2,1:T(2,128)S(1)} async-done(((f32[32,8,2]{0,2,1:T(2,128)}), f32[32,8,2]{0,2,1:T(2,128)S(1)}, u32[]{:S(2)}, u32[]{:S(2)}) %all-to-all-start.3) | async-done | bytes 2080 | tf_op jit(solution)/shard_map/all_to_all | solution.py:12
  91.6 0.1 multiply_add_fusion.1
  91.7 0.1 multiply_add_fusion
  91.8 0.0 copy-start.2
  91.8 8.6 %all_gather.6.xs_ref = f32[128,1536]{1,0:T(8,128)S(1)} all-gather(f32[32,1536]{1,0:T(8,128)S(1)} %pad_maximum_fusion.3), channel_id=1, replica_groups=mesh['vx'=2,'vy'=4,'col'=4] {'col'}, dimensions={0}, use_global_device_ids=true | all-gather | bytes 983040 | tf_op jit(solution)/shard_map/all_gather | solution.py:225
  100.4 5.1 %shard_map.70 = f32[1,4096]{1,0:T(1,128)S(1)} custom-call(f32[128,1536]{1,0:T(8,128)S(1)} %all_gather.6.xs_ref, s32[1,4096]{1,0:T(1,128)S(1)} %get-tuple-element.31.head_ref, s32[1,4096]{1,0:T(1,128)S(1)} %get-tuple-element.30.tail_ref, f32[1,4096]{1,0:T(1,128)S(1)} %bitcast.39), custom_call_target="tpu_custom_call" | custom-call | tf_op jit(solution)/shard_map/pallas_call | solution.py:132
  105.5 0.0 copy-done.2
  105.5 5.2 %all-gather = f32[1,16384]{1,0:T(1,128)S(1)} all-gather(f32[1,4096]{1,0:T(1,128)S(1)} %shard_map.70), channel_id=2, replica_groups=mesh['vx'=2,'vy'=4,'col'=4] {'col'}, dimensions={1}, use_global_device_ids=true | all-gather | bytes 81920 | tf_op jit(solution)/shard_map/all_gather | solution.py:226
  110.8 0.6 copy.79
  (15 shorter events, 0.2 us)
Async XLA Ops:
  2.9 8.5 %copy-start.3 = (s32[2,16384]{1,0:T(2,128)S(1)}, s32[2,16384]{1,0:T(2,128)}, u32[]{:S(2)}) copy-start(s32[2,16384]{1,0:T(2,128)} %param.7) | copy-start | bytes 393220
  3.2 16.7 %copy-start.1 = (f32[32,1024]{1,0:T(8,128)S(1)}, f32[32,1024]{1,0:T(8,128)}, u32[]{:S(2)}) copy-start(f32[32,1024]{1,0:T(8,128)} %param.5) | copy-start | bytes 393220
  4.0 16.0 %copy-start = (f32[16384]{0:T(1024)S(1)}, f32[16384]{0:T(1024)}, u32[]{:S(2)}) copy-start(f32[16384]{0:T(1024)} %param.8) | copy-start | bytes 196612
  4.0 14.4 %all-to-all-start = ((f32[8,1,2048]{2,1,0:T(1,128)}), f32[8,1,2048]{2,1,0:T(1,128)S(1)}, u32[]{:S(2)}, u32[]{:S(2)}) async-start(f32[8,1,2048]{2,1,0:T(1,128)} %reshape.75), calls=%async_computation | async-start | bytes 131072 | tf_op jit(solution)/shard_map/all_to_all | solution.py:12
  45.9 10.4 %copy-start.5 = (s32[8,64]{1,0:T(8,128)S(1)}, s32[8,64]{1,0:T(8,128)}, u32[]{:S(2)}) copy-start(s32[8,64]{1,0:T(8,128)} %param.9) | copy-start | bytes 6148
  56.3 0.7 copy-start.4
  58.9 10.3 %all-to-all-start.2 = ((f32[8,1,2048]{2,1,0:T(1,128)}), f32[8,1,2048]{2,1,0:T(1,128)S(1)}, u32[]{:S(2)}, u32[]{:S(2)}) async-start(f32[8,1,2048]{2,1,0:T(1,128)} %reshape.77), calls=%async_computation.2 | async-start | bytes 131072 | tf_op jit(solution)/shard_map/all_to_all | solution.py:12
  81.7 9.8 %all-to-all-start.3 = ((f32[32,8,2]{0,2,1:T(2,128)}), f32[32,8,2]{0,2,1:T(2,128)S(1)}, u32[]{:S(2)}, u32[]{:S(2)}) async-start(f32[32,8,2]{0,2,1:T(2,128)} %broadcast_in_dim.8), calls=%async_computation.3 | async-start | bytes 16384 | tf_op jit(solution)/shard_map/all_to_all | solution.py:12
  91.8 13.8 %copy-start.2 = (f32[32,1024]{1,0:T(8,128)}, f32[32,1024]{1,0:T(8,128)S(1)}, u32[]{:S(2)}) copy-start(f32[32,1024]{1,0:T(8,128)S(1)} %multiply_add_fusion) | copy-start | bytes 393220

commit v17 on v16

--- a/solution.py
+++ b/solution.py
@@ -113,7 +113,7 @@
     width, rows = extended.shape
     edges = head_rows.shape[1]
     tile = edge_tile(rows)
-    if mode == "gap" and rows <= 2048 and edges % 4096 == 0:
+    if mode != "scatter" and rows <= 2048 and edges % 4096 == 0:
         tile = 4096
     edge_spec = pl.BlockSpec((1, tile), lambda i: (0, i))
     full = pl.BlockSpec((width, rows), lambda i: (0, 0))

time: 112 us -> 111 us (level)
  no operation moved by 1% of the time
where the time goes in v17:
time: 111 us
  Pallas kernels  40.6 us (37%)
  blocking collectives  24 us (22%)
  waiting for transfers between devices  20 us (18%)
  starting transfers between devices  14.1 us (13%)
  local copies, waits for them, and re-layouts  4.89 us (4%)
  other arithmetic  4 us (4%)
  matrix products  2.3 us (2%)
    pallas_call x3, Pallas kernels, edge_pass(): pl.pallas_call(flow_kernel(mode, local), grid=(edges // tile,), in_specs=...  40.6 us
    all_to_all x3, waiting for transfers between devices, trade(): lax.all_to_all(blocks, ('vx', 'vy'), split_axis=1, concat_axis=1, tiled=T...  20 us
    all_to_all x3, starting transfers between devices, trade(): lax.all_to_all(blocks, ('vx', 'vy'), split_axis=1, concat_axis=1, tiled=T...  14.1 us
    all_to_all x1, blocking collectives, trade(): lax.all_to_all(blocks, ('vx', 'vy'), split_axis=1, concat_axis=1, tiled=T...  9.91 us
    all_gather x1, blocking collectives, body(): lax.all_gather(extended, 'col', axis=0, tiled=True)  8.81 us
    all_gather x1, blocking collectives, body(): resistance = lax.all_gather(total, 'col', axis=0, tiled=True)  5.25 us
    unnamed x17, local copies, waits for them, and re-layouts  2.42 us
    dot_general x3, matrix products, pick(): jnp.einsum(pattern, parts3(values), choice, preferred_element_type=jnp.fl...  2.3 us
  transfers between devices with their start and end apart: 3, of which 3 were waited for; matrix products, arithmetic and copies ran while one was open for 0% of the time, Pallas kernels for 0%

profile of v17, /device:TPU:0, one launch (start us, length us, event | category | flops | bytes accessed | tf_op | source)
XLA Modules:
  0.0 110.7 jit_solution(17696889030577521476)
XLA Ops:
  0.6 1.1 reduce-precision_convert_fusion.5
  1.7 1.2 %fusion.2 = f32[96,8,64]{0,2,1:T(8,128)S(1)} fusion(s32[8,64]{1,0:T(8,128)} %param.9, bf16[32,1024]{1,0:T(8,128)(2,1)S(1)} %get-tuple-element.26, bf16[32,1024]{1,0:T(8,128)(2,1)S(1)} %get-tuple-element.29, bf16[32,1024]{1,0:T(8,128)(2,1)S(1)} %get-tuple-element.25), kind=kOutput, calls=%fused_computation.3 | convolution fusion | flops 101777408 | bytes 395264 | tf_op jit(solution)/shard_map/cv,psv->cps/dot_general | solution.py:161
  2.9 0.0 copy-start.3
  2.9 0.2 slice_add_fusion.2
  3.1 0.1 copy.58
  3.2 0.0 copy-start.1
  3.2 0.8 reshape.75
  4.0 0.0 copy-start
  4.0 7.4 %all-to-all-start = ((f32[8,1,2048]{2,1,0:T(1,128)}), f32[8,1,2048]{2,1,0:T(1,128)S(1)}, u32[]{:S(2)}, u32[]{:S(2)}) async-start(f32[8,1,2048]{2,1,0:T(1,128)} %reshape.75), calls=%async_computation | async-start | bytes 131072 | tf_op jit(solution)/shard_map/all_to_all | solution.py:12
  11.4 0.0 copy-done.3
  11.4 0.1 fusion.29
  11.5 0.1 copy.60
  11.6 0.1 copy.61
  11.7 6.7 %all-to-all-done = f32[8,1,2048]{2,1,0:T(1,128)S(1)} async-done(((f32[8,1,2048]{2,1,0:T(1,128)}), f32[8,1,2048]{2,1,0:T(1,128)S(1)}, u32[]{:S(2)}, u32[]{:S(2)}) %all-to-all-start) | async-done | bytes 65568 | tf_op jit(solution)/shard_map/all_to_all | solution.py:12
  18.4 0.5 broadcast.6
  18.9 0.8 reduce.4
  19.7 0.1 reshape.76
  19.8 0.1 copy.59
  19.9 0.1 reshape.66
  20.0 0.0 copy-done.1
  20.0 0.0 copy-done
  20.0 25.6 %shard_map.68 = (f32[32,1536]{1,0:T(8,128)S(1)}, f32[32,1]{1,0:T(8,128)S(1)}) custom-call(f32[32,1536]{1,0:T(8,128)S(1)} %pad_maximum_fusion.xs_ref, s32[1,16384]{1,0:T(1,128)S(1)} %get-tuple-element.24.head_ref, s32[1,16384]{1,0:T(1,128)S(1)} %get-tuple-element.23.tail_ref, f32[1,16384]{1,0:T(1,128)S(1)} %bitcast.37), custom_call_target="tpu_custom_call" | custom-call | tf_op jit(solution)/shard_map/pallas_call | solution.py:132
  45.6 0.1 reshape.67
  45.7 0.1 pad_maximum_fusion.5
  45.8 0.1 pad_maximum_fusion.4
  45.9 0.0 copy-start.5
  45.9 9.9 %all_to_all.20 = f32[32,8,66]{2,0,1:T(8,128)S(1)} all-to-all(f32[32,8,66]{2,0,1:T(8,128)S(1)} %copy.62), channel_id=1, replica_groups=mesh['vx'=2,'vy'=4,'col'=4] {'vx','vy'}, dimensions={1} | all-to-all | bytes 135168 | tf_op jit(solution)/shard_map/all_to_all | solution.py:12
  55.9 0.1 slice_reduce_fusion
  56.0 0.2 slice_reduce_fusion.1
  56.1 0.1 reduce-precision_convert_fusion.3
  56.3 0.0 copy-done.5
  56.3 0.0 copy-start.4
  56.3 0.6 fusion.3
  57.0 0.1 copy-done.4
  57.0 0.1 reduce-precision_convert_fusion.1
  57.1 0.2 reduce-precision_convert_fusion
  57.2 0.5 fusion
  57.8 0.2 slice_add_fusion
  58.0 0.1 copy.65
  58.1 0.8 reshape.77
  58.9 3.4 %all-to-all-start.2 = ((f32[8,1,2048]{2,1,0:T(1,128)}), f32[8,1,2048]{2,1,0:T(1,128)S(1)}, u32[]{:S(2)}, u32[]{:S(2)}) async-start(f32[8,1,2048]{2,1,0:T(1,128)} %reshape.77), calls=%async_computation.2 | async-start | bytes 131072 | tf_op jit(solution)/shard_map/all_to_all | solution.py:12
  62.2 0.1 copy.67
  62.3 6.8 %all-to-all-done.2 = f32[8,1,2048]{2,1,0:T(1,128)S(1)} async-done(((f32[8,1,2048]{2,1,0:T(1,128)}), f32[8,1,2048]{2,1,0:T(1,128)S(1)}, u32[]{:S(2)}, u32[]{:S(2)}) %all-to-all-start.2) | async-done | bytes 65568 | tf_op jit(solution)/shard_map/all_to_all | solution.py:12
  69.1 0.8 reduce.5
  69.9 0.1 reshape.78
  70.0 0.1 copy.66
  70.1 0.1 reshape.68
  70.2 9.9 %shard_map.69 = f32[32,1]{1,0:T(8,128)S(1)} custom-call(f32[32,1536]{1,0:T(8,128)S(1)} %pad_maximum_fusion.2.xs_ref, s32[1,16384]{1,0:T(1,128)S(1)} %get-tuple-element.24.head_ref, s32[1,16384]{1,0:T(1,128)S(1)} %get-tuple-element.23.tail_ref, f32[1,16384]{1,0:T(1,128)S(1)} %bitcast.38), custom_call_target="tpu_custom_call" | custom-call | tf_op jit(solution)/shard_map/pallas_call | solution.py:132
  80.2 0.1 copy.68
  80.2 0.6 broadcast_in_dim.8
  80.9 3.3 %all-to-all-start.3 = ((f32[32,8,2]{0,2,1:T(2,128)}), f32[32,8,2]{0,2,1:T(2,128)S(1)}, u32[]{:S(2)}, u32[]{:S(2)}) async-start(f32[32,8,2]{0,2,1:T(2,128)} %broadcast_in_dim.8), calls=%async_computation.3 | async-start | bytes 16384 | tf_op jit(solution)/shard_map/all_to_all | solution.py:12
  84.2 6.4 %all-to-all-done.3 = f32[32,8,2]{0,2,1:T(2,128)S(1)} async-done(((f32[32,8,2]{0,2,1:T(2,128)}), f32[32,8,2]{0,2,1:T(2,128)S(1)}, u32[]{:S(2)}, u32[]{:S(2)}) %all-to-all-start.3) | async-done | bytes 2080 | tf_op jit(solution)/shard_map/all_to_all | solution.py:12
  90.7 0.1 multiply_add_fusion.1
  90.8 0.1 multiply_add_fusion
  90.9 0.0 copy-start.2
  90.9 8.8 %all_gather.6.xs_ref = f32[128,1536]{1,0:T(8,128)S(1)} all-gather(f32[32,1536]{1,0:T(8,128)S(1)} %pad_maximum_fusion.3), channel_id=1, replica_groups=mesh['vx'=2,'vy'=4,'col'=4] {'col'}, dimensions={0}, use_global_device_ids=true | all-gather | bytes 983040 | tf_op jit(solution)/shard_map/all_gather | solution.py:225
  99.7 5.1 %shard_map.70 = f32[1,4096]{1,0:T(1,128)S(1)} custom-call(f32[128,1536]{1,0:T(8,128)S(1)} %all_gather.6.xs_ref, s32[1,4096]{1,0:T(1,128)S(1)} %get-tuple-element.31.head_ref, s32[1,4096]{1,0:T(1,128)S(1)} %get-tuple-element.30.tail_ref, f32[1,4096]{1,0:T(1,128)S(1)} %bitcast.39), custom_call_target="tpu_custom_call" | custom-call | tf_op jit(solution)/shard_map/pallas_call | solution.py:132
  104.8 0.0 copy-done.2
  104.8 5.2 %all-gather = f32[1,16384]{1,0:T(1,128)S(1)} all-gather(f32[1,4096]{1,0:T(1,128)S(1)} %shard_map.70), channel_id=2, replica_groups=mesh['vx'=2,'vy'=4,'col'=4] {'col'}, dimensions={1}, use_global_device_ids=true | all-gather | bytes 81920 | tf_op jit(solution)/shard_map/all_gather | solution.py:226
  110.1 0.6 copy.79
  (15 shorter events, 0.2 us)
Async XLA Ops:
  2.9 8.5 %copy-start.3 = (s32[2,16384]{1,0:T(2,128)S(1)}, s32[2,16384]{1,0:T(2,128)}, u32[]{:S(2)}) copy-start(s32[2,16384]{1,0:T(2,128)} %param.7) | copy-start | bytes 393220
  3.2 16.7 %copy-start.1 = (f32[32,1024]{1,0:T(8,128)S(1)}, f32[32,1024]{1,0:T(8,128)}, u32[]{:S(2)}) copy-start(f32[32,1024]{1,0:T(8,128)} %param.5) | copy-start | bytes 393220
  4.0 16.0 %copy-start = (f32[16384]{0:T(1024)S(1)}, f32[16384]{0:T(1024)}, u32[]{:S(2)}) copy-start(f32[16384]{0:T(1024)} %param.8) | copy-start | bytes 196612
  4.0 14.4 %all-to-all-start = ((f32[8,1,2048]{2,1,0:T(1,128)}), f32[8,1,2048]{2,1,0:T(1,128)S(1)}, u32[]{:S(2)}, u32[]{:S(2)}) async-start(f32[8,1,2048]{2,1,0:T(1,128)} %reshape.75), calls=%async_computation | async-start | bytes 131072 | tf_op jit(solution)/shard_map/all_to_all | solution.py:12
  45.9 10.4 %copy-start.5 = (s32[8,64]{1,0:T(8,128)S(1)}, s32[8,64]{1,0:T(8,128)}, u32[]{:S(2)}) copy-start(s32[8,64]{1,0:T(8,128)} %param.9) | copy-start | bytes 6148
  56.3 0.7 copy-start.4
  58.9 10.3 %all-to-all-start.2 = ((f32[8,1,2048]{2,1,0:T(1,128)}), f32[8,1,2048]{2,1,0:T(1,128)S(1)}, u32[]{:S(2)}, u32[]{:S(2)}) async-start(f32[8,1,2048]{2,1,0:T(1,128)} %reshape.77), calls=%async_computation.2 | async-start | bytes 131072 | tf_op jit(solution)/shard_map/all_to_all | solution.py:12
  80.9 9.8 %all-to-all-start.3 = ((f32[32,8,2]{0,2,1:T(2,128)}), f32[32,8,2]{0,2,1:T(2,128)S(1)}, u32[]{:S(2)}, u32[]{:S(2)}) async-start(f32[32,8,2]{0,2,1:T(2,128)} %broadcast_in_dim.8), calls=%async_computation.3 | async-start | bytes 16384 | tf_op jit(solution)/shard_map/all_to_all | solution.py:12
  90.9 13.9 %copy-start.2 = (f32[32,1024]{1,0:T(8,128)}, f32[32,1024]{1,0:T(8,128)S(1)}, u32[]{:S(2)}) copy-start(f32[32,1024]{1,0:T(8,128)S(1)} %multiply_add_fusion) | copy-start | bytes 393220

commit v18 on v17

--- a/solution.py
+++ b/solution.py
@@ -113,7 +113,7 @@
     width, rows = extended.shape
     edges = head_rows.shape[1]
     tile = edge_tile(rows)
-    if mode != "scatter" and rows <= 2048 and edges % 4096 == 0:
+    if rows <= 2048 and edges % 4096 == 0:
         tile = 4096
     edge_spec = pl.BlockSpec((1, tile), lambda i: (0, i))
     full = pl.BlockSpec((width, rows), lambda i: (0, 0))

time: 111 us -> 111 us (level)
  no operation moved by 1% of the time
where the time goes in v18:
time: 111 us; the launch traced here: 110 us
  Pallas kernels  40 us (36%)
  blocking collectives  24 us (22%)
  waiting for transfers between devices  20 us (18%)
  starting transfers between devices  14.1 us (13%)
  local copies, waits for them, and re-layouts  4.89 us (4%)
  other arithmetic  4 us (4%)
  matrix products  2.3 us (2%)
    pallas_call x3, Pallas kernels, edge_pass(): pl.pallas_call(flow_kernel(mode, local), grid=(edges // tile,), in_specs=...  40 us
    all_to_all x3, waiting for transfers between devices, trade(): lax.all_to_all(blocks, ('vx', 'vy'), split_axis=1, concat_axis=1, tiled=T...  20 us
    all_to_all x3, starting transfers between devices, trade(): lax.all_to_all(blocks, ('vx', 'vy'), split_axis=1, concat_axis=1, tiled=T...  14.1 us
    all_to_all x1, blocking collectives, trade(): lax.all_to_all(blocks, ('vx', 'vy'), split_axis=1, concat_axis=1, tiled=T...  9.91 us
    all_gather x1, blocking collectives, body(): lax.all_gather(extended, 'col', axis=0, tiled=True)  8.81 us
    all_gather x1, blocking collectives, body(): resistance = lax.all_gather(total, 'col', axis=0, tiled=True)  5.25 us
    unnamed x17, local copies, waits for them, and re-layouts  2.42 us
    dot_general x3, matrix products, pick(): jnp.einsum(pattern, parts3(values), choice, preferred_element_type=jnp.fl...  2.3 us
  transfers between devices with their start and end apart: 3, of which 3 were waited for; matrix products, arithmetic and copies ran while one was open for 0% of the time, Pallas kernels for 0%

profile of v18, /device:TPU:0, one launch (start us, length us, event | category | flops | bytes accessed | tf_op | source)
XLA Modules:
  0.0 110.1 jit_solution(1107837253075937900)
XLA Ops:
  0.6 1.1 reduce-precision_convert_fusion.5
  1.7 1.2 %fusion.2 = f32[96,8,64]{0,2,1:T(8,128)S(1)} fusion(s32[8,64]{1,0:T(8,128)} %param.9, bf16[32,1024]{1,0:T(8,128)(2,1)S(1)} %get-tuple-element.26, bf16[32,1024]{1,0:T(8,128)(2,1)S(1)} %get-tuple-element.29, bf16[32,1024]{1,0:T(8,128)(2,1)S(1)} %get-tuple-element.25), kind=kOutput, calls=%fused_computation.3 | convolution fusion | flops 101777408 | bytes 395264 | tf_op jit(solution)/shard_map/cv,psv->cps/dot_general | solution.py:161
  2.9 0.0 copy-start.3
  2.9 0.2 slice_add_fusion.2
  3.1 0.1 copy.58
  3.2 0.0 copy-start.1
  3.2 0.8 reshape.75
  4.0 0.0 copy-start
  4.0 7.4 %all-to-all-start = ((f32[8,1,2048]{2,1,0:T(1,128)}), f32[8,1,2048]{2,1,0:T(1,128)S(1)}, u32[]{:S(2)}, u32[]{:S(2)}) async-start(f32[8,1,2048]{2,1,0:T(1,128)} %reshape.75), calls=%async_computation | async-start | bytes 131072 | tf_op jit(solution)/shard_map/all_to_all | solution.py:12
  11.4 0.0 copy-done.3
  11.4 0.1 fusion.29
  11.5 0.1 copy.60
  11.6 0.1 copy.61
  11.7 6.7 %all-to-all-done = f32[8,1,2048]{2,1,0:T(1,128)S(1)} async-done(((f32[8,1,2048]{2,1,0:T(1,128)}), f32[8,1,2048]{2,1,0:T(1,128)S(1)}, u32[]{:S(2)}, u32[]{:S(2)}) %all-to-all-start) | async-done | bytes 65568 | tf_op jit(solution)/shard_map/all_to_all | solution.py:12
  18.4 0.5 broadcast.6
  18.9 0.8 reduce.4
  19.7 0.1 reshape.76
  19.8 0.1 copy.59
  19.9 0.1 reshape.66
  20.0 0.0 copy-done.1
  20.0 0.0 copy-done
  20.0 25.0 %shard_map.68 = (f32[32,1536]{1,0:T(8,128)S(1)}, f32[32,1]{1,0:T(8,128)S(1)}) custom-call(f32[32,1536]{1,0:T(8,128)S(1)} %pad_maximum_fusion.xs_ref, s32[1,16384]{1,0:T(1,128)S(1)} %get-tuple-element.24.head_ref, s32[1,16384]{1,0:T(1,128)S(1)} %get-tuple-element.23.tail_ref, f32[1,16384]{1,0:T(1,128)S(1)} %bitcast.37), custom_call_target="tpu_custom_call" | custom-call | tf_op jit(solution)/shard_map/pallas_call | solution.py:132
  45.0 0.1 reshape.67
  45.1 0.1 pad_maximum_fusion.5
  45.2 0.1 pad_maximum_fusion.4
  45.3 0.0 copy-start.5
  45.3 9.9 %all_to_all.20 = f32[32,8,66]{2,0,1:T(8,128)S(1)} all-to-all(f32[32,8,66]{2,0,1:T(8,128)S(1)} %copy.62), channel_id=1, replica_groups=mesh['vx'=2,'vy'=4,'col'=4] {'vx','vy'}, dimensions={1} | all-to-all | bytes 135168 | tf_op jit(solution)/shard_map/all_to_all | solution.py:12
  55.3 0.1 slice_reduce_fusion
  55.4 0.2 slice_reduce_fusion.1
  55.5 0.1 reduce-precision_convert_fusion.3
  55.7 0.0 copy-done.5
  55.7 0.0 copy-start.4
  55.7 0.6 fusion.3
  56.4 0.1 copy-done.4
  56.4 0.1 reduce-precision_convert_fusion.1
  56.5 0.2 reduce-precision_convert_fusion
  56.6 0.5 fusion
  57.2 0.2 slice_add_fusion
  57.4 0.1 copy.65
  57.5 0.8 reshape.77
  58.2 3.4 %all-to-all-start.2 = ((f32[8,1,2048]{2,1,0:T(1,128)}), f32[8,1,2048]{2,1,0:T(1,128)S(1)}, u32[]{:S(2)}, u32[]{:S(2)}) async-start(f32[8,1,2048]{2,1,0:T(1,128)} %reshape.77), calls=%async_computation.2 | async-start | bytes 131072 | tf_op jit(solution)/shard_map/all_to_all | solution.py:12
  61.6 0.1 copy.67
  61.7 6.8 %all-to-all-done.2 = f32[8,1,2048]{2,1,0:T(1,128)S(1)} async-done(((f32[8,1,2048]{2,1,0:T(1,128)}), f32[8,1,2048]{2,1,0:T(1,128)S(1)}, u32[]{:S(2)}, u32[]{:S(2)}) %all-to-all-start.2) | async-done | bytes 65568 | tf_op jit(solution)/shard_map/all_to_all | solution.py:12
  68.5 0.8 reduce.5
  69.3 0.1 reshape.78
  69.4 0.1 copy.66
  69.5 0.1 reshape.68
  69.6 9.9 %shard_map.69 = f32[32,1]{1,0:T(8,128)S(1)} custom-call(f32[32,1536]{1,0:T(8,128)S(1)} %pad_maximum_fusion.2.xs_ref, s32[1,16384]{1,0:T(1,128)S(1)} %get-tuple-element.24.head_ref, s32[1,16384]{1,0:T(1,128)S(1)} %get-tuple-element.23.tail_ref, f32[1,16384]{1,0:T(1,128)S(1)} %bitcast.38), custom_call_target="tpu_custom_call" | custom-call | tf_op jit(solution)/shard_map/pallas_call | solution.py:132
  79.6 0.1 copy.68
  79.6 0.6 broadcast_in_dim.8
  80.3 3.3 %all-to-all-start.3 = ((f32[32,8,2]{0,2,1:T(2,128)}), f32[32,8,2]{0,2,1:T(2,128)S(1)}, u32[]{:S(2)}, u32[]{:S(2)}) async-start(f32[32,8,2]{0,2,1:T(2,128)} %broadcast_in_dim.8), calls=%async_computation.3 | async-start | bytes 16384 | tf_op jit(solution)/shard_map/all_to_all | solution.py:12
  83.6 6.4 %all-to-all-done.3 = f32[32,8,2]{0,2,1:T(2,128)S(1)} async-done(((f32[32,8,2]{0,2,1:T(2,128)}), f32[32,8,2]{0,2,1:T(2,128)S(1)}, u32[]{:S(2)}, u32[]{:S(2)}) %all-to-all-start.3) | async-done | bytes 2080 | tf_op jit(solution)/shard_map/all_to_all | solution.py:12
  90.1 0.1 multiply_add_fusion.1
  90.2 0.1 multiply_add_fusion
  90.3 0.0 copy-start.2
  90.3 8.8 %all_gather.6.xs_ref = f32[128,1536]{1,0:T(8,128)S(1)} all-gather(f32[32,1536]{1,0:T(8,128)S(1)} %pad_maximum_fusion.3), channel_id=1, replica_groups=mesh['vx'=2,'vy'=4,'col'=4] {'col'}, dimensions={0}, use_global_device_ids=true | all-gather | bytes 983040 | tf_op jit(solution)/shard_map/all_gather | solution.py:225
  99.1 5.1 %shard_map.70 = f32[1,4096]{1,0:T(1,128)S(1)} custom-call(f32[128,1536]{1,0:T(8,128)S(1)} %all_gather.6.xs_ref, s32[1,4096]{1,0:T(1,128)S(1)} %get-tuple-element.31.head_ref, s32[1,4096]{1,0:T(1,128)S(1)} %get-tuple-element.30.tail_ref, f32[1,4096]{1,0:T(1,128)S(1)} %bitcast.39), custom_call_target="tpu_custom_call" | custom-call | tf_op jit(solution)/shard_map/pallas_call | solution.py:132
  104.2 0.0 copy-done.2
  104.2 5.2 %all-gather = f32[1,16384]{1,0:T(1,128)S(1)} all-gather(f32[1,4096]{1,0:T(1,128)S(1)} %shard_map.70), channel_id=2, replica_groups=mesh['vx'=2,'vy'=4,'col'=4] {'col'}, dimensions={1}, use_global_device_ids=true | all-gather | bytes 81920 | tf_op jit(solution)/shard_map/all_gather | solution.py:226
  109.5 0.6 copy.79
  (15 shorter events, 0.2 us)
Async XLA Ops:
  2.9 8.5 %copy-start.3 = (s32[2,16384]{1,0:T(2,128)S(1)}, s32[2,16384]{1,0:T(2,128)}, u32[]{:S(2)}) copy-start(s32[2,16384]{1,0:T(2,128)} %param.7) | copy-start | bytes 393220
  3.2 16.7 %copy-start.1 = (f32[32,1024]{1,0:T(8,128)S(1)}, f32[32,1024]{1,0:T(8,128)}, u32[]{:S(2)}) copy-start(f32[32,1024]{1,0:T(8,128)} %param.5) | copy-start | bytes 393220
  4.0 16.0 %copy-start = (f32[16384]{0:T(1024)S(1)}, f32[16384]{0:T(1024)}, u32[]{:S(2)}) copy-start(f32[16384]{0:T(1024)} %param.8) | copy-start | bytes 196612
  4.0 14.4 %all-to-all-start = ((f32[8,1,2048]{2,1,0:T(1,128)}), f32[8,1,2048]{2,1,0:T(1,128)S(1)}, u32[]{:S(2)}, u32[]{:S(2)}) async-start(f32[8,1,2048]{2,1,0:T(1,128)} %reshape.75), calls=%async_computation | async-start | bytes 131072 | tf_op jit(solution)/shard_map/all_to_all | solution.py:12
  45.3 10.4 %copy-start.5 = (s32[8,64]{1,0:T(8,128)S(1)}, s32[8,64]{1,0:T(8,128)}, u32[]{:S(2)}) copy-start(s32[8,64]{1,0:T(8,128)} %param.9) | copy-start | bytes 6148
  55.7 0.7 copy-start.4
  58.2 10.3 %all-to-all-start.2 = ((f32[8,1,2048]{2,1,0:T(1,128)}), f32[8,1,2048]{2,1,0:T(1,128)S(1)}, u32[]{:S(2)}, u32[]{:S(2)}) async-start(f32[8,1,2048]{2,1,0:T(1,128)} %reshape.77), calls=%async_computation.2 | async-start | bytes 131072 | tf_op jit(solution)/shard_map/all_to_all | solution.py:12
  80.3 9.8 %all-to-all-start.3 = ((f32[32,8,2]{0,2,1:T(2,128)}), f32[32,8,2]{0,2,1:T(2,128)S(1)}, u32[]{:S(2)}, u32[]{:S(2)}) async-start(f32[32,8,2]{0,2,1:T(2,128)} %broadcast_in_dim.8), calls=%async_computation.3 | async-start | bytes 16384 | tf_op jit(solution)/shard_map/all_to_all | solution.py:12
  90.3 13.9 %copy-start.2 = (f32[32,1024]{1,0:T(8,128)}, f32[32,1024]{1,0:T(8,128)S(1)}, u32[]{:S(2)}) copy-start(f32[32,1024]{1,0:T(8,128)S(1)} %multiply_add_fusion) | copy-start | bytes 393220

commit v19 on v18

--- a/solution.py
+++ b/solution.py
@@ -57,8 +57,8 @@
     return build
 
 
-def pieces(rows):
-    step = 256 if rows % 256 == 0 else (128 if rows % 128 == 0 else rows)
+def pieces(rows, wide=False):
+    step = 512 if wide and rows % 512 == 0 else (256 if rows % 256 == 0 else (128 if rows % 128 == 0 else rows))
     return [(first, step) for first in range(0, rows, step)]
 
 
@@ -75,7 +75,7 @@
         parts = []
         gap = None
         build = incidence(head, tail, rows, local)
-        for first, size in pieces(rows):
+        for first, size in pieces(rows, mode != "gap"):
             ends = build(first, size)
             parts.append(ends)
             term = jnp.dot(xs[:, first:first + size], ends, preferred_element_type=jnp.float32)
@@ -95,7 +95,7 @@
         energy_ref[...] = jnp.where(step == 0, 0.0, energy_ref[...]) + energy
         flow = split3(weighted)
         dims = (((1,), (1,)), ((), ()))
-        for (first, size), ends in zip(pieces(rows), parts):
+        for (first, size), ends in zip(pieces(rows, True), parts):
             window = total[:, first:first + size]
             total[:, first:first + size] = jnp.where(step == 0, 0.0, window) + lax.dot_general(
                 flow, ends, dims, preferred_element_type=jnp.float32

time: 111 us -> 110 us (level)
  no operation moved by 1% of the time
where the time goes in v19:
time: 110 us
  Pallas kernels  39.7 us (36%)
  blocking collectives  24 us (22%)
  waiting for transfers between devices  20 us (18%)
  starting transfers between devices  14.1 us (13%)
  local copies, waits for them, and re-layouts  4.89 us (4%)
  other arithmetic  4 us (4%)
  matrix products  2.3 us (2%)
    pallas_call x3, Pallas kernels, edge_pass(): pl.pallas_call(flow_kernel(mode, local), grid=(edges // tile,), in_specs=...  39.7 us
    all_to_all x3, waiting for transfers between devices, trade(): lax.all_to_all(blocks, ('vx', 'vy'), split_axis=1, concat_axis=1, tiled=T...  20 us
    all_to_all x3, starting transfers between devices, trade(): lax.all_to_all(blocks, ('vx', 'vy'), split_axis=1, concat_axis=1, tiled=T...  14.1 us
    all_to_all x1, blocking collectives, trade(): lax.all_to_all(blocks, ('vx', 'vy'), split_axis=1, concat_axis=1, tiled=T...  9.91 us
    all_gather x1, blocking collectives, body(): lax.all_gather(extended, 'col', axis=0, tiled=True)  8.81 us
    all_gather x1, blocking collectives, body(): resistance = lax.all_gather(total, 'col', axis=0, tiled=True)  5.25 us
    unnamed x17, local copies, waits for them, and re-layouts  2.42 us
    dot_general x3, matrix products, pick(): jnp.einsum(pattern, parts3(values), choice, preferred_element_type=jnp.fl...  2.3 us
  transfers between devices with their start and end apart: 3, of which 3 were waited for; matrix products, arithmetic and copies ran while one was open for 0% of the time, Pallas kernels for 0%

profile of v19, /device:TPU:0, one launch (start us, length us, event | category | flops | bytes accessed | tf_op | source)
XLA Modules:
  0.0 109.9 jit_solution(16151431149478116728)
XLA Ops:
  0.6 1.1 reduce-precision_convert_fusion.5
  1.7 1.2 %fusion.2 = f32[96,8,64]{0,2,1:T(8,128)S(1)} fusion(s32[8,64]{1,0:T(8,128)} %param.9, bf16[32,1024]{1,0:T(8,128)(2,1)S(1)} %get-tuple-element.26, bf16[32,1024]{1,0:T(8,128)(2,1)S(1)} %get-tuple-element.29, bf16[32,1024]{1,0:T(8,128)(2,1)S(1)} %get-tuple-element.25), kind=kOutput, calls=%fused_computation.3 | convolution fusion | flops 101777408 | bytes 395264 | tf_op jit(solution)/shard_map/cv,psv->cps/dot_general | solution.py:161
  2.9 0.0 copy-start.3
  2.9 0.2 slice_add_fusion.2
  3.1 0.1 copy.58
  3.2 0.0 copy-start.1
  3.2 0.8 reshape.75
  4.0 0.0 copy-start
  4.0 7.4 %all-to-all-start = ((f32[8,1,2048]{2,1,0:T(1,128)}), f32[8,1,2048]{2,1,0:T(1,128)S(1)}, u32[]{:S(2)}, u32[]{:S(2)}) async-start(f32[8,1,2048]{2,1,0:T(1,128)} %reshape.75), calls=%async_computation | async-start | bytes 131072 | tf_op jit(solution)/shard_map/all_to_all | solution.py:12
  11.4 0.0 copy-done.3
  11.4 0.1 fusion.29
  11.5 0.1 copy.60
  11.6 0.1 copy.61
  11.7 6.7 %all-to-all-done = f32[8,1,2048]{2,1,0:T(1,128)S(1)} async-done(((f32[8,1,2048]{2,1,0:T(1,128)}), f32[8,1,2048]{2,1,0:T(1,128)S(1)}, u32[]{:S(2)}, u32[]{:S(2)}) %all-to-all-start) | async-done | bytes 65568 | tf_op jit(solution)/shard_map/all_to_all | solution.py:12
  18.4 0.5 broadcast.6
  18.9 0.8 reduce.4
  19.7 0.1 reshape.76
  19.8 0.1 copy.59
  19.9 0.1 reshape.66
  20.0 0.0 copy-done.1
  20.0 0.0 copy-done
  20.0 24.9 %shard_map.68 = (f32[32,1536]{1,0:T(8,128)S(1)}, f32[32,1]{1,0:T(8,128)S(1)}) custom-call(f32[32,1536]{1,0:T(8,128)S(1)} %pad_maximum_fusion.xs_ref, s32[1,16384]{1,0:T(1,128)S(1)} %get-tuple-element.24.head_ref, s32[1,16384]{1,0:T(1,128)S(1)} %get-tuple-element.23.tail_ref, f32[1,16384]{1,0:T(1,128)S(1)} %bitcast.37), custom_call_target="tpu_custom_call" | custom-call | tf_op jit(solution)/shard_map/pallas_call | solution.py:132
  45.0 0.1 reshape.67
  45.1 0.1 pad_maximum_fusion.5
  45.1 0.1 pad_maximum_fusion.4
  45.3 0.0 copy-start.5
  45.3 9.9 %all_to_all.20 = f32[32,8,66]{2,0,1:T(8,128)S(1)} all-to-all(f32[32,8,66]{2,0,1:T(8,128)S(1)} %copy.62), channel_id=1, replica_groups=mesh['vx'=2,'vy'=4,'col'=4] {'vx','vy'}, dimensions={1} | all-to-all | bytes 135168 | tf_op jit(solution)/shard_map/all_to_all | solution.py:12
  55.2 0.1 slice_reduce_fusion
  55.3 0.2 slice_reduce_fusion.1
  55.5 0.1 reduce-precision_convert_fusion.3
  55.7 0.0 copy-done.5
  55.7 0.0 copy-start.4
  55.7 0.6 fusion.3
  56.3 0.1 copy-done.4
  56.4 0.1 reduce-precision_convert_fusion.1
  56.5 0.2 reduce-precision_convert_fusion
  56.6 0.5 fusion
  57.1 0.2 slice_add_fusion
  57.3 0.1 copy.65
  57.4 0.8 reshape.77
  58.2 3.4 %all-to-all-start.2 = ((f32[8,1,2048]{2,1,0:T(1,128)}), f32[8,1,2048]{2,1,0:T(1,128)S(1)}, u32[]{:S(2)}, u32[]{:S(2)}) async-start(f32[8,1,2048]{2,1,0:T(1,128)} %reshape.77), calls=%async_computation.2 | async-start | bytes 131072 | tf_op jit(solution)/shard_map/all_to_all | solution.py:12
  61.6 0.1 copy.67
  61.7 6.8 %all-to-all-done.2 = f32[8,1,2048]{2,1,0:T(1,128)S(1)} async-done(((f32[8,1,2048]{2,1,0:T(1,128)}), f32[8,1,2048]{2,1,0:T(1,128)S(1)}, u32[]{:S(2)}, u32[]{:S(2)}) %all-to-all-start.2) | async-done | bytes 65568 | tf_op jit(solution)/shard_map/all_to_all | solution.py:12
  68.5 0.8 reduce.5
  69.3 0.1 reshape.78
  69.4 0.1 copy.66
  69.5 0.1 reshape.68
  69.6 9.7 %shard_map.69 = f32[32,1]{1,0:T(8,128)S(1)} custom-call(f32[32,1536]{1,0:T(8,128)S(1)} %pad_maximum_fusion.2.xs_ref, s32[1,16384]{1,0:T(1,128)S(1)} %get-tuple-element.24.head_ref, s32[1,16384]{1,0:T(1,128)S(1)} %get-tuple-element.23.tail_ref, f32[1,16384]{1,0:T(1,128)S(1)} %bitcast.38), custom_call_target="tpu_custom_call" | custom-call | tf_op jit(solution)/shard_map/pallas_call | solution.py:132
  79.3 0.1 copy.68
  79.4 0.6 broadcast_in_dim.8
  80.0 3.3 %all-to-all-start.3 = ((f32[32,8,2]{0,2,1:T(2,128)}), f32[32,8,2]{0,2,1:T(2,128)S(1)}, u32[]{:S(2)}, u32[]{:S(2)}) async-start(f32[32,8,2]{0,2,1:T(2,128)} %broadcast_in_dim.8), calls=%async_computation.3 | async-start | bytes 16384 | tf_op jit(solution)/shard_map/all_to_all | solution.py:12
  83.4 6.4 %all-to-all-done.3 = f32[32,8,2]{0,2,1:T(2,128)S(1)} async-done(((f32[32,8,2]{0,2,1:T(2,128)}), f32[32,8,2]{0,2,1:T(2,128)S(1)}, u32[]{:S(2)}, u32[]{:S(2)}) %all-to-all-start.3) | async-done | bytes 2080 | tf_op jit(solution)/shard_map/all_to_all | solution.py:12
  89.9 0.1 multiply_add_fusion.1
  90.0 0.1 multiply_add_fusion
  90.1 0.0 copy-start.2
  90.1 8.8 %all_gather.6.xs_ref = f32[128,1536]{1,0:T(8,128)S(1)} all-gather(f32[32,1536]{1,0:T(8,128)S(1)} %pad_maximum_fusion.3), channel_id=1, replica_groups=mesh['vx'=2,'vy'=4,'col'=4] {'col'}, dimensions={0}, use_global_device_ids=true | all-gather | bytes 983040 | tf_op jit(solution)/shard_map/all_gather | solution.py:225
  98.9 5.1 %shard_map.70 = f32[1,4096]{1,0:T(1,128)S(1)} custom-call(f32[128,1536]{1,0:T(8,128)S(1)} %all_gather.6.xs_ref, s32[1,4096]{1,0:T(1,128)S(1)} %get-tuple-element.31.head_ref, s32[1,4096]{1,0:T(1,128)S(1)} %get-tuple-element.30.tail_ref, f32[1,4096]{1,0:T(1,128)S(1)} %bitcast.39), custom_call_target="tpu_custom_call" | custom-call | tf_op jit(solution)/shard_map/pallas_call | solution.py:132
  104.0 0.0 copy-done.2
  104.0 5.2 %all-gather = f32[1,16384]{1,0:T(1,128)S(1)} all-gather(f32[1,4096]{1,0:T(1,128)S(1)} %shard_map.70), channel_id=2, replica_groups=mesh['vx'=2,'vy'=4,'col'=4] {'col'}, dimensions={1}, use_global_device_ids=true | all-gather | bytes 81920 | tf_op jit(solution)/shard_map/all_gather | solution.py:226
  109.2 0.6 copy.79
  (15 shorter events, 0.2 us)
Async XLA Ops:
  2.9 8.5 %copy-start.3 = (s32[2,16384]{1,0:T(2,128)S(1)}, s32[2,16384]{1,0:T(2,128)}, u32[]{:S(2)}) copy-start(s32[2,16384]{1,0:T(2,128)} %param.7) | copy-start | bytes 393220
  3.2 16.7 %copy-start.1 = (f32[32,1024]{1,0:T(8,128)S(1)}, f32[32,1024]{1,0:T(8,128)}, u32[]{:S(2)}) copy-start(f32[32,1024]{1,0:T(8,128)} %param.5) | copy-start | bytes 393220
  4.0 16.0 %copy-start = (f32[16384]{0:T(1024)S(1)}, f32[16384]{0:T(1024)}, u32[]{:S(2)}) copy-start(f32[16384]{0:T(1024)} %param.8) | copy-start | bytes 196612
  4.0 14.4 %all-to-all-start = ((f32[8,1,2048]{2,1,0:T(1,128)}), f32[8,1,2048]{2,1,0:T(1,128)S(1)}, u32[]{:S(2)}, u32[]{:S(2)}) async-start(f32[8,1,2048]{2,1,0:T(1,128)} %reshape.75), calls=%async_computation | async-start | bytes 131072 | tf_op jit(solution)/shard_map/all_to_all | solution.py:12
  45.3 10.4 %copy-start.5 = (s32[8,64]{1,0:T(8,128)S(1)}, s32[8,64]{1,0:T(8,128)}, u32[]{:S(2)}) copy-start(s32[8,64]{1,0:T(8,128)} %param.9) | copy-start | bytes 6148
  55.7 0.7 copy-start.4
  58.2 10.3 %all-to-all-start.2 = ((f32[8,1,2048]{2,1,0:T(1,128)}), f32[8,1,2048]{2,1,0:T(1,128)S(1)}, u32[]{:S(2)}, u32[]{:S(2)}) async-start(f32[8,1,2048]{2,1,0:T(1,128)} %reshape.77), calls=%async_computation.2 | async-start | bytes 131072 | tf_op jit(solution)/shard_map/all_to_all | solution.py:12
  80.0 9.8 %all-to-all-start.3 = ((f32[32,8,2]{0,2,1:T(2,128)}), f32[32,8,2]{0,2,1:T(2,128)S(1)}, u32[]{:S(2)}, u32[]{:S(2)}) async-start(f32[32,8,2]{0,2,1:T(2,128)} %broadcast_in_dim.8), calls=%async_computation.3 | async-start | bytes 16384 | tf_op jit(solution)/shard_map/all_to_all | solution.py:12
  90.1 13.9 %copy-start.2 = (f32[32,1024]{1,0:T(8,128)}, f32[32,1024]{1,0:T(8,128)S(1)}, u32[]{:S(2)}) copy-start(f32[32,1024]{1,0:T(8,128)S(1)} %multiply_add_fusion) | copy-start | bytes 393220

commit v20 on v19

--- a/solution.py
+++ b/solution.py
@@ -114,7 +114,7 @@
     edges = head_rows.shape[1]
     tile = edge_tile(rows)
     if rows <= 2048 and edges % 4096 == 0:
-        tile = 4096
+        tile = 8192 if mode == "energy" and edges % 8192 == 0 else 4096
     edge_spec = pl.BlockSpec((1, tile), lambda i: (0, i))
     full = pl.BlockSpec((width, rows), lambda i: (0, 0))
     if mode == "scatter":

time: 110 us -> 110 us (level)
  no operation moved by 1% of the time
where the time goes in v20:
time: 110 us; the launch traced here: 109 us
  Pallas kernels  39.2 us (36%)
  blocking collectives  23.8 us (22%)
  waiting for transfers between devices  19.8 us (18%)
  starting transfers between devices  14.2 us (13%)
  local copies, waits for them, and re-layouts  4.89 us (4%)
  other arithmetic  4 us (4%)
  matrix products  2.3 us (2%)
    pallas_call x3, Pallas kernels, edge_pass(): pl.pallas_call(flow_kernel(mode, local), grid=(edges // tile,), in_specs=...  39.2 us
    all_to_all x3, waiting for transfers between devices, trade(): lax.all_to_all(blocks, ('vx', 'vy'), split_axis=1, concat_axis=1, tiled=T...  19.8 us
    all_to_all x3, starting transfers between devices, trade(): lax.all_to_all(blocks, ('vx', 'vy'), split_axis=1, concat_axis=1, tiled=T...  14.2 us
    all_to_all x1, blocking collectives, trade(): lax.all_to_all(blocks, ('vx', 'vy'), split_axis=1, concat_axis=1, tiled=T...  9.91 us
    all_gather x1, blocking collectives, body(): lax.all_gather(extended, 'col', axis=0, tiled=True)  8.63 us
    all_gather x1, blocking collectives, body(): resistance = lax.all_gather(total, 'col', axis=0, tiled=True)  5.25 us
    unnamed x17, local copies, waits for them, and re-layouts  2.42 us
    dot_general x3, matrix products, pick(): jnp.einsum(pattern, parts3(values), choice, preferred_element_type=jnp.fl...  2.3 us
  transfers between devices with their start and end apart: 3, of which 3 were waited for; matrix products, arithmetic and copies ran while one was open for 0% of the time, Pallas kernels for 0%

profile of v20, /device:TPU:0, one launch (start us, length us, event | category | flops | bytes accessed | tf_op | source)
XLA Modules:
  0.0 109.2 jit_solution(1283244352014507420)
XLA Ops:
  0.6 1.1 reduce-precision_convert_fusion.5
  1.7 1.2 %fusion.2 = f32[96,8,64]{0,2,1:T(8,128)S(1)} fusion(s32[8,64]{1,0:T(8,128)} %param.9, bf16[32,1024]{1,0:T(8,128)(2,1)S(1)} %get-tuple-element.26, bf16[32,1024]{1,0:T(8,128)(2,1)S(1)} %get-tuple-element.29, bf16[32,1024]{1,0:T(8,128)(2,1)S(1)} %get-tuple-element.25), kind=kOutput, calls=%fused_computation.3 | convolution fusion | flops 101777408 | bytes 395264 | tf_op jit(solution)/shard_map/cv,psv->cps/dot_general | solution.py:161
  2.9 0.0 copy-start.3
  2.9 0.2 slice_add_fusion.2
  3.1 0.1 copy.58
  3.2 0.0 copy-start.1
  3.2 0.8 reshape.75
  4.0 0.0 copy-start
  4.0 7.4 %all-to-all-start = ((f32[8,1,2048]{2,1,0:T(1,128)}), f32[8,1,2048]{2,1,0:T(1,128)S(1)}, u32[]{:S(2)}, u32[]{:S(2)}) async-start(f32[8,1,2048]{2,1,0:T(1,128)} %reshape.75), calls=%async_computation | async-start | bytes 131072 | tf_op jit(solution)/shard_map/all_to_all | solution.py:12
  11.4 0.0 copy-done.3
  11.4 0.1 fusion.29
  11.5 0.1 copy.60
  11.6 0.1 copy.61
  11.7 6.7 %all-to-all-done = f32[8,1,2048]{2,1,0:T(1,128)S(1)} async-done(((f32[8,1,2048]{2,1,0:T(1,128)}), f32[8,1,2048]{2,1,0:T(1,128)S(1)}, u32[]{:S(2)}, u32[]{:S(2)}) %all-to-all-start) | async-done | bytes 65568 | tf_op jit(solution)/shard_map/all_to_all | solution.py:12
  18.4 0.5 broadcast.6
  18.9 0.8 reduce.4
  19.7 0.1 reshape.76
  19.8 0.1 copy.59
  19.9 0.1 reshape.66
  20.0 0.0 copy-done.1
  20.0 0.0 copy-done
  20.0 24.9 %shard_map.68 = (f32[32,1536]{1,0:T(8,128)S(1)}, f32[32,1]{1,0:T(8,128)S(1)}) custom-call(f32[32,1536]{1,0:T(8,128)S(1)} %pad_maximum_fusion.xs_ref, s32[1,16384]{1,0:T(1,128)S(1)} %get-tuple-element.24.head_ref, s32[1,16384]{1,0:T(1,128)S(1)} %get-tuple-element.23.tail_ref, f32[1,16384]{1,0:T(1,128)S(1)} %bitcast.37), custom_call_target="tpu_custom_call" | custom-call | tf_op jit(solution)/shard_map/pallas_call | solution.py:132
  45.0 0.1 reshape.67
  45.1 0.1 pad_maximum_fusion.5
  45.1 0.1 pad_maximum_fusion.4
  45.3 0.0 copy-start.5
  45.3 9.9 %all_to_all.20 = f32[32,8,66]{2,0,1:T(8,128)S(1)} all-to-all(f32[32,8,66]{2,0,1:T(8,128)S(1)} %copy.62), channel_id=1, replica_groups=mesh['vx'=2,'vy'=4,'col'=4] {'vx','vy'}, dimensions={1} | all-to-all | bytes 135168 | tf_op jit(solution)/shard_map/all_to_all | solution.py:12
  55.2 0.1 slice_reduce_fusion
  55.3 0.2 slice_reduce_fusion.1
  55.5 0.1 reduce-precision_convert_fusion.3
  55.7 0.0 copy-done.5
  55.7 0.0 copy-start.4
  55.7 0.6 fusion.3
  56.3 0.1 copy-done.4
  56.4 0.1 reduce-precision_convert_fusion.1
  56.5 0.2 reduce-precision_convert_fusion
  56.6 0.5 fusion
  57.1 0.2 slice_add_fusion
  57.3 0.1 copy.65
  57.4 0.8 reshape.77
  58.2 3.4 %all-to-all-start.2 = ((f32[8,1,2048]{2,1,0:T(1,128)}), f32[8,1,2048]{2,1,0:T(1,128)S(1)}, u32[]{:S(2)}, u32[]{:S(2)}) async-start(f32[8,1,2048]{2,1,0:T(1,128)} %reshape.77), calls=%async_computation.2 | async-start | bytes 131072 | tf_op jit(solution)/shard_map/all_to_all | solution.py:12
  61.6 0.1 copy.67
  61.7 6.8 %all-to-all-done.2 = f32[8,1,2048]{2,1,0:T(1,128)S(1)} async-done(((f32[8,1,2048]{2,1,0:T(1,128)}), f32[8,1,2048]{2,1,0:T(1,128)S(1)}, u32[]{:S(2)}, u32[]{:S(2)}) %all-to-all-start.2) | async-done | bytes 65568 | tf_op jit(solution)/shard_map/all_to_all | solution.py:12
  68.5 0.8 reduce.5
  69.3 0.1 reshape.78
  69.4 0.1 copy.66
  69.5 0.1 reshape.68
  69.6 9.2 %shard_map.69 = f32[32,1]{1,0:T(8,128)S(1)} custom-call(f32[32,1536]{1,0:T(8,128)S(1)} %pad_maximum_fusion.2.xs_ref, s32[1,16384]{1,0:T(1,128)S(1)} %get-tuple-element.24.head_ref, s32[1,16384]{1,0:T(1,128)S(1)} %get-tuple-element.23.tail_ref, f32[1,16384]{1,0:T(1,128)S(1)} %bitcast.38), custom_call_target="tpu_custom_call" | custom-call | tf_op jit(solution)/shard_map/pallas_call | solution.py:132
  78.8 0.1 copy.68
  78.9 0.6 broadcast_in_dim.8
  79.5 3.5 %all-to-all-start.3 = ((f32[32,8,2]{0,2,1:T(2,128)}), f32[32,8,2]{0,2,1:T(2,128)S(1)}, u32[]{:S(2)}, u32[]{:S(2)}) async-start(f32[32,8,2]{0,2,1:T(2,128)} %broadcast_in_dim.8), calls=%async_computation.3 | async-start | bytes 16384 | tf_op jit(solution)/shard_map/all_to_all | solution.py:12
  83.0 6.2 %all-to-all-done.3 = f32[32,8,2]{0,2,1:T(2,128)S(1)} async-done(((f32[32,8,2]{0,2,1:T(2,128)}), f32[32,8,2]{0,2,1:T(2,128)S(1)}, u32[]{:S(2)}, u32[]{:S(2)}) %all-to-all-start.3) | async-done | bytes 2080 | tf_op jit(solution)/shard_map/all_to_all | solution.py:12
  89.3 0.1 multiply_add_fusion.1
  89.4 0.1 multiply_add_fusion
  89.5 0.0 copy-start.2
  89.5 8.6 %all_gather.6.xs_ref = f32[128,1536]{1,0:T(8,128)S(1)} all-gather(f32[32,1536]{1,0:T(8,128)S(1)} %pad_maximum_fusion.3), channel_id=1, replica_groups=mesh['vx'=2,'vy'=4,'col'=4] {'col'}, dimensions={0}, use_global_device_ids=true | all-gather | bytes 983040 | tf_op jit(solution)/shard_map/all_gather | solution.py:225
  98.2 5.1 %shard_map.70 = f32[1,4096]{1,0:T(1,128)S(1)} custom-call(f32[128,1536]{1,0:T(8,128)S(1)} %all_gather.6.xs_ref, s32[1,4096]{1,0:T(1,128)S(1)} %get-tuple-element.31.head_ref, s32[1,4096]{1,0:T(1,128)S(1)} %get-tuple-element.30.tail_ref, f32[1,4096]{1,0:T(1,128)S(1)} %bitcast.39), custom_call_target="tpu_custom_call" | custom-call | tf_op jit(solution)/shard_map/pallas_call | solution.py:132
  103.3 0.0 copy-done.2
  103.3 5.2 %all-gather = f32[1,16384]{1,0:T(1,128)S(1)} all-gather(f32[1,4096]{1,0:T(1,128)S(1)} %shard_map.70), channel_id=2, replica_groups=mesh['vx'=2,'vy'=4,'col'=4] {'col'}, dimensions={1}, use_global_device_ids=true | all-gather | bytes 81920 | tf_op jit(solution)/shard_map/all_gather | solution.py:226
  108.5 0.6 copy.79
  (15 shorter events, 0.2 us)
Async XLA Ops:
  2.9 8.5 %copy-start.3 = (s32[2,16384]{1,0:T(2,128)S(1)}, s32[2,16384]{1,0:T(2,128)}, u32[]{:S(2)}) copy-start(s32[2,16384]{1,0:T(2,128)} %param.7) | copy-start | bytes 393220
  3.2 16.7 %copy-start.1 = (f32[32,1024]{1,0:T(8,128)S(1)}, f32[32,1024]{1,0:T(8,128)}, u32[]{:S(2)}) copy-start(f32[32,1024]{1,0:T(8,128)} %param.5) | copy-start | bytes 393220
  4.0 16.0 %copy-start = (f32[16384]{0:T(1024)S(1)}, f32[16384]{0:T(1024)}, u32[]{:S(2)}) copy-start(f32[16384]{0:T(1024)} %param.8) | copy-start | bytes 196612
  4.0 14.4 %all-to-all-start = ((f32[8,1,2048]{2,1,0:T(1,128)}), f32[8,1,2048]{2,1,0:T(1,128)S(1)}, u32[]{:S(2)}, u32[]{:S(2)}) async-start(f32[8,1,2048]{2,1,0:T(1,128)} %reshape.75), calls=%async_computation | async-start | bytes 131072 | tf_op jit(solution)/shard_map/all_to_all | solution.py:12
  45.3 10.4 %copy-start.5 = (s32[8,64]{1,0:T(8,128)S(1)}, s32[8,64]{1,0:T(8,128)}, u32[]{:S(2)}) copy-start(s32[8,64]{1,0:T(8,128)} %param.9) | copy-start | bytes 6148
  55.7 0.7 copy-start.4
  58.2 10.3 %all-to-all-start.2 = ((f32[8,1,2048]{2,1,0:T(1,128)}), f32[8,1,2048]{2,1,0:T(1,128)S(1)}, u32[]{:S(2)}, u32[]{:S(2)}) async-start(f32[8,1,2048]{2,1,0:T(1,128)} %reshape.77), calls=%async_computation.2 | async-start | bytes 131072 | tf_op jit(solution)/shard_map/all_to_all | solution.py:12
  79.5 9.8 %all-to-all-start.3 = ((f32[32,8,2]{0,2,1:T(2,128)}), f32[32,8,2]{0,2,1:T(2,128)S(1)}, u32[]{:S(2)}, u32[]{:S(2)}) async-start(f32[32,8,2]{0,2,1:T(2,128)} %broadcast_in_dim.8), calls=%async_computation.3 | async-start | bytes 16384 | tf_op jit(solution)/shard_map/all_to_all | solution.py:12
  89.5 13.8 %copy-start.2 = (f32[32,1024]{1,0:T(8,128)}, f32[32,1024]{1,0:T(8,128)S(1)}, u32[]{:S(2)}) copy-start(f32[32,1024]{1,0:T(8,128)S(1)} %multiply_add_fusion) | copy-start | bytes 393220

commit v21 on v20

--- a/solution.py
+++ b/solution.py
@@ -114,7 +114,7 @@
     edges = head_rows.shape[1]
     tile = edge_tile(rows)
     if rows <= 2048 and edges % 4096 == 0:
-        tile = 8192 if mode == "energy" and edges % 8192 == 0 else 4096
+        tile = 16384 if mode == "energy" and edges == 16384 else 4096
     edge_spec = pl.BlockSpec((1, tile), lambda i: (0, i))
     full = pl.BlockSpec((width, rows), lambda i: (0, 0))
     if mode == "scatter":

time: 110 us -> 109 us (level)
  no operation moved by 1% of the time
where the time goes in v21:
time: 109 us
  Pallas kernels  38.9 us (36%)
  blocking collectives  23.8 us (22%)
  waiting for transfers between devices  19.8 us (18%)
  starting transfers between devices  14.2 us (13%)
  local copies, waits for them, and re-layouts  4.9 us (4%)
  other arithmetic  4 us (4%)
  matrix products  2.3 us (2%)
    pallas_call x3, Pallas kernels, edge_pass(): pl.pallas_call(flow_kernel(mode, local), grid=(edges // tile,), in_specs=...  38.9 us
    all_to_all x3, waiting for transfers between devices, trade(): lax.all_to_all(blocks, ('vx', 'vy'), split_axis=1, concat_axis=1, tiled=T...  19.8 us
    all_to_all x3, starting transfers between devices, trade(): lax.all_to_all(blocks, ('vx', 'vy'), split_axis=1, concat_axis=1, tiled=T...  14.2 us
    all_to_all x1, blocking collectives, trade(): lax.all_to_all(blocks, ('vx', 'vy'), split_axis=1, concat_axis=1, tiled=T...  9.91 us
    all_gather x1, blocking collectives, body(): lax.all_gather(extended, 'col', axis=0, tiled=True)  8.63 us
    all_gather x1, blocking collectives, body(): resistance = lax.all_gather(total, 'col', axis=0, tiled=True)  5.25 us
    unnamed x17, local copies, waits for them, and re-layouts  2.42 us
    dot_general x3, matrix products, pick(): jnp.einsum(pattern, parts3(values), choice, preferred_element_type=jnp.fl...  2.3 us
  transfers between devices with their start and end apart: 3, of which 3 were waited for; matrix products, arithmetic and copies ran while one was open for 0% of the time, Pallas kernels for 0%

profile of v21, /device:TPU:0, one launch (start us, length us, event | category | flops | bytes accessed | tf_op | source)
XLA Modules:
  0.0 108.9 jit_solution(4444955194236935560)
XLA Ops:
  0.6 1.1 reduce-precision_convert_fusion.5
  1.7 1.2 %fusion.2 = f32[96,8,64]{0,2,1:T(8,128)S(1)} fusion(s32[8,64]{1,0:T(8,128)} %param.9, bf16[32,1024]{1,0:T(8,128)(2,1)S(1)} %get-tuple-element.26, bf16[32,1024]{1,0:T(8,128)(2,1)S(1)} %get-tuple-element.29, bf16[32,1024]{1,0:T(8,128)(2,1)S(1)} %get-tuple-element.25), kind=kOutput, calls=%fused_computation.3 | convolution fusion | flops 101777408 | bytes 395264 | tf_op jit(solution)/shard_map/cv,psv->cps/dot_general | solution.py:161
  2.9 0.0 copy-start.3
  2.9 0.2 slice_add_fusion.2
  3.1 0.1 copy.58
  3.2 0.0 copy-start.1
  3.2 0.8 reshape.75
  4.0 0.0 copy-start
  4.0 7.4 %all-to-all-start = ((f32[8,1,2048]{2,1,0:T(1,128)}), f32[8,1,2048]{2,1,0:T(1,128)S(1)}, u32[]{:S(2)}, u32[]{:S(2)}) async-start(f32[8,1,2048]{2,1,0:T(1,128)} %reshape.75), calls=%async_computation | async-start | bytes 131072 | tf_op jit(solution)/shard_map/all_to_all | solution.py:12
  11.4 0.0 copy-done.3
  11.4 0.1 fusion.29
  11.5 0.1 copy.60
  11.6 0.1 copy.61
  11.7 6.7 %all-to-all-done = f32[8,1,2048]{2,1,0:T(1,128)S(1)} async-done(((f32[8,1,2048]{2,1,0:T(1,128)}), f32[8,1,2048]{2,1,0:T(1,128)S(1)}, u32[]{:S(2)}, u32[]{:S(2)}) %all-to-all-start) | async-done | bytes 65568 | tf_op jit(solution)/shard_map/all_to_all | solution.py:12
  18.4 0.5 broadcast.6
  18.9 0.8 reduce.4
  19.7 0.1 reshape.76
  19.8 0.1 copy.59
  19.9 0.1 reshape.66
  20.0 0.0 copy-done.1
  20.0 0.0 copy-done
  20.0 24.9 %shard_map.68 = (f32[32,1536]{1,0:T(8,128)S(1)}, f32[32,1]{1,0:T(8,128)S(1)}) custom-call(f32[32,1536]{1,0:T(8,128)S(1)} %pad_maximum_fusion.xs_ref, s32[1,16384]{1,0:T(1,128)S(1)} %get-tuple-element.24.head_ref, s32[1,16384]{1,0:T(1,128)S(1)} %get-tuple-element.23.tail_ref, f32[1,16384]{1,0:T(1,128)S(1)} %bitcast.37), custom_call_target="tpu_custom_call" | custom-call | tf_op jit(solution)/shard_map/pallas_call | solution.py:132
  45.0 0.1 reshape.67
  45.1 0.1 pad_maximum_fusion.5
  45.1 0.1 pad_maximum_fusion.4
  45.3 0.0 copy-start.5
  45.3 9.9 %all_to_all.20 = f32[32,8,66]{2,0,1:T(8,128)S(1)} all-to-all(f32[32,8,66]{2,0,1:T(8,128)S(1)} %copy.62), channel_id=1, replica_groups=mesh['vx'=2,'vy'=4,'col'=4] {'vx','vy'}, dimensions={1} | all-to-all | bytes 135168 | tf_op jit(solution)/shard_map/all_to_all | solution.py:12
  55.2 0.1 slice_reduce_fusion
  55.3 0.2 slice_reduce_fusion.1
  55.5 0.1 reduce-precision_convert_fusion.3
  55.7 0.0 copy-done.5
  55.7 0.0 copy-start.4
  55.7 0.6 fusion.3
  56.3 0.1 copy-done.4
  56.4 0.1 reduce-precision_convert_fusion.1
  56.5 0.2 reduce-precision_convert_fusion
  56.6 0.5 fusion
  57.1 0.2 slice_add_fusion
  57.3 0.1 copy.65
  57.4 0.8 reshape.77
  58.2 3.5 %all-to-all-start.2 = ((f32[8,1,2048]{2,1,0:T(1,128)}), f32[8,1,2048]{2,1,0:T(1,128)S(1)}, u32[]{:S(2)}, u32[]{:S(2)}) async-start(f32[8,1,2048]{2,1,0:T(1,128)} %reshape.77), calls=%async_computation.2 | async-start | bytes 131072 | tf_op jit(solution)/shard_map/all_to_all | solution.py:12
  61.8 0.1 copy.67
  61.8 6.7 %all-to-all-done.2 = f32[8,1,2048]{2,1,0:T(1,128)S(1)} async-done(((f32[8,1,2048]{2,1,0:T(1,128)}), f32[8,1,2048]{2,1,0:T(1,128)S(1)}, u32[]{:S(2)}, u32[]{:S(2)}) %all-to-all-start.2) | async-done | bytes 65568 | tf_op jit(solution)/shard_map/all_to_all | solution.py:12
  68.5 0.8 reduce.5
  69.3 0.1 reshape.78
  69.4 0.1 copy.66
  69.5 0.1 reshape.68
  69.6 8.9 %shard_map.69 = f32[32,1]{1,0:T(8,128)S(1)} custom-call(f32[32,1536]{1,0:T(8,128)S(1)} %pad_maximum_fusion.2.xs_ref, s32[1,16384]{1,0:T(1,128)S(1)} %get-tuple-element.24.head_ref, s32[1,16384]{1,0:T(1,128)S(1)} %get-tuple-element.23.tail_ref, f32[1,16384]{1,0:T(1,128)S(1)} %bitcast.38), custom_call_target="tpu_custom_call" | custom-call | tf_op jit(solution)/shard_map/pallas_call | solution.py:132
  78.5 0.1 copy.68
  78.6 0.6 broadcast_in_dim.8
  79.2 3.3 %all-to-all-start.3 = ((f32[32,8,2]{0,2,1:T(2,128)}), f32[32,8,2]{0,2,1:T(2,128)S(1)}, u32[]{:S(2)}, u32[]{:S(2)}) async-start(f32[32,8,2]{0,2,1:T(2,128)} %broadcast_in_dim.8), calls=%async_computation.3 | async-start | bytes 16384 | tf_op jit(solution)/shard_map/all_to_all | solution.py:12
  82.6 6.4 %all-to-all-done.3 = f32[32,8,2]{0,2,1:T(2,128)S(1)} async-done(((f32[32,8,2]{0,2,1:T(2,128)}), f32[32,8,2]{0,2,1:T(2,128)S(1)}, u32[]{:S(2)}, u32[]{:S(2)}) %all-to-all-start.3) | async-done | bytes 2080 | tf_op jit(solution)/shard_map/all_to_all | solution.py:12
  89.0 0.1 multiply_add_fusion.1
  89.1 0.1 multiply_add_fusion
  89.2 0.0 copy-start.2
  89.3 8.6 %all_gather.6.xs_ref = f32[128,1536]{1,0:T(8,128)S(1)} all-gather(f32[32,1536]{1,0:T(8,128)S(1)} %pad_maximum_fusion.3), channel_id=1, replica_groups=mesh['vx'=2,'vy'=4,'col'=4] {'col'}, dimensions={0}, use_global_device_ids=true | all-gather | bytes 983040 | tf_op jit(solution)/shard_map/all_gather | solution.py:225
  97.9 5.1 %shard_map.70 = f32[1,4096]{1,0:T(1,128)S(1)} custom-call(f32[128,1536]{1,0:T(8,128)S(1)} %all_gather.6.xs_ref, s32[1,4096]{1,0:T(1,128)S(1)} %get-tuple-element.31.head_ref, s32[1,4096]{1,0:T(1,128)S(1)} %get-tuple-element.30.tail_ref, f32[1,4096]{1,0:T(1,128)S(1)} %bitcast.39), custom_call_target="tpu_custom_call" | custom-call | tf_op jit(solution)/shard_map/pallas_call | solution.py:132
  103.0 0.0 copy-done.2
  103.0 5.2 %all-gather = f32[1,16384]{1,0:T(1,128)S(1)} all-gather(f32[1,4096]{1,0:T(1,128)S(1)} %shard_map.70), channel_id=2, replica_groups=mesh['vx'=2,'vy'=4,'col'=4] {'col'}, dimensions={1}, use_global_device_ids=true | all-gather | bytes 81920 | tf_op jit(solution)/shard_map/all_gather | solution.py:226
  108.2 0.6 copy.79
  (15 shorter events, 0.2 us)
Async XLA Ops:
  2.9 8.5 %copy-start.3 = (s32[2,16384]{1,0:T(2,128)S(1)}, s32[2,16384]{1,0:T(2,128)}, u32[]{:S(2)}) copy-start(s32[2,16384]{1,0:T(2,128)} %param.7) | copy-start | bytes 393220
  3.2 16.7 %copy-start.1 = (f32[32,1024]{1,0:T(8,128)S(1)}, f32[32,1024]{1,0:T(8,128)}, u32[]{:S(2)}) copy-start(f32[32,1024]{1,0:T(8,128)} %param.5) | copy-start | bytes 393220
  4.0 16.0 %copy-start = (f32[16384]{0:T(1024)S(1)}, f32[16384]{0:T(1024)}, u32[]{:S(2)}) copy-start(f32[16384]{0:T(1024)} %param.8) | copy-start | bytes 196612
  4.0 14.4 %all-to-all-start = ((f32[8,1,2048]{2,1,0:T(1,128)}), f32[8,1,2048]{2,1,0:T(1,128)S(1)}, u32[]{:S(2)}, u32[]{:S(2)}) async-start(f32[8,1,2048]{2,1,0:T(1,128)} %reshape.75), calls=%async_computation | async-start | bytes 131072 | tf_op jit(solution)/shard_map/all_to_all | solution.py:12
  45.3 10.4 %copy-start.5 = (s32[8,64]{1,0:T(8,128)S(1)}, s32[8,64]{1,0:T(8,128)}, u32[]{:S(2)}) copy-start(s32[8,64]{1,0:T(8,128)} %param.9) | copy-start | bytes 6148
  55.7 0.7 copy-start.4
  58.2 10.3 %all-to-all-start.2 = ((f32[8,1,2048]{2,1,0:T(1,128)}), f32[8,1,2048]{2,1,0:T(1,128)S(1)}, u32[]{:S(2)}, u32[]{:S(2)}) async-start(f32[8,1,2048]{2,1,0:T(1,128)} %reshape.77), calls=%async_computation.2 | async-start | bytes 131072 | tf_op jit(solution)/shard_map/all_to_all | solution.py:12
  79.2 9.8 %all-to-all-start.3 = ((f32[32,8,2]{0,2,1:T(2,128)}), f32[32,8,2]{0,2,1:T(2,128)S(1)}, u32[]{:S(2)}, u32[]{:S(2)}) async-start(f32[32,8,2]{0,2,1:T(2,128)} %broadcast_in_dim.8), calls=%async_computation.3 | async-start | bytes 16384 | tf_op jit(solution)/shard_map/all_to_all | solution.py:12
  89.2 13.8 %copy-start.2 = (f32[32,1024]{1,0:T(8,128)}, f32[32,1024]{1,0:T(8,128)S(1)}, u32[]{:S(2)}) copy-start(f32[32,1024]{1,0:T(8,128)S(1)} %multiply_add_fusion) | copy-start | bytes 393220
